TPU v7x, 256 devices: a whole 4x4x8 slice. The times are simulated.
256 devices in a mesh: dom: 32 (over y, x, core), rot: 8 (over z).
Axes of the slice: x: 4, y: 4, z: 8, core: 2. Of those that a mesh axis runs over, the one named last changes fastest.
Arguments:
- particles: bfloat16 [2048, 8192], P('dom'), may hold values from -8 to 8, as said below
- assign: int32 [2048], P('dom'), may hold values from 0 to 191, as said below
- rot_index: int32 [2048], P('dom'), may hold values from 0 to 63
- group: int32 [2048], P('dom'), may hold values from 0 to 31
- ctf_table: float32 [32, 64], replicated, may hold values from -1 to 1
Outputs:
- refs: bfloat16 [192, 8192], P('dom')
- best_scores: float32 [2048, 192], P(('dom', 'rot'))
Inputs may be any that keep to these rules, and one draw needn't show every extreme that they name: `particles`: rows in custom order; values real. `assign`: owner o holds classes o * 6 to o * 6 + 5. The 64 particles of one index of dom form 8 shares of 8 consecutive particles; within each share at most 2 particles are assigned to the classes of one owner.
All inputs are finite; a program needn't handle non-finite values.
Results may differ from a plain program's by a relative error of at most 0.0027.
Values may be sent and summed in bfloat16 or wider, within the bound.
No kernel may reach another device: no remote copies, remote signals or barrier semaphores. Data moves between devices by JAX's collectives and lax.ppermute only.
A program may use at most 128 MiB of HBM per device.

v0:
```python
import math

import jax
import jax.numpy as jnp
from jax import lax
from jax.sharding import PartitionSpec as P

CYCLES = 64
MFREQ = 64
CLS_DEV = 6
ROT_DEV = 8
K = 8192


def angles(index, total):
    freqs = jnp.arange(MFREQ, dtype=jnp.int32)
    phase = freqs[None, :] * index[:, None] % total
    return phase.astype(jnp.float32) * (2.0 * math.pi / total)


def derotate(spec, rotation, ctf_rows, total):
    count = spec.shape[0]
    layered = spec.reshape(count, 2, CYCLES, MFREQ)
    real_part = layered[:, 0]
    imag_part = layered[:, 1]
    angle = angles(rotation, total)
    cosine = jnp.cos(angle)[:, None, :]
    sine = jnp.sin(angle)[:, None, :]
    turned = jnp.stack(
        [real_part * cosine + imag_part * sine, imag_part * cosine - real_part * sine], axis=1
    )
    return (turned * ctf_rows[:, None, :, None]).reshape(count, K)


def rotate_refs(refs, rotation, total):
    count = refs.shape[0]
    layered = refs.astype(jnp.float32).reshape(count, 2, CYCLES, MFREQ)
    real_part = layered[:, 0]
    imag_part = layered[:, 1]
    angle = angles(jnp.reshape(rotation, (1,)), total)
    cosine = jnp.cos(angle)
    sine = jnp.sin(angle)
    turned = jnp.stack(
        [real_part * cosine - imag_part * sine, real_part * sine + imag_part * cosine], axis=1
    )
    return turned.reshape(count, K).astype(jnp.bfloat16)


def table_rows(group, ctf_table):
    onehot = (group[:, None] == jnp.arange(ctf_table.shape[0], dtype=jnp.int32)[None, :]).astype(
        jnp.float32
    )
    return jnp.dot(
        onehot, ctf_table, precision=lax.Precision.HIGHEST, preferred_element_type=jnp.float32
    )


def accumulate(spec, labels, rotation, group, ctf_table, count, total):
    ctf_rows = table_rows(group, ctf_table)
    weighted = derotate(spec.astype(jnp.float32), rotation, ctf_rows, total)
    member = (jnp.arange(count, dtype=jnp.int32)[:, None] == labels[None, :]).astype(jnp.float32)
    numer = jnp.dot(
        member, weighted, precision=lax.Precision.HIGHEST, preferred_element_type=jnp.float32
    )
    denom = jnp.dot(
        member,
        ctf_rows * ctf_rows,
        precision=lax.Precision.HIGHEST,
        preferred_element_type=jnp.float32,
    )
    return (numer, denom)


def local(particles, assign, rot_index, group, ctf_table):
    dom_count = lax.axis_size("dom")
    rot_count = lax.axis_size("rot")
    rot_rank = lax.axis_index("rot")
    total = ROT_DEV * rot_count
    share = particles.shape[0] // rot_count
    first = rot_rank * share
    mine = lax.dynamic_slice_in_dim(particles, first, share, 0)
    mine_assign = lax.dynamic_slice_in_dim(assign, first, share, 0)
    mine_rot = lax.dynamic_slice_in_dim(rot_index, first, share, 0)
    mine_group = lax.dynamic_slice_in_dim(group, first, share, 0)
    numer_all, denom_all = accumulate(
        mine, mine_assign, mine_rot, mine_group, ctf_table, CLS_DEV * dom_count, total
    )
    numer, denom = (
        lax.psum_scatter(numer_all, "dom", scatter_dimension=0, tiled=True),
        lax.psum_scatter(denom_all, "dom", scatter_dimension=0, tiled=True),
    )
    numer, denom = lax.psum((numer, denom), "rot")
    plain = numer.reshape(CLS_DEV, 2, CYCLES, MFREQ) / (denom[:, None, :, None] + 1.0)
    spread = jnp.mean(plain * plain, axis=(1, 2, 3))
    refs = (
        (plain / jnp.sqrt(spread + 1e-06)[:, None, None, None])
        .reshape(CLS_DEV, K)
        .astype(jnp.bfloat16)
    )
    ctf_all = table_rows(group, ctf_table)
    modulated = (
        (particles.reshape(-1, 2, CYCLES, MFREQ) * ctf_all[:, None, :, None])
        .reshape(-1, K)
        .astype(jnp.bfloat16)
    )
    scale = 1.0 / math.sqrt(K)
    piece = lax.all_gather(refs, "dom", axis=0, tiled=True)
    best = None
    for turn in range(ROT_DEV):
        rotation = rot_rank * ROT_DEV + turn
        turned = rotate_refs(piece, rotation, total)
        found = (
            lax.dot_general(
                modulated, turned, (((1,), (1,)), ((), ())), preferred_element_type=jnp.float32
            )
            * scale
        )
        best = found if best is None else jnp.maximum(best, found)
    highest = lax.pmax(best, "rot")
    best_scores = lax.dynamic_slice_in_dim(highest, first, share, 0)
    return (refs, best_scores)


def solution(mesh):
    in_specs = (P("dom", None), P("dom"), P("dom"), P("dom"), P())
    out_specs = (P("dom", None), P(("dom", "rot"), None))
    return jax.shard_map(local, mesh=mesh, in_specs=in_specs, out_specs=out_specs, check_vma=False)
```

profile of v0, /device:TPU:2, one launch (start us, length us, event | category | flops | bytes accessed | tf_op | source)
XLA Modules:
  0.0 625.5 jit_solution(1488995482470117098)
XLA Ops:
  15.7 76.7 %fusion = f32[8,8192]{1,0:T(8,128)S(1)} fusion(f32[192,8192]{1,0:T(8,128)} %fusion.9), kind=kCustom, calls=%all-reduce-scatter | all-reduce-scatter fusion | flops 2097153 | bytes 6554624
  106.4 7.6 %collective-permute-start.2 = (f32[8,8192]{1,0:T(8,128)S(1)}, f32[8,8192]{1,0:T(8,128)S(1)}, u32[]{:S(2)}, u32[]{:S(2)}) collective-permute-start(f32[8,8192]{1,0:T(8,128)S(1)} %fusion), channel_id=1, source_target_pairs={{0,24},{8,32},{16,40},{24,48},{32,56},{40,64},{48,72},{56,80},{64,... | collective-permute-start | bytes 786440
  117.8 11.7 %collective-permute-start = (f32[8,8192]{1,0:T(8,128)S(1)}, f32[8,8192]{1,0:T(8,128)}, u32[]{:S(2)}, u32[]{:S(2)}) collective-permute-start(f32[8,8192]{1,0:T(8,128)S(1)} %fusion), channel_id=1, source_target_pairs={{0,8},{8,16},{16,24},{24,32},{32,40},{40,48},{48,56},{56,64},{64,7... | collective-permute-start | bytes 786440
  129.6 117.6 %all-reduce.1 = f32[192,64]{1,0:T(8,128)S(1)} all-reduce(f32[192,64]{1,0:T(8,128)S(1)} %fusion.8), channel_id=3, replica_groups=mesh['dom'=32,'rot'=8] {'dom'}, use_global_device_ids=true, to_apply=%region_2.3.clone | all-reduce | flops 12288 | bytes 98304
  247.3 20.0 %psum.15 = f32[6,64]{1,0:T(8,128)S(1)} all-reduce(f32[6,64]{1,0:T(8,128)S(1)} %constant_dynamic-slice_fusion.1), channel_id=1, replica_groups=mesh['dom'=32,'rot'=8] {'rot'}, use_global_device_ids=true, to_apply=%region_3.4 | all-reduce | flops 384 | bytes 3072 | tf_op jit(solution)/shard_map/psum | solution.py:92
  268.9 11.3 %concatenate = f32[70,8192]{1,0:T(8,128)S(1)} concatenate(f32[6,8192]{1,0:T(8,128)S(1)} %collective-permute-done.7, f32[8,8192]{1,0:T(8,128)S(1)} %collective-permute-done.6, f32[8,8192]{1,0:T(8,128)S(1)} %collective-permute-done.5, f32[8,8192]{1,0:T(8,128)} %copy-done.6, f32[8,8192]{1,0:T(8,128)} %copy-done.7, f32[8,8192]{1,0:T(8,128)} %copy-done.8, f32[8,8192]{1,0:T(8,128)} %copy-done.9, ...), dimensions={0} | concatenate | bytes 4587520
  281.3 70.8 %all-reduce.5.cloned.1.call-done = f32[6,8192]{1,0:T(8,128)} async-done(((f32[6,8192]{1,0:T(8,128)}), f32[6,8192]{1,0:T(8,128)}) %all-reduce.5.cloned.1.call-update) | async-done | bytes 196624 | tf_op jit(solution)/shard_map/psum | solution.py:92
  363.2 41.3 %all-gather.3.cloned.1.call-done = bf16[32,6,8192]{2,1,0:T(8,128)(2,1)} async-done(((bf16[1,6,8192]{2,1,0:T(8,128)(2,1)}), bf16[32,6,8192]{2,1,0:T(8,128)(2,1)}) %all-gather.3.cloned.1.call-update) | async-done | bytes 3145744 | tf_op jit(solution)/shard_map/all_gather | solution.py:107
  404.5 10.4 %reshape.402 = f32[192,2,64,64]{3,2,1,0:T(8,128)} reshape(bf16[32,6,8192]{2,1,0:T(8,128)(2,1)} %all-gather.3.cloned.1.call-done) | data formatting | bytes 9437184 | tf_op jit(solution)/shard_map/reshape | solution.py:37
  414.9 7.9 %subtract_convert_fusion.1 = (bf16[192,1,64,64]{3,2,1,0:T(8,128)(2,1)}, bf16[192,1,64,64]{3,2,1,0:T(8,128)(2,1)}, bf16[192,1,64,64]{3,2,1,0:T(8,128)(2,1)S(1)}, bf16[192,1,64,64]{3,2,1,0:T(8,128)(2,1)S(1)}) fusion(f32[64]{0:T(128)S(1)} %get-tuple-element.38, f32[64]{0:T(128)S(1)} %get-tuple-element.39, f32[192,2,64,64]{3,2,1,0:T(8,128)} %reshape.402, ...), kind=kLoop, calls=%fused_computation.11 | loop fusion | flops 12582912 | bytes 12583936 | tf_op jit(solution)/shard_map/convert.4
  426.7 9.2 %copy.22 = bf16[192,2,64,64]{0,3,2,1:T(8,128)(2,1)} copy(bf16[192,2,64,64]{3,2,1,0:T(8,128)(2,1)} %pad_maximum_fusion.7) | data formatting | bytes 6291456 | tf_op jit(solution)/shard_map/stack | solution.py:43
  435.9 6.7 %pad_maximum_fusion.6 = bf16[192,2,64,64]{3,2,1,0:T(8,128)(2,1)} fusion(bf16[192,1,64,64]{3,2,1,0:T(8,128)(2,1)} %get-tuple-element.15, bf16[192,1,64,64]{3,2,1,0:T(8,128)(2,1)} %get-tuple-element.14), kind=kLoop, calls=%fused_computation.6 | loop fusion | flops 1572864 | bytes 6291456 | tf_op jit(solution)/shard_map/stack | solution.py:43
  442.5 9.2 %copy.21 = bf16[192,2,64,64]{0,3,2,1:T(8,128)(2,1)} copy(bf16[192,2,64,64]{3,2,1,0:T(8,128)(2,1)} %pad_maximum_fusion.6) | data formatting | bytes 6291456 | tf_op jit(solution)/shard_map/stack | solution.py:43
  457.8 12.4 %subtract_convert_fusion.4 = (bf16[192,1,64,64]{3,2,1,0:T(8,128)(2,1)}, bf16[192,1,64,64]{3,2,1,0:T(8,128)(2,1)}, bf16[192,1,64,64]{3,2,1,0:T(8,128)(2,1)}, bf16...) fusion(f32[64]{0:T(128)S(1)} %get-tuple-element.44, ...), kind=kLoop, calls=%fused_computation.17 | loop fusion | flops 18874368 | bytes 15730176 | tf_op jit(solution)/shard_map/convert.10
  474.0 9.2 %copy.20 = bf16[192,2,64,64]{0,3,2,1:T(8,128)(2,1)} copy(bf16[192,2,64,64]{3,2,1,0:T(8,128)(2,1)} %pad_maximum_fusion.5) | data formatting | bytes 6291456 | tf_op jit(solution)/shard_map/stack | solution.py:43
  492.1 9.2 %copy.19 = bf16[192,2,64,64]{0,3,2,1:T(8,128)(2,1)} copy(bf16[192,2,64,64]{3,2,1,0:T(8,128)(2,1)} %pad_maximum_fusion.4) | data formatting | bytes 6291456 | tf_op jit(solution)/shard_map/stack | solution.py:43
  510.2 9.2 %copy.18 = bf16[192,2,64,64]{0,3,2,1:T(8,128)(2,1)} copy(bf16[192,2,64,64]{3,2,1,0:T(8,128)(2,1)} %pad_maximum_fusion.3) | data formatting | bytes 6291456 | tf_op jit(solution)/shard_map/stack | solution.py:43
  522.4 12.5 %subtract_convert_fusion.7 = (bf16[192,1,64,64]{3,2,1,0:T(8,128)(2,1)}, bf16[192,1,64,64]{3,2,1,0:T(8,128)(2,1)}, bf16[192,1,64,64]{3,2,1,0:T(8,128)(2,1)}, bf16...) fusion(f32[64]{0:T(128)S(1)} %get-tuple-element.34, ...), kind=kLoop, calls=%fused_computation.23 | loop fusion | flops 18874368 | bytes 15730176 | tf_op jit(solution)/shard_map/convert.16
  538.8 9.2 %copy.17 = bf16[192,2,64,64]{0,3,2,1:T(8,128)(2,1)} copy(bf16[192,2,64,64]{3,2,1,0:T(8,128)(2,1)} %pad_maximum_fusion.2) | data formatting | bytes 6291456 | tf_op jit(solution)/shard_map/stack | solution.py:43
  551.2 5.8 pad_maximum_fusion.1
  556.9 9.2 %copy.16 = bf16[192,2,64,64]{0,3,2,1:T(8,128)(2,1)} copy(bf16[192,2,64,64]{3,2,1,0:T(8,128)(2,1)} %pad_maximum_fusion.1) | data formatting | bytes 6291456 | tf_op jit(solution)/shard_map/stack | solution.py:43
  569.4 5.8 pad_maximum_fusion
  575.1 9.2 %copy.15 = bf16[192,2,64,64]{0,3,2,1:T(8,128)(2,1)} copy(bf16[192,2,64,64]{3,2,1,0:T(8,128)(2,1)} %pad_maximum_fusion) | data formatting | bytes 6291456 | tf_op jit(solution)/shard_map/stack | solution.py:43
  587.4 30.7 %pmax.7 = f32[64,192]{1,0:T(8,128)S(1)} all-reduce(f32[64,192]{1,0:T(8,128)S(1)} %fusion.7), channel_id=1, replica_groups=mesh['dom'=32,'rot'=8] {'rot'}, use_global_device_ids=true, to_apply=%region_5.6 | all-reduce | flops 12288 | bytes 98304 | tf_op jit(solution)/shard_map/pmax | solution.py:119
  (90 shorter events, 86.6 us)
Async XLA Ops:
  7.2 2.8 copy-start
  7.2 345.0 %all-reduce.5.cloned.1.call-start = ((), (), s32[]{:S(2)}) async-start(), calls=%async_computation | async-start | bytes 524288 | tf_op jit(solution)/shard_map/psum | solution.py:92
  11.3 91.3 %copy-start.10 = (u32[256]{0:T(256)S(1)}, u32[256]{0:T(256)}, u32[]{:S(2)}) copy-start(u32[256]{0:T(256)} %constant.95) | copy-start | bytes 3076
  15.7 339.3 %copy-start.11 = (s32[64]{0:T(128)S(1)}, s32[64]{0:T(128)}, u32[]{:S(2)}) copy-start(s32[64]{0:T(128)} %param.8) | copy-start | bytes 772
  92.4 21.6 %collective-permute-start.6 = (f32[8,8192]{1,0:T(8,128)S(1)}, f32[8,8192]{1,0:T(8,128)S(1)}, u32[]{:S(2)}, u32[]{:S(2)}) collective-permute-start(f32[8,8192]{1,0:T(8,128)S(1)} %fusion), channel_id=1, source_target_pairs={{0,56},{8,64},{16,72},{24,80},{32,88},{40,96},{48,104},{56,112},{6... | collective-permute-start | bytes 786440
  93.8 24.0 %collective-permute-start.5 = (f32[8,8192]{1,0:T(8,128)S(1)}, f32[8,8192]{1,0:T(8,128)S(1)}, u32[]{:S(2)}, u32[]{:S(2)}) collective-permute-start(f32[8,8192]{1,0:T(8,128)S(1)} %fusion), channel_id=1, source_target_pairs={{0,48},{8,56},{16,64},{24,72},{32,80},{40,88},{48,96},{56,104},{64... | collective-permute-start | bytes 786440
  95.1 11.3 %collective-permute-start.7 = (f32[6,8192]{1,0:T(8,128)S(1)}, f32[6,8192]{1,0:T(8,128)S(1)}, u32[]{:S(2)}, u32[]{:S(2)}) collective-permute-start(f32[6,8192]{1,0:T(8,128)S(1)} %slice.16), channel_id=1, source_target_pairs={{0,64},{8,72},{16,80},{24,88},{32,96},{40,104},{48,112},{56,120},{... | collective-permute-start | bytes 589832
  96.4 170.9 %collective-permute-start.4 = (f32[8,8192]{1,0:T(8,128)S(1)}, f32[8,8192]{1,0:T(8,128)S(1)}, u32[]{:S(2)}, u32[]{:S(2)}) collective-permute-start(f32[8,8192]{1,0:T(8,128)S(1)} %fusion), channel_id=1, source_target_pairs={{0,40},{8,48},{16,56},{24,64},{32,72},{40,80},{48,88},{56,96},{64,... | collective-permute-start | bytes 786440
  98.1 169.2 %collective-permute-start.3 = (f32[8,8192]{1,0:T(8,128)S(1)}, f32[8,8192]{1,0:T(8,128)S(1)}, u32[]{:S(2)}, u32[]{:S(2)}) collective-permute-start(f32[8,8192]{1,0:T(8,128)S(1)} %fusion), channel_id=1, source_target_pairs={{0,32},{8,40},{16,48},{24,56},{32,64},{40,72},{48,80},{56,88},{64,... | collective-permute-start | bytes 786440
  106.4 160.9 %collective-permute-start.2 = (f32[8,8192]{1,0:T(8,128)S(1)}, f32[8,8192]{1,0:T(8,128)S(1)}, u32[]{:S(2)}, u32[]{:S(2)}) collective-permute-start(f32[8,8192]{1,0:T(8,128)S(1)} %fusion), channel_id=1, source_target_pairs={{0,24},{8,32},{16,40},{24,48},{32,56},{40,64},{48,72},{56,80},{64,... | collective-permute-start | bytes 786440
  114.1 153.2 %collective-permute-start.1 = (f32[8,8192]{1,0:T(8,128)S(1)}, f32[8,8192]{1,0:T(8,128)S(1)}, u32[]{:S(2)}, u32[]{:S(2)}) collective-permute-start(f32[8,8192]{1,0:T(8,128)S(1)} %fusion), channel_id=1, source_target_pairs={{0,16},{8,24},{16,32},{24,40},{32,48},{40,56},{48,64},{56,72},{64,... | collective-permute-start | bytes 786440
  117.8 151.1 %collective-permute-start = (f32[8,8192]{1,0:T(8,128)S(1)}, f32[8,8192]{1,0:T(8,128)}, u32[]{:S(2)}, u32[]{:S(2)}) collective-permute-start(f32[8,8192]{1,0:T(8,128)S(1)} %fusion), channel_id=1, source_target_pairs={{0,8},{8,16},{16,24},{24,32},{32,40},{40,48},{48,56},{56,64},{64,7... | collective-permute-start | bytes 786440
  267.3 0.7 copy-start.6
  267.3 0.8 copy-start.7
  267.3 0.9 copy-start.8
  268.2 0.7 copy-start.9
  281.0 123.5 %all-gather.3.cloned.1.call-start = ((), (), s32[]{:S(2)}) async-start(), calls=%async_computation.1 | async-start | bytes 4325376 | tf_op jit(solution)/shard_map/all_gather | solution.py:107
  483.2 3.2 copy-start.5
  501.3 3.2 copy-start.3
  548.0 3.2 copy-start.4
  566.2 3.2 copy-start.2
  569.3 49.3 %copy-start.1 = (f32[32,64]{1,0:T(8,128)S(1)}, f32[32,64]{1,0:T(8,128)}, u32[]{:S(2)}) copy-start(f32[32,64]{1,0:T(8,128)} %param.9) | copy-start | bytes 24580
Sparse Core Ops, SparseCore 0:
  281.1 70.9 all-reduce.4
  355.3 49.1 all-gather.2
where the time goes:
time: 628 us; the launch traced here: 625 us
  blocking collectives  245 us (39%)
  waiting for transfers between devices  114 us (18%)
  local copies, waits for them, and re-layouts  108 us (17%)
  other arithmetic  79.9 us (13%)
  starting transfers between devices  33.1 us (5%)
  matrix products  29.4 us (5%)
  between operations  15.7 us (2%)
    unnamed x2, blocking collectives  194 us
    another operation x8, local copies, waits for them, and re-layouts, rotate_refs(): jnp.stack([real_part * cosine - imag_part * sine, real_part * sine + imag...  73.9 us
    psum x1, waiting for transfers between devices, local(): numer, denom = lax.psum((numer, denom), 'rot')  70.8 us
    all_gather x1, waiting for transfers between devices, local(): piece = lax.all_gather(refs, 'dom', axis=0, tiled=True)  41.3 us
    another operation x8, other arithmetic, rotate_refs(): jnp.stack([real_part * cosine - imag_part * sine, real_part * sine + imag...  41.1 us
    unnamed x8, starting transfers between devices  33 us
    another operation x3, other arithmetic  32.9 us
    pmax x1, blocking collectives, local(): highest = lax.pmax(best, 'rot')  30.7 us
  transfers between devices with their start and end apart: 10, of which 3 were waited for; matrix products, arithmetic and copies ran while one was open for 1% of the time, Pallas kernels for 0%

commit v1 on v0

v1 whole, which is shorter than its diff:
```python
import math

import jax
import jax.numpy as jnp
from jax import lax
from jax.sharding import PartitionSpec as P

CYCLES = 64
MFREQ = 64
CLS_DEV = 6
K = 8192


def angles(index, total):
    freqs = jnp.arange(MFREQ, dtype=jnp.int32)
    phase = freqs[None, :] * index[:, None] % total
    return phase.astype(jnp.float32) * (2.0 * math.pi / total)


def derotate(spec, rotation, ctf_rows, total):
    count = spec.shape[0]
    layered = spec.reshape(count, 2, CYCLES, MFREQ)
    real_part = layered[:, 0]
    imag_part = layered[:, 1]
    angle = angles(rotation, total)
    cosine = jnp.cos(angle)[:, None, :]
    sine = jnp.sin(angle)[:, None, :]
    turned = jnp.stack(
        [real_part * cosine + imag_part * sine, imag_part * cosine - real_part * sine], axis=1
    )
    return (turned * ctf_rows[:, None, :, None]).reshape(count, K)


def rotate_all(refs, total):
    count = refs.shape[0]
    layered = refs.astype(jnp.float32).reshape(count, 2, CYCLES, MFREQ)
    real_part = layered[None, :, 0]
    imag_part = layered[None, :, 1]
    angle = angles(jnp.arange(total, dtype=jnp.int32), total)
    cosine = jnp.cos(angle)[:, None, None, :]
    sine = jnp.sin(angle)[:, None, None, :]
    turned = jnp.stack(
        [real_part * cosine - imag_part * sine, real_part * sine + imag_part * cosine], axis=2
    )
    return turned.reshape(total * count, K).astype(jnp.bfloat16)


def local(particles, assign, rot_index, group, ctf_table):
    dom_rank = lax.axis_index("dom")
    rot_count = lax.axis_size("rot")
    rot_rank = lax.axis_index("rot")
    dom_count = lax.axis_size("dom")
    classes = CLS_DEV * dom_count
    block = classes // rot_count
    owners_per_block = block // CLS_DEV
    total = 8 * rot_count
    count = particles.shape[0]

    ctf_rows = ctf_table[group]
    spec = particles.astype(jnp.float32)
    weighted = derotate(spec, rot_index, ctf_rows, total)
    first_class = rot_rank * block
    member = (
        (first_class + jnp.arange(block, dtype=jnp.int32))[:, None] == assign[None, :]
    ).astype(jnp.float32)
    numer = jnp.dot(
        member, weighted, precision=lax.Precision.HIGHEST, preferred_element_type=jnp.float32
    )
    denom = jnp.dot(
        member,
        ctf_rows * ctf_rows,
        precision=lax.Precision.HIGHEST,
        preferred_element_type=jnp.float32,
    )
    numer, denom = lax.psum((numer, denom), "dom")
    plain = numer.reshape(block, 2, CYCLES, MFREQ) / (denom[:, None, :, None] + 1.0)
    spread = jnp.mean(plain * plain, axis=(1, 2, 3))
    refs_block = (
        (plain / jnp.sqrt(spread + 1e-06)[:, None, None, None])
        .reshape(block, K)
        .astype(jnp.bfloat16)
    )

    modulated = (
        (spec.reshape(count, 2, CYCLES, MFREQ) * ctf_rows[:, None, :, None])
        .reshape(count, K)
        .astype(jnp.bfloat16)
    )
    turned = rotate_all(refs_block, total)
    found = lax.dot_general(
        modulated, turned, (((1,), (1,)), ((), ())), preferred_element_type=jnp.float32
    )
    best = jnp.max(found.reshape(count, total, block), axis=1) * (1.0 / math.sqrt(K))
    best_scores = lax.all_to_all(best, "rot", 0, 1, tiled=True)

    mine = lax.dynamic_slice_in_dim(refs_block, (dom_rank % owners_per_block) * CLS_DEV, CLS_DEV, 0)
    keep = (dom_rank // owners_per_block) == rot_rank
    refs = lax.psum(jnp.where(keep, mine, jnp.zeros_like(mine)), "rot")
    return (refs, best_scores)


def solution(mesh):
    in_specs = (P("dom", None), P("dom"), P("dom"), P("dom"), P())
    out_specs = (P("dom", None), P(("dom", "rot"), None))
    return jax.shard_map(local, mesh=mesh, in_specs=in_specs, out_specs=out_specs, check_vma=False)
```

time: 628 us -> 328 us (0.52)
  waiting for transfers between devices: 114 us -> 0.06 us
  blocking collectives: 245 us -> 140 us
  starting transfers between devices: 33.1 us -> 0.08 us
  local copies, waits for them, and re-layouts: 108 us -> 90 us
  other arithmetic: 79.9 us -> 63.3 us
  matrix products: 29.4 us -> 15.2 us
    unnamed x2 -> x0, blocking collectives: 194 us -> none
    psum x1, blocking collectives: 20 us -> 124 us  [local(): numer, denom = lax.psum((numer, denom), 'dom')]
    psum x1 -> x2, waiting for transfers between devices: 70.8 us -> 0.02 us  [the longest x1 0.02 us: local(): numer, denom = lax.psum((numer, denom), 'dom')]
    another operation x8 -> x1, local copies, waits for them, and re-layouts: 73.9 us -> 4.79 us  [derotate(): jnp.stack([real_part * cosine + imag_part * sine, imag_part * cosine - re...]
    convert_element_type x0 -> x1, local copies, waits for them, and re-layouts: none -> 64.5 us  [rotate_all(): return turned.reshape(total * count, K).astype(jnp.bfloat16)]
    all_gather x1 -> x0, waiting for transfers between devices: 41.3 us -> none  [local(): piece = lax.all_gather(refs, 'dom', axis=0, tiled=True)]
    unnamed x8 -> x0, starting transfers between devices: 33 us -> none
    pmax x1 -> x0, blocking collectives: 30.7 us -> none  [local(): highest = lax.pmax(best, 'rot')]
  transfers between devices with their start and end apart: 10 -> 2, of which waited for: 3 -> 0; matrix products, arithmetic and copies ran while one was open for 1% -> 42% of each run, Pallas kernels for 0% -> 0%
where the time goes in v1:
time: 328 us; the launch traced here: 322 us
  blocking collectives  140 us (43%)
  local copies, waits for them, and re-layouts  90 us (27%)
  other arithmetic  63.3 us (19%)
  matrix products  15.2 us (5%)
  between operations  14.2 us (4%)
    psum x1, blocking collectives, local(): numer, denom = lax.psum((numer, denom), 'dom')  124 us
    convert_element_type x1, local copies, waits for them, and re-layouts, rotate_all(): return turned.reshape(total * count, K).astype(jnp.bfloat16)  64.5 us
    another operation x1, other arithmetic, rotate_all(): jnp.stack([real_part * cosine - imag_part * sine, real_part * sine + imag...  33.9 us
    another operation x1, other arithmetic  19.7 us
    all_to_all x1, blocking collectives, local(): best_scores = lax.all_to_all(best, 'rot', 0, 1, tiled=True)  16 us
    dot_general x1, matrix products, local(): lax.dot_general(modulated, turned, (((1,), (1,)), ((), ())), preferred_el...  11.7 us
  transfers between devices with their start and end apart: 2, of which 0 were waited for; matrix products, arithmetic and copies ran while one was open for 42% of the time, Pallas kernels for 0%

profile of v1, /device:TPU:2, one launch (start us, length us, event | category | flops | bytes accessed | tf_op | source)
XLA Modules:
  0.0 322.4 jit_solution(13810873585188060015)
XLA Ops:
  7.2 4.3 %reshape.146 = f32[64,2,64,64]{3,2,1,0:T(8,128)} reshape(bf16[64,8192]{1,0:T(8,128)(2,1)} %param.5) | data formatting | bytes 3145728 | tf_op jit(solution)/shard_map/reshape | solution.py:22
  11.8 2.9 multiply_add_fusion
  14.6 2.4 pad_maximum_fusion.1
  17.0 4.8 %stack.14 = f32[64,8192]{1,0:T(8,128)} reshape(f32[64,2,64,64]{3,2,1,0:T(8,128)} %pad_maximum_fusion.1) | data formatting | bytes 4194304 | tf_op jit(solution)/shard_map/stack | solution.py:28
  21.8 0.6 gather_fusion
  22.4 2.5 mul.248
  25.0 3.5 %mul.249 = f32[64,8192]{1,0:T(8,128)S(1)} reshape(f32[64,2,64,64]{3,2,1,0:T(8,128)} %mul.248) | data formatting | bytes 4194304 | tf_op jit(solution)/shard_map/mul | solution.py:31
  28.5 3.4 %fusion = f32[24,8192]{1,0:T(8,128)} fusion(f32[64,8192]{1,0:T(8,128)} %stack.14, f32[64,8192]{1,0:T(8,128)S(1)} %mul.249, s32[64]{0:T(128)S(1)} %copy-done.4, s32[24]{0:T(128)S(1)} %iota_add_fusion), kind=kOutput, calls=%fused_computation.6 | convolution fusion | flops 151520768 | bytes 4981088 | tf_op jit(solution)/shard_map/dot_general | solution.py:66
  32.2 123.6 %psum.22 = f32[24,64]{1,0:T(8,128)S(1)} all-reduce(f32[24,64]{1,0:T(8,128)S(1)} %fusion.13), channel_id=1, replica_groups=mesh['dom'=32,'rot'=8] {'dom'}, use_global_device_ids=true, to_apply=%region_1.2 | all-reduce | flops 1536 | bytes 12288 | tf_op jit(solution)/shard_map/psum | solution.py:75
  155.8 1.4 div.34
  157.2 1.9 div.35
  159.3 1.4 multiply_reduce_fusion
  160.7 1.3 divide_convert_fusion
  162.0 1.9 reshape.150
  163.9 0.7 dynamic-slice_select_fusion
  164.6 1.5 slice_bitcast_fusion.1
  166.1 19.7 %subtract_convert_fusion = (bf16[64,24,1,64,64]{4,3,2,0,1:T(8,128)(2,1)}, bf16[64,24,1,64,64]{4,3,2,0,1:T(8,128)(2,1)}) fusion(f32[64,64]{1,0:T(8,128)S(1)} %get-tuple-element.10, f32[24,64,64]{2,1,0:T(8,128)S(1)} %get-tuple-element.7, f32[64,64]{1,0:T(8,128)S(1)} %get-tuple-element.11, f32[24,64,64]{2,1,0:T(8,128)S(1)} %get-tuple-element.6), kind=kLoop, calls=%fused_computation.3 | loop fusion | flops 50331648 | bytes 25985024 | tf_op jit(solution)/shard_map/convert.1
  185.8 33.9 %pad_maximum_fusion = bf16[64,24,2,64,64]{4,3,2,0,1:T(8,128)(2,1)} fusion(bf16[64,24,1,64,64]{4,3,2,0,1:T(8,128)(2,1)} %get-tuple-element.5, bf16[64,24,1,64,64]{4,3,2,0,1:T(8,128)(2,1)} %get-tuple-element.4), kind=kLoop, calls=%fused_computation.1 | loop fusion | flops 12582912 | bytes 50331648 | tf_op jit(solution)/shard_map/stack | solution.py:42
  219.7 64.5 %convert_element_type.47 = bf16[64,24,8192]{2,0,1:T(8,128)(2,1)} reshape(bf16[64,24,2,64,64]{4,3,2,0,1:T(8,128)(2,1)} %pad_maximum_fusion) | data formatting | bytes 50331648 | tf_op jit(solution)/shard_map/convert_element_type | solution.py:45
  284.2 11.7 %convolution_reduce_fusion = f32[64,24]{0,1:T(8,128)S(1)} fusion(bf16[64,24,8192]{2,0,1:T(8,128)(2,1)} %convert_element_type.47, f32[64,8192]{1,0:T(8,128)S(1)} %mul.249, bf16[64,8192]{1,0:T(8,128)(2,1)S(1)} %copy-done.2), kind=kOutput, calls=%fused_computation.10 | convolution fusion | flops 1612282368 | bytes 28317696 | tf_op jit(solution)/shard_map/dot_general | solution.py:90
  296.1 16.0 %all_to_all.16 = f32[8,1,192]{2,1,0:T(1,128)S(1)} all-to-all(f32[8,1,192]{2,1,0:T(1,128)S(1)} %reshape.161), channel_id=1, replica_groups=mesh['dom'=32,'rot'=8] {'rot'}, dimensions={0} | all-to-all | bytes 12288 | tf_op jit(solution)/shard_map/all_to_all | solution.py:94
  312.6 0.7 reduce.1
  313.3 0.7 all_to_all.14
  314.0 1.6 copy.12
  (32 shorter events, 1.5 us)
Async XLA Ops:
  7.2 14.6 %copy-start = (f32[32,64]{1,0:T(8,128)S(1)}, f32[32,64]{1,0:T(8,128)}, u32[]{:S(2)}) copy-start(f32[32,64]{1,0:T(8,128)} %param.9) | copy-start | bytes 24580
  7.2 4.4 %copy-start.3 = (s32[64]{0:T(128)S(1)}, s32[64]{0:T(128)}, u32[]{:S(2)}) copy-start(s32[64]{0:T(128)} %param.7) | copy-start | bytes 772
  7.2 152.1 %all-reduce.3.cloned.1.call-start = ((), (), s32[]{:S(2)}) async-start(), calls=%async_computation.1 | async-start | bytes 1572864 | tf_op jit(solution)/shard_map/psum | solution.py:75
  17.0 4.8 %copy-start.5 = (s32[64]{0:T(128)S(1)}, s32[64]{0:T(128)}, u32[]{:S(2)}) copy-start(s32[64]{0:T(128)} %param.8) | copy-start | bytes 772
  24.9 3.6 %copy-start.4 = (s32[64]{0:T(128)S(1)}, s32[64]{0:T(128)}, u32[]{:S(2)}) copy-start(s32[64]{0:T(128)} %param.6) | copy-start | bytes 772
  31.9 282.1 %all-reduce.5.cloned.1.call-start = ((), (), s32[]{:S(2)}) async-start(), calls=%async_computation.2 | async-start | bytes 262144 | tf_op jit(solution)/shard_map/psum | solution.py:98
  219.7 64.5 %copy-start.2 = (bf16[64,8192]{1,0:T(8,128)(2,1)S(1)}, bf16[64,8192]{1,0:T(8,128)(2,1)}, u32[]{:S(2)}) copy-start(bf16[64,8192]{1,0:T(8,128)(2,1)} %param.5) | copy-start | bytes 3145732
  284.2 31.4 %copy-start.1 = (f32[32,64]{1,0:T(8,128)S(1)}, f32[32,64]{1,0:T(8,128)}, u32[]{:S(2)}) copy-start(f32[32,64]{1,0:T(8,128)} %param.9) | copy-start | bytes 24580
Sparse Core Ops, SparseCore 0:
  32.0 116.8 all-reduce.2
  164.7 75.4 all-reduce.4

commit v2 on v1

--- a/solution.py
+++ b/solution.py
@@ -33,13 +33,13 @@
 
 def rotate_all(refs, total):
     count = refs.shape[0]
-    layered = refs.astype(jnp.float32).reshape(count, 2, CYCLES, MFREQ)
-    real_part = layered[None, :, 0]
-    imag_part = layered[None, :, 1]
+    half = K // 2
+    real_part = refs[None, :, :half]
+    imag_part = refs[None, :, half:]
     angle = angles(jnp.arange(total, dtype=jnp.int32), total)
-    cosine = jnp.cos(angle)[:, None, None, :]
-    sine = jnp.sin(angle)[:, None, None, :]
-    turned = jnp.stack(
+    cosine = jnp.tile(jnp.cos(angle), (1, CYCLES))[:, None, :]
+    sine = jnp.tile(jnp.sin(angle), (1, CYCLES))[:, None, :]
+    turned = jnp.concatenate(
         [real_part * cosine - imag_part * sine, real_part * sine + imag_part * cosine], axis=2
     )
     return turned.reshape(total * count, K).astype(jnp.bfloat16)
@@ -72,21 +72,35 @@
         precision=lax.Precision.HIGHEST,
         preferred_element_type=jnp.float32,
     )
-    numer, denom = lax.psum((numer, denom), "dom")
-    plain = numer.reshape(block, 2, CYCLES, MFREQ) / (denom[:, None, :, None] + 1.0)
-    spread = jnp.mean(plain * plain, axis=(1, 2, 3))
-    refs_block = (
-        (plain / jnp.sqrt(spread + 1e-06)[:, None, None, None])
-        .reshape(block, K)
-        .astype(jnp.bfloat16)
+    chunks = dom_count
+    width = K // chunks
+    per_chunk = width // MFREQ
+    payload = jnp.concatenate(
+        [
+            numer.reshape(block, chunks, width).transpose(1, 0, 2),
+            jnp.broadcast_to(denom[None], (chunks, block, CYCLES)),
+        ],
+        axis=2,
     )
+    summed = jnp.sum(lax.all_to_all(payload, "dom", 0, 0, tiled=True), axis=0)
+    numer_chunk = summed[:, :width].reshape(block, per_chunk, MFREQ)
+    first_cycle = (dom_rank * per_chunk) % CYCLES
+    denom_chunk = lax.dynamic_slice_in_dim(summed[:, width:], first_cycle, per_chunk, 1)
+    plain_chunk = (numer_chunk / (denom_chunk[:, :, None] + 1.0)).reshape(block, width)
+    plain = lax.all_to_all(
+        jnp.broadcast_to(plain_chunk[None], (chunks, block, width)), "dom", 0, 0, tiled=True
+    )
+    plain = plain.transpose(1, 0, 2).reshape(block, K)
+    spread = jnp.mean(plain * plain, axis=1)
+    refs_f32 = plain / jnp.sqrt(spread + 1e-06)[:, None]
+    refs_block = refs_f32.astype(jnp.bfloat16)
 
     modulated = (
         (spec.reshape(count, 2, CYCLES, MFREQ) * ctf_rows[:, None, :, None])
         .reshape(count, K)
         .astype(jnp.bfloat16)
     )
-    turned = rotate_all(refs_block, total)
+    turned = rotate_all(refs_block.astype(jnp.float32), total)
     found = lax.dot_general(
         modulated, turned, (((1,), (1,)), ((), ())), preferred_element_type=jnp.float32
     )
@@ -94,8 +108,10 @@
     best_scores = lax.all_to_all(best, "rot", 0, 1, tiled=True)
 
     mine = lax.dynamic_slice_in_dim(refs_block, (dom_rank % owners_per_block) * CLS_DEV, CLS_DEV, 0)
-    keep = (dom_rank // owners_per_block) == rot_rank
-    refs = lax.psum(jnp.where(keep, mine, jnp.zeros_like(mine)), "rot")
+    spread_out = lax.all_to_all(
+        jnp.broadcast_to(mine[None], (rot_count,) + mine.shape), "rot", 0, 0, tiled=True
+    )
+    refs = lax.dynamic_index_in_dim(spread_out, dom_rank // owners_per_block, 0, keepdims=False)
     return (refs, best_scores)
 
 

time: 328 us -> 148 us (0.45)
  blocking collectives: 140 us -> 0 us
  local copies, waits for them, and re-layouts: 90 us -> 30.7 us
  waiting for transfers between devices: 0.06 us -> 55.3 us
  other arithmetic: 63.3 us -> 21.3 us
  starting transfers between devices: 0.08 us -> 24.7 us
  between operations: 14.2 us -> 0.88 us
    psum x1 -> x0, blocking collectives: 124 us -> none  [local(): numer, denom = lax.psum((numer, denom), 'dom')]
    convert_element_type x1 -> x0, local copies, waits for them, and re-layouts: 64.5 us -> none  [rotate_all(): return turned.reshape(total * count, K).astype(jnp.bfloat16)]
    all_to_all x0 -> x4, waiting for transfers between devices: none -> 55.3 us  [the longest x1 26.1 us: local(): lax.all_to_all(jnp.broadcast_to(mine[None], (rot_count,) + mine.shape), '...]
    another operation x2 -> x1, other arithmetic: 53.6 us -> 10.8 us  [the longest x1 33.9 us: rotate_all(): jnp.stack([real_part * cosine - imag_part * sine, real_part * sine + imag...]
    all_to_all x0 -> x4, starting transfers between devices: none -> 24.7 us  [the longest x1 8.46 us: local(): best_scores = lax.all_to_all(best, 'rot', 0, 1, tiled=True)]
    all_to_all x1 -> x0, blocking collectives: 16 us -> none  [local(): best_scores = lax.all_to_all(best, 'rot', 0, 1, tiled=True)]
    another operation x0 -> x4, local copies, waits for them, and re-layouts: none -> 8.81 us  [the longest x2 4.41 us: rotate_all(): sine = jnp.tile(jnp.sin(angle), (1, CYCLES))[:, None, :]]
  transfers between devices with their start and end apart: 2 -> 4, of which waited for: 0 -> 4; matrix products, arithmetic and copies ran while one was open for 42% -> 7% of each run, Pallas kernels for 0% -> 0%
where the time goes in v2:
time: 148 us; the launch traced here: 146 us
  waiting for transfers between devices  55.3 us (37%)
  local copies, waits for them, and re-layouts  30.7 us (21%)
  starting transfers between devices  24.7 us (17%)
  other arithmetic  21.3 us (14%)
  matrix products  12.6 us (9%)
    all_to_all x1, waiting for transfers between devices, local(): lax.all_to_all(jnp.broadcast_to(mine[None], (rot_count,) + mine.shape), '...  26.1 us
    all_to_all x1, waiting for transfers between devices, local(): summed = jnp.sum(lax.all_to_all(payload, 'dom', 0, 0, tiled=True), axis=0)  17.4 us
    dot_general x1, matrix products, local(): lax.dot_general(modulated, turned, (((1,), (1,)), ((), ())), preferred_el...  11.6 us
    another operation x1, other arithmetic  10.8 us
    all_to_all x1, starting transfers between devices, local(): best_scores = lax.all_to_all(best, 'rot', 0, 1, tiled=True)  8.46 us
    all_to_all x1, waiting for transfers between devices, local(): best_scores = lax.all_to_all(best, 'rot', 0, 1, tiled=True)  7.68 us
    all_to_all x1, starting transfers between devices, local(): summed = jnp.sum(lax.all_to_all(payload, 'dom', 0, 0, tiled=True), axis=0)  7.62 us
    mul x2, local copies, waits for them, and re-layouts, derotate(): return (turned * ctf_rows[:, None, :, None]).reshape(count, K)  6.08 us
  transfers between devices with their start and end apart: 4, of which 4 were waited for; matrix products, arithmetic and copies ran while one was open for 7% of the time, Pallas kernels for 0%

profile of v2, /device:TPU:2, one launch (start us, length us, event | category | flops | bytes accessed | tf_op | source)
XLA Modules:
  0.0 145.6 jit_solution(8342705551566969074)
XLA Ops:
  1.3 4.3 %reshape.155 = f32[64,2,64,64]{3,2,1,0:T(8,128)} reshape(bf16[64,8192]{1,0:T(8,128)(2,1)} %param.5) | data formatting | bytes 3145728 | tf_op jit(solution)/shard_map/reshape | solution.py:22
  5.9 2.9 %multiply_add_fusion = (f32[64,1,64,64]{3,2,1,0:T(8,128)S(1)}, f32[64,1,64,64]{3,2,1,0:T(8,128)S(1)}) fusion(f32[64,2,64,64]{3,2,1,0:T(8,128)} %reshape.155, f32[64,64]{1,0:T(8,128)S(1)} %get-tuple-element.9, f32[64,64]{1,0:T(8,128)S(1)} %get-tuple-element.8), kind=kLoop, calls=%fused_computation.13 | loop fusion | flops 1572864 | bytes 4227072 | tf_op jit(solution)/shard_map/add | solution.py:29
  8.7 2.4 %pad_maximum_fusion = f32[64,2,64,64]{3,2,1,0:T(8,128)} fusion(f32[64,1,64,64]{3,2,1,0:T(8,128)S(1)} %get-tuple-element.3, f32[64,1,64,64]{3,2,1,0:T(8,128)S(1)} %get-tuple-element.2), kind=kLoop, calls=%fused_computation.7 | loop fusion | flops 524288 | bytes 4194304 | tf_op jit(solution)/shard_map/stack | solution.py:28
  11.1 4.8 %stack.8 = f32[64,8192]{1,0:T(8,128)} reshape(f32[64,2,64,64]{3,2,1,0:T(8,128)} %pad_maximum_fusion) | data formatting | bytes 4194304 | tf_op jit(solution)/shard_map/stack | solution.py:28
  16.5 2.6 %mul.227 = f32[64,2,64,64]{3,2,1,0:T(8,128)} broadcast(f32[64,64]{1,0:T(8,128)S(1)} %gather_fusion), dimensions={0,2} | broadcast | bytes 2113536 | tf_op jit(solution)/shard_map/mul | solution.py:31
  19.0 3.5 %mul.228 = f32[64,8192]{1,0:T(8,128)S(1)} reshape(f32[64,2,64,64]{3,2,1,0:T(8,128)} %mul.227) | data formatting | bytes 4194304 | tf_op jit(solution)/shard_map/mul | solution.py:31
  22.8 1.8 %mul.229 = f32[64,8192]{1,0:T(8,128)S(1)} multiply(f32[64,8192]{1,0:T(8,128)} %stack.8, f32[64,8192]{1,0:T(8,128)S(1)} %mul.228) | non-fusion elementwise | flops 524288 | bytes 6291456 | tf_op jit(solution)/shard_map/mul | solution.py:31
  25.5 1.1 pad_maximum_fusion.1
  26.6 7.6 %all-to-all-start = ((f32[32,24,320]{2,1,0:T(8,128)}), f32[32,24,320]{2,1,0:T(8,128)S(1)}, u32[]{:S(2)}, u32[]{:S(2)}) async-start(f32[32,24,320]{2,1,0:T(8,128)} %pad_maximum_fusion.1), calls=%async_computation | async-start | bytes 2359296 | tf_op jit(solution)/shard_map/all_to_all | solution.py:85
  34.2 17.4 %all-to-all-done = f32[32,24,320]{2,1,0:T(8,128)S(1)} async-done(((f32[32,24,320]{2,1,0:T(8,128)}), f32[32,24,320]{2,1,0:T(8,128)S(1)}, u32[]{:S(2)}, u32[]{:S(2)}) %all-to-all-start) | async-done | bytes 983072 | tf_op jit(solution)/shard_map/all_to_all | solution.py:85
  52.0 0.9 broadcast_in_dim.10
  52.9 5.1 %all-to-all-start.1 = ((f32[32,24,256]{2,1,0:T(8,128)}), f32[32,24,256]{2,1,0:T(8,128)S(1)}, u32[]{:S(2)}, u32[]{:S(2)}) async-start(f32[32,24,256]{2,1,0:T(8,128)} %broadcast_in_dim.10), calls=%async_computation.1 | async-start | bytes 1572864 | tf_op jit(solution)/shard_map/all_to_all | solution.py:90
  58.2 1.5 %tile.26 = f32[64,64,64]{2,1,0:T(8,128)} broadcast(f32[64,64]{1,0:T(8,128)S(1)} %fusion.31), dimensions={0,2} | broadcast | bytes 1064960 | tf_op jit(solution)/shard_map/tile | solution.py:41
  59.7 2.9 %tile.27 = f32[64,4096]{1,0:T(8,128)} reshape(f32[64,64,64]{2,1,0:T(8,128)} %tile.26) | data formatting | bytes 2097152 | tf_op jit(solution)/shard_map/tile | solution.py:41
  62.7 1.5 %tile.24 = f32[64,64,64]{2,1,0:T(8,128)} broadcast(f32[64,64]{1,0:T(8,128)S(1)} %fusion.32), dimensions={0,2} | broadcast | bytes 1064960 | tf_op jit(solution)/shard_map/tile | solution.py:40
  64.2 2.9 %tile.25 = f32[64,4096]{1,0:T(8,128)} reshape(f32[64,64,64]{2,1,0:T(8,128)} %tile.24) | data formatting | bytes 2097152 | tf_op jit(solution)/shard_map/tile | solution.py:40
  67.1 4.2 %all-to-all-done.1 = f32[32,24,256]{2,1,0:T(8,128)S(1)} async-done(((f32[32,24,256]{2,1,0:T(8,128)}), f32[32,24,256]{2,1,0:T(8,128)S(1)}, u32[]{:S(2)}, u32[]{:S(2)}) %all-to-all-start.1) | async-done | bytes 786464 | tf_op jit(solution)/shard_map/all_to_all | solution.py:90
  72.9 10.8 %subtract_convert_fusion = (bf16[64,24,4096]{2,0,1:T(8,128)(2,1)}, bf16[64,24,4096]{2,0,1:T(8,128)(2,1)}) fusion(f32[64,4096]{1,0:T(8,128)S(1)} %copy-done.1, f32[24,4096]{1,0:T(8,128)S(1)} %get-tuple-element.7, f32[64,4096]{1,0:T(8,128)S(1)} %copy-done.2, f32[24,4096]{1,0:T(8,128)S(1)} %get-tuple-element.6), kind=kLoop, calls=%fused_computation.6 | loop fusion | flops 50331648 | bytes 28049408 | tf_op jit(solution)/shard_map/convert
  83.7 11.6 %fusion.10 = f32[64,24]{0,1:T(8,128)S(1)} fusion(bf16[64,24,4096]{2,0,1:T(8,128)(2,1)} %get-tuple-element.5, bf16[64,24,4096]{2,0,1:T(8,128)(2,1)} %get-tuple-element.4, f32[64,8192]{1,0:T(8,128)S(1)} %mul.228, bf16[64,8192]{1,0:T(8,128)(2,1)S(1)} %copy-done.3), kind=kOutput, calls=%fused_computation.16 | convolution fusion | flops 1662614016 | bytes 28317696 | tf_op jit(solution)/shard_map/dot_general | solution.py:104
  96.1 8.5 %all-to-all-start.3 = ((f32[8,1,192]{2,1,0:T(1,128)}), f32[8,1,192]{2,1,0:T(1,128)S(1)}, u32[]{:S(2)}, u32[]{:S(2)}) async-start(f32[8,1,192]{2,1,0:T(1,128)} %reshape.168), calls=%async_computation.3 | async-start | bytes 16384 | tf_op jit(solution)/shard_map/all_to_all | solution.py:108
  104.6 7.7 %all-to-all-done.3 = f32[8,1,192]{2,1,0:T(1,128)S(1)} async-done(((f32[8,1,192]{2,1,0:T(1,128)}), f32[8,1,192]{2,1,0:T(1,128)S(1)}, u32[]{:S(2)}, u32[]{:S(2)}) %all-to-all-start.3) | async-done | bytes 6176 | tf_op jit(solution)/shard_map/all_to_all | solution.py:108
  112.3 1.0 broadcast_in_dim.11
  113.3 3.6 %all-to-all-start.2 = ((bf16[8,6,8192]{2,1,0:T(8,128)(2,1)}), bf16[8,6,8192]{2,1,0:T(8,128)(2,1)S(1)}, u32[]{:S(2)}, u32[]{:S(2)}) async-start(bf16[8,6,8192]{2,1,0:T(8,128)(2,1)} %broadcast_in_dim.11), calls=%async_computation.2 | async-start | bytes 2097152 | tf_op jit(solution)/shard_map/all_to_all | solution.py:111
  118.8 26.1 %all-to-all-done.2 = bf16[8,6,8192]{2,1,0:T(8,128)(2,1)S(1)} async-done(((bf16[8,6,8192]{2,1,0:T(8,128)(2,1)}), bf16[8,6,8192]{2,1,0:T(8,128)(2,1)S(1)}, u32[]{:S(2)}, u32[]{:S(2)}) %all-to-all-start.2) | async-done | bytes 786464 | tf_op jit(solution)/shard_map/all_to_all | solution.py:111
  (43 shorter events, 8.1 us)
Async XLA Ops:
  0.6 15.3 %copy-start = (f32[32,64]{1,0:T(8,128)S(1)}, f32[32,64]{1,0:T(8,128)}, u32[]{:S(2)}) copy-start(f32[32,64]{1,0:T(8,128)} %param.9) | copy-start | bytes 24580
  0.6 5.0 %copy-start.4 = (s32[64]{0:T(128)S(1)}, s32[64]{0:T(128)}, u32[]{:S(2)}) copy-start(s32[64]{0:T(128)} %param.7) | copy-start | bytes 772
  19.0 3.5 %copy-start.5 = (s32[64]{0:T(128)S(1)}, s32[64]{0:T(128)}, u32[]{:S(2)}) copy-start(s32[64]{0:T(128)} %param.6) | copy-start | bytes 772
  26.6 25.0 %all-to-all-start = ((f32[32,24,320]{2,1,0:T(8,128)}), f32[32,24,320]{2,1,0:T(8,128)S(1)}, u32[]{:S(2)}, u32[]{:S(2)}) async-start(f32[32,24,320]{2,1,0:T(8,128)} %pad_maximum_fusion.1), calls=%async_computation | async-start | bytes 2359296 | tf_op jit(solution)/shard_map/all_to_all | solution.py:85
  52.9 18.4 %all-to-all-start.1 = ((f32[32,24,256]{2,1,0:T(8,128)}), f32[32,24,256]{2,1,0:T(8,128)S(1)}, u32[]{:S(2)}, u32[]{:S(2)}) async-start(f32[32,24,256]{2,1,0:T(8,128)} %broadcast_in_dim.10), calls=%async_computation.1 | async-start | bytes 1572864 | tf_op jit(solution)/shard_map/all_to_all | solution.py:90
  71.3 1.2 copy-start.1
  71.3 1.5 %copy-start.2 = (f32[64,4096]{1,0:T(8,128)S(1)}, f32[64,4096]{1,0:T(8,128)}, u32[]{:S(2)}) copy-start(f32[64,4096]{1,0:T(8,128)} %tile.25) | copy-start | bytes 3145732
  72.9 10.8 %copy-start.3 = (bf16[64,8192]{1,0:T(8,128)(2,1)S(1)}, bf16[64,8192]{1,0:T(8,128)(2,1)}, u32[]{:S(2)}) copy-start(bf16[64,8192]{1,0:T(8,128)(2,1)} %param.5) | copy-start | bytes 3145732
  96.1 16.2 %all-to-all-start.3 = ((f32[8,1,192]{2,1,0:T(1,128)}), f32[8,1,192]{2,1,0:T(1,128)S(1)}, u32[]{:S(2)}, u32[]{:S(2)}) async-start(f32[8,1,192]{2,1,0:T(1,128)} %reshape.168), calls=%async_computation.3 | async-start | bytes 16384 | tf_op jit(solution)/shard_map/all_to_all | solution.py:108
  113.3 31.6 %all-to-all-start.2 = ((bf16[8,6,8192]{2,1,0:T(8,128)(2,1)}), bf16[8,6,8192]{2,1,0:T(8,128)(2,1)S(1)}, u32[]{:S(2)}, u32[]{:S(2)}) async-start(bf16[8,6,8192]{2,1,0:T(8,128)(2,1)} %broadcast_in_dim.11), calls=%async_computation.2 | async-start | bytes 2097152 | tf_op jit(solution)/shard_map/all_to_all | solution.py:111

commit v3 on v2

--- a/solution.py
+++ b/solution.py
@@ -17,18 +17,17 @@
     return phase.astype(jnp.float32) * (2.0 * math.pi / total)
 
 
-def derotate(spec, rotation, ctf_rows, total):
-    count = spec.shape[0]
-    layered = spec.reshape(count, 2, CYCLES, MFREQ)
-    real_part = layered[:, 0]
-    imag_part = layered[:, 1]
+def derotate(real_part, imag_part, rotation, ctf_cols, total):
     angle = angles(rotation, total)
-    cosine = jnp.cos(angle)[:, None, :]
-    sine = jnp.sin(angle)[:, None, :]
-    turned = jnp.stack(
-        [real_part * cosine + imag_part * sine, imag_part * cosine - real_part * sine], axis=1
+    cosine = jnp.tile(jnp.cos(angle), (1, CYCLES))
+    sine = jnp.tile(jnp.sin(angle), (1, CYCLES))
+    return jnp.concatenate(
+        [
+            (real_part * cosine + imag_part * sine) * ctf_cols,
+            (imag_part * cosine - real_part * sine) * ctf_cols,
+        ],
+        axis=1,
     )
-    return (turned * ctf_rows[:, None, :, None]).reshape(count, K)
 
 
 def rotate_all(refs, total):
@@ -57,8 +56,10 @@
     count = particles.shape[0]
 
     ctf_rows = ctf_table[group]
+    ctf_cols = jnp.repeat(ctf_rows, MFREQ, axis=1)
     spec = particles.astype(jnp.float32)
-    weighted = derotate(spec, rot_index, ctf_rows, total)
+    half = K // 2
+    weighted = derotate(spec[:, :half], spec[:, half:], rot_index, ctf_cols, total)
     first_class = rot_rank * block
     member = (
         (first_class + jnp.arange(block, dtype=jnp.int32))[:, None] == assign[None, :]
@@ -95,11 +96,20 @@
     refs_f32 = plain / jnp.sqrt(spread + 1e-06)[:, None]
     refs_block = refs_f32.astype(jnp.bfloat16)
 
-    modulated = (
-        (spec.reshape(count, 2, CYCLES, MFREQ) * ctf_rows[:, None, :, None])
-        .reshape(count, K)
-        .astype(jnp.bfloat16)
+    others = rot_count - 1
+    pairs = []
+    for plane in range(rot_count):
+        for sender in range(owners_per_block * others):
+            owner = plane * owners_per_block + sender // others
+            target = (plane + 1 + sender % others) % rot_count
+            pairs.append((sender * rot_count + plane, owner * rot_count + target))
+    sent = lax.dynamic_slice_in_dim(
+        refs_block, jnp.minimum(dom_rank // others, owners_per_block - 1) * CLS_DEV, CLS_DEV, 0
     )
+    got = lax.ppermute(sent, ("dom", "rot"), pairs)
+    mine = lax.dynamic_slice_in_dim(refs_block, (dom_rank % owners_per_block) * CLS_DEV, CLS_DEV, 0)
+    refs = jnp.where((dom_rank // owners_per_block) == rot_rank, mine, got)
+    modulated = (spec * jnp.concatenate([ctf_cols, ctf_cols], axis=1)).astype(jnp.bfloat16)
     turned = rotate_all(refs_block.astype(jnp.float32), total)
     found = lax.dot_general(
         modulated, turned, (((1,), (1,)), ((), ())), preferred_element_type=jnp.float32
@@ -107,11 +117,6 @@
     best = jnp.max(found.reshape(count, total, block), axis=1) * (1.0 / math.sqrt(K))
     best_scores = lax.all_to_all(best, "rot", 0, 1, tiled=True)
 
-    mine = lax.dynamic_slice_in_dim(refs_block, (dom_rank % owners_per_block) * CLS_DEV, CLS_DEV, 0)
-    spread_out = lax.all_to_all(
-        jnp.broadcast_to(mine[None], (rot_count,) + mine.shape), "rot", 0, 0, tiled=True
-    )
-    refs = lax.dynamic_index_in_dim(spread_out, dom_rank // owners_per_block, 0, keepdims=False)
     return (refs, best_scores)
 
 

time: 148 us -> 109 us (0.74)
  waiting for transfers between devices: 55.3 us -> 34.6 us
  local copies, waits for them, and re-layouts: 30.7 us -> 12.4 us
    all_to_all x1 -> x0, waiting for transfers between devices: 26.1 us -> none  [local(): lax.all_to_all(jnp.broadcast_to(mine[None], (rot_count,) + mine.shape), '...]
    ppermute x0 -> x1, starting transfers between devices: none -> 7.55 us  [local(): got = lax.ppermute(sent, ('dom', 'rot'), pairs)]
    mul x2 -> x0, local copies, waits for them, and re-layouts: 6.08 us -> none  [derotate(): return (turned * ctf_rows[:, None, :, None]).reshape(count, K)]
    all_to_all x1, waiting for transfers between devices: 4.17 us -> 9.45 us  [local(): lax.all_to_all(jnp.broadcast_to(plain_chunk[None], (chunks, block, width)...]
    reshape x1 -> x2, local copies, waits for them, and re-layouts: 4.3 us -> 0.71 us  [the longest x1 0.65 us: local(): ctf_cols = jnp.repeat(ctf_rows, MFREQ, axis=1)]
    all_to_all x1 -> x0, starting transfers between devices: 3.56 us -> none  [local(): lax.all_to_all(jnp.broadcast_to(mine[None], (rot_count,) + mine.shape), '...]
    add x1 -> x0, other arithmetic: 2.87 us -> none  [derotate(): real_part * cosine + imag_part * sine]
    another operation x2, local copies, waits for them, and re-layouts: 4.41 us -> 1.74 us  [rotate_all(): sine = jnp.tile(jnp.sin(angle), (1, CYCLES))[:, None, :]]
  transfers between devices with their start and end apart: 4 -> 4, of which waited for: 4 -> 3; matrix products, arithmetic and copies ran while one was open for 7% -> 28% of each run, Pallas kernels for 0% -> 0%
where the time goes in v3:
time: 109 us; the launch traced here: 108 us
  waiting for transfers between devices  34.6 us (32%)
  starting transfers between devices  26.1 us (24%)
  other arithmetic  21 us (19%)
  matrix products  12.6 us (12%)
  local copies, waits for them, and re-layouts  12.4 us (11%)
    all_to_all x1, waiting for transfers between devices, local(): summed = jnp.sum(lax.all_to_all(payload, 'dom', 0, 0, tiled=True), axis=0)  17.4 us
    another operation x1, other arithmetic  12.9 us
    dot_general x1, matrix products, local(): lax.dot_general(modulated, turned, (((1,), (1,)), ((), ())), preferred_el...  11.6 us
    all_to_all x1, waiting for transfers between devices, local(): lax.all_to_all(jnp.broadcast_to(plain_chunk[None], (chunks, block, width)...  9.45 us
    all_to_all x1, waiting for transfers between devices, local(): best_scores = lax.all_to_all(best, 'rot', 0, 1, tiled=True)  7.73 us
    all_to_all x1, starting transfers between devices, local(): summed = jnp.sum(lax.all_to_all(payload, 'dom', 0, 0, tiled=True), axis=0)  7.62 us
    ppermute x1, starting transfers between devices, local(): got = lax.ppermute(sent, ('dom', 'rot'), pairs)  7.55 us
    all_to_all x1, starting transfers between devices, local(): best_scores = lax.all_to_all(best, 'rot', 0, 1, tiled=True)  5.83 us
  transfers between devices with their start and end apart: 4, of which 3 were waited for; matrix products, arithmetic and copies ran while one was open for 28% of the time, Pallas kernels for 0%

profile of v3, /device:TPU:2, one launch (start us, length us, event | category | flops | bytes accessed | tf_op | source)
XLA Modules:
  0.0 107.6 jit_solution(13197614941265002422)
XLA Ops:
  0.7 0.7 compare_select_fusion
  3.2 0.9 fusion.33
  4.3 1.6 %tile.45 = f32[64,4096]{1,0:T(8,128)} reshape(f32[64,64,64]{2,1,0:T(8,128)S(1)} %tile.44) | data formatting | bytes 2097152 | tf_op jit(solution)/shard_map/tile | solution.py:23
  6.0 1.7 %tile.43 = f32[64,4096]{1,0:T(8,128)} reshape(f32[64,64,64]{2,1,0:T(8,128)S(1)} %tile.42) | data formatting | bytes 2097152 | tf_op jit(solution)/shard_map/tile | solution.py:22
  7.7 1.4 %convert_element_type.41 = f32[64,8192]{1,0:T(8,128)S(1)} convert(bf16[64,8192]{1,0:T(8,128)(2,1)} %param.5) | non-fusion elementwise | flops 524288 | bytes 3145728 | tf_op jit(solution)/shard_map/convert_element_type | solution.py:60
  9.3 2.0 %add_multiply_fusion = (f32[64,4096]{1,0:T(8,128)S(1)}, f32[64,4096]{1,0:T(8,128)S(1)}) fusion(f32[64,4096]{1,0:T(8,128)S(1)} %reshape.156, f32[64,4096]{1,0:T(8,128)} %tile.45, f32[64,4096]{1,0:T(8,128)} %tile.43, f32[64,8192]{1,0:T(8,128)S(1)} %convert_element_type.41), kind=kLoop, calls=%fused_computation.17 | loop fusion | flops 2097152 | bytes 7340032 | tf_op jit(solution)/shard_map/mul | solution.py:26
  11.2 0.8 fusion.4
  12.2 1.1 %pad_maximum_fusion = f32[32,24,320]{2,1,0:T(8,128)} fusion(f32[32,24,64]{2,1,0:T(8,128)S(1)} %broadcast_in_dim.10, f32[32,24,256]{2,1,0:T(8,128)S(1)} %bitcast.21), kind=kLoop, calls=%fused_computation.13 | loop fusion | flops 245760 | bytes 1966080 | tf_op jit(solution)/shard_map/concatenate | solution.py:79
  13.3 7.6 %all-to-all-start = ((f32[32,24,320]{2,1,0:T(8,128)}), f32[32,24,320]{2,1,0:T(8,128)S(1)}, u32[]{:S(2)}, u32[]{:S(2)}) async-start(f32[32,24,320]{2,1,0:T(8,128)} %pad_maximum_fusion), calls=%async_computation | async-start | bytes 2359296 | tf_op jit(solution)/shard_map/all_to_all | solution.py:86
  20.9 17.4 %all-to-all-done = f32[32,24,320]{2,1,0:T(8,128)S(1)} async-done(((f32[32,24,320]{2,1,0:T(8,128)}), f32[32,24,320]{2,1,0:T(8,128)S(1)}, u32[]{:S(2)}, u32[]{:S(2)}) %all-to-all-start) | async-done | bytes 983072 | tf_op jit(solution)/shard_map/all_to_all | solution.py:86
  38.7 0.9 broadcast_in_dim.11
  39.6 5.1 %all-to-all-start.1 = ((f32[32,24,256]{2,1,0:T(8,128)}), f32[32,24,256]{2,1,0:T(8,128)S(1)}, u32[]{:S(2)}, u32[]{:S(2)}) async-start(f32[32,24,256]{2,1,0:T(8,128)} %broadcast_in_dim.11), calls=%async_computation.1 | async-start | bytes 1572864 | tf_op jit(solution)/shard_map/all_to_all | solution.py:91
  45.0 1.6 %tile.49 = f32[64,4096]{1,0:T(8,128)} reshape(f32[64,64,64]{2,1,0:T(8,128)S(1)} %tile.48) | data formatting | bytes 2097152 | tf_op jit(solution)/shard_map/tile | solution.py:40
  46.9 1.6 %tile.47 = f32[64,4096]{1,0:T(8,128)} reshape(f32[64,64,64]{2,1,0:T(8,128)S(1)} %tile.46) | data formatting | bytes 2097152 | tf_op jit(solution)/shard_map/tile | solution.py:39
  48.6 9.4 %all-to-all-done.1 = f32[32,24,256]{2,1,0:T(8,128)S(1)} async-done(((f32[32,24,256]{2,1,0:T(8,128)}), f32[32,24,256]{2,1,0:T(8,128)S(1)}, u32[]{:S(2)}, u32[]{:S(2)}) %all-to-all-start.1) | async-done | bytes 786464 | tf_op jit(solution)/shard_map/all_to_all | solution.py:91
  58.5 7.5 %collective-permute-start = (bf16[6,8192]{1,0:T(8,128)(2,1)S(1)}, bf16[6,8192]{1,0:T(8,128)(2,1)S(1)}, u32[]{:S(2)}, u32[]{:S(2)}) collective-permute-start(bf16[6,8192]{1,0:T(8,128)(2,1)S(1)} %constant_dynamic-slice_fusion), channel_id=1, source_target_pairs={{0,1},{8,2},{16,3},{24,4},{32,5},{40,6},{48,7},{56,9},{64,10},{72,... | collective-permute-start | bytes 294920 | tf_op jit(solution)/shard_map/ppermute | solution.py:109
  66.1 12.9 %subtract_convert_fusion = (bf16[64,24,4096]{2,0,1:T(8,128)(2,1)}, bf16[64,24,4096]{2,0,1:T(8,128)(2,1)}) fusion(f32[64,4096]{1,0:T(8,128)} %tile.49, f32[24,4096]{1,0:T(8,128)S(1)} %get-tuple-element.7, f32[64,4096]{1,0:T(8,128)} %tile.47, f32[24,4096]{1,0:T(8,128)S(1)} %get-tuple-element.6), kind=kLoop, calls=%fused_computation.6 | loop fusion | flops 50331648 | bytes 28049408 | tf_op jit(solution)/shard_map/convert
  79.0 11.6 %fusion.9 = f32[64,24]{0,1:T(8,128)S(1)} fusion(bf16[64,24,4096]{2,0,1:T(8,128)(2,1)} %get-tuple-element.5, bf16[64,24,4096]{2,0,1:T(8,128)(2,1)} %get-tuple-element.4, f32[64,4096]{1,0:T(8,128)S(1)} %copy-done.2, bf16[64,8192]{1,0:T(8,128)(2,1)S(1)} %copy-done.3), kind=kOutput, calls=%fused_computation.14 | convolution fusion | flops 1663138304 | bytes 27269120 | tf_op jit(solution)/shard_map/dot_general | solution.py:114
  90.7 0.7 reshape.169
  91.4 5.8 %all-to-all-start.2 = ((f32[8,1,192]{2,1,0:T(1,128)}), f32[8,1,192]{2,1,0:T(1,128)S(1)}, u32[]{:S(2)}, u32[]{:S(2)}) async-start(f32[8,1,192]{2,1,0:T(1,128)} %reshape.169), calls=%async_computation.2 | async-start | bytes 16384 | tf_op jit(solution)/shard_map/all_to_all | solution.py:118
  97.2 7.7 %all-to-all-done.2 = f32[8,1,192]{2,1,0:T(1,128)S(1)} async-done(((f32[8,1,192]{2,1,0:T(1,128)}), f32[8,1,192]{2,1,0:T(1,128)S(1)}, u32[]{:S(2)}, u32[]{:S(2)}) %all-to-all-start.2) | async-done | bytes 6176 | tf_op jit(solution)/shard_map/all_to_all | solution.py:118
  105.5 0.7 reduce.1
  106.2 0.7 all_to_all.22
  106.9 0.7 dynamic-slice_select_fusion
  (42 shorter events, 4.5 us)
Async XLA Ops:
  0.6 0.7 copy-start
  0.6 8.4 %copy-start.4 = (s32[64]{0:T(128)S(1)}, s32[64]{0:T(128)}, u32[]{:S(2)}) copy-start(s32[64]{0:T(128)} %param.6) | copy-start | bytes 772
  3.2 8.9 %copy-start.1 = (f32[64,4096]{1,0:T(8,128)}, f32[64,4096]{1,0:T(8,128)S(1)}, u32[]{:S(2)}) copy-start(f32[64,4096]{1,0:T(8,128)S(1)} %reshape.156) | copy-start | bytes 3145732
  13.3 25.0 %all-to-all-start = ((f32[32,24,320]{2,1,0:T(8,128)}), f32[32,24,320]{2,1,0:T(8,128)S(1)}, u32[]{:S(2)}, u32[]{:S(2)}) async-start(f32[32,24,320]{2,1,0:T(8,128)} %pad_maximum_fusion), calls=%async_computation | async-start | bytes 2359296 | tf_op jit(solution)/shard_map/all_to_all | solution.py:86
  39.6 18.4 %all-to-all-start.1 = ((f32[32,24,256]{2,1,0:T(8,128)}), f32[32,24,256]{2,1,0:T(8,128)S(1)}, u32[]{:S(2)}, u32[]{:S(2)}) async-start(f32[32,24,256]{2,1,0:T(8,128)} %broadcast_in_dim.11), calls=%async_computation.1 | async-start | bytes 1572864 | tf_op jit(solution)/shard_map/all_to_all | solution.py:91
  58.5 48.4 %collective-permute-start = (bf16[6,8192]{1,0:T(8,128)(2,1)S(1)}, bf16[6,8192]{1,0:T(8,128)(2,1)S(1)}, u32[]{:S(2)}, u32[]{:S(2)}) collective-permute-start(bf16[6,8192]{1,0:T(8,128)(2,1)S(1)} %constant_dynamic-slice_fusion), channel_id=1, source_target_pairs={{0,1},{8,2},{16,3},{24,4},{32,5},{40,6},{48,7},{56,9},{64,10},{72,... | collective-permute-start | bytes 294920 | tf_op jit(solution)/shard_map/ppermute | solution.py:109
  66.1 12.9 %copy-start.2 = (f32[64,4096]{1,0:T(8,128)S(1)}, f32[64,4096]{1,0:T(8,128)}, u32[]{:S(2)}) copy-start(f32[64,4096]{1,0:T(8,128)} %copy-done.1) | copy-start | bytes 3145732
  66.1 12.9 %copy-start.3 = (bf16[64,8192]{1,0:T(8,128)(2,1)S(1)}, bf16[64,8192]{1,0:T(8,128)(2,1)}, u32[]{:S(2)}) copy-start(bf16[64,8192]{1,0:T(8,128)(2,1)} %param.5) | copy-start | bytes 3145732
  91.4 13.6 %all-to-all-start.2 = ((f32[8,1,192]{2,1,0:T(1,128)}), f32[8,1,192]{2,1,0:T(1,128)S(1)}, u32[]{:S(2)}, u32[]{:S(2)}) async-start(f32[8,1,192]{2,1,0:T(1,128)} %reshape.169), calls=%async_computation.2 | async-start | bytes 16384 | tf_op jit(solution)/shard_map/all_to_all | solution.py:118

commit v4 on v3

--- a/solution.py
+++ b/solution.py
@@ -30,18 +30,18 @@
     )
 
 
-def rotate_all(refs, total):
+def rotate_all(refs, turns, total):
     count = refs.shape[0]
     half = K // 2
     real_part = refs[None, :, :half]
     imag_part = refs[None, :, half:]
-    angle = angles(jnp.arange(total, dtype=jnp.int32), total)
+    angle = angles(jnp.arange(turns, dtype=jnp.int32), total)
     cosine = jnp.tile(jnp.cos(angle), (1, CYCLES))[:, None, :]
     sine = jnp.tile(jnp.sin(angle), (1, CYCLES))[:, None, :]
     turned = jnp.concatenate(
         [real_part * cosine - imag_part * sine, real_part * sine + imag_part * cosine], axis=2
     )
-    return turned.reshape(total * count, K).astype(jnp.bfloat16)
+    return turned.reshape(turns * count, K).astype(jnp.bfloat16)
 
 
 def local(particles, assign, rot_index, group, ctf_table):
@@ -110,11 +110,22 @@
     mine = lax.dynamic_slice_in_dim(refs_block, (dom_rank % owners_per_block) * CLS_DEV, CLS_DEV, 0)
     refs = jnp.where((dom_rank // owners_per_block) == rot_rank, mine, got)
     modulated = (spec * jnp.concatenate([ctf_cols, ctf_cols], axis=1)).astype(jnp.bfloat16)
-    turned = rotate_all(refs_block.astype(jnp.float32), total)
+    quarter = total // 4
+    real_part = modulated[:, :half]
+    imag_part = modulated[:, half:]
+    freq = jnp.arange(half, dtype=jnp.int32) % MFREQ
+    variants = []
+    for u in range(4):
+        step = (freq * u) % 4
+        re_u = jnp.where(step == 0, real_part, jnp.where(step == 1, imag_part, jnp.where(step == 2, -real_part, -imag_part)))
+        im_u = jnp.where(step == 0, imag_part, jnp.where(step == 1, -real_part, jnp.where(step == 2, -imag_part, real_part)))
+        variants.append(jnp.concatenate([re_u, im_u], axis=1))
+    stacked = jnp.concatenate(variants, axis=0)
+    turned = rotate_all(refs_block.astype(jnp.float32), quarter, total)
     found = lax.dot_general(
-        modulated, turned, (((1,), (1,)), ((), ())), preferred_element_type=jnp.float32
+        stacked, turned, (((1,), (1,)), ((), ())), preferred_element_type=jnp.float32
     )
-    best = jnp.max(found.reshape(count, total, block), axis=1) * (1.0 / math.sqrt(K))
+    best = jnp.max(found.reshape(4, count, quarter, block), axis=(0, 2)) * (1.0 / math.sqrt(K))
     best_scores = lax.all_to_all(best, "rot", 0, 1, tiled=True)
 
     return (refs, best_scores)

time: 109 us -> 89.4 us (0.82)
  waiting for transfers between devices: 34.6 us -> 23.2 us
  matrix products: 12.6 us -> 4.49 us
  local copies, waits for them, and re-layouts: 12.4 us -> 9.31 us
  other arithmetic: 21 us -> 23.9 us
    another operation x1, other arithmetic: 12.9 us -> 2.04 us
    dot_general x1, matrix products: 11.6 us -> 3.47 us  [local(): lax.dot_general(stacked, turned, (((1,), (1,)), ((), ())), preferred_elem...]
    concatenate x0 -> x1, other arithmetic: none -> 8.11 us  [local(): stacked = jnp.concatenate(variants, axis=0)]
    all_to_all x1, waiting for transfers between devices: 17.4 us -> 10.3 us  [local(): summed = jnp.sum(lax.all_to_all(payload, 'dom', 0, 0, tiled=True), axis=0)]
    all_to_all x1, waiting for transfers between devices: 9.45 us -> 5.18 us  [local(): lax.all_to_all(jnp.broadcast_to(plain_chunk[None], (chunks, block, width)...]
    select_n x0 -> x2, other arithmetic: none -> 3.74 us  [local(): jnp.where(step == 0, real_part, jnp.where(step == 1, imag_part, jnp.where...]
    another operation x2, local copies, waits for them, and re-layouts: 1.77 us -> 0.22 us  [rotate_all(): cosine = jnp.tile(jnp.cos(angle), (1, CYCLES))[:, None, :]]
    another operation x2, local copies, waits for them, and re-layouts: 1.74 us -> 0.22 us  [rotate_all(): sine = jnp.tile(jnp.sin(angle), (1, CYCLES))[:, None, :]]
  transfers between devices with their start and end apart: 4 -> 4, of which waited for: 3 -> 3; matrix products, arithmetic and copies ran while one was open for 28% -> 26% of each run, Pallas kernels for 0% -> 0%
where the time goes in v4:
time: 89.4 us; the launch traced here: 88.4 us
  starting transfers between devices  26.5 us (30%)
  other arithmetic  23.9 us (27%)
  waiting for transfers between devices  23.2 us (26%)
  local copies, waits for them, and re-layouts  9.31 us (10%)
  matrix products  4.49 us (5%)
  between operations  0.96 us (1%)
    all_to_all x1, waiting for transfers between devices, local(): summed = jnp.sum(lax.all_to_all(payload, 'dom', 0, 0, tiled=True), axis=0)  10.3 us
    concatenate x1, other arithmetic, local(): stacked = jnp.concatenate(variants, axis=0)  8.11 us
    ppermute x1, starting transfers between devices, local(): got = lax.ppermute(sent, ('dom', 'rot'), pairs)  7.99 us
    all_to_all x1, waiting for transfers between devices, local(): best_scores = lax.all_to_all(best, 'rot', 0, 1, tiled=True)  7.73 us
    all_to_all x1, starting transfers between devices, local(): summed = jnp.sum(lax.all_to_all(payload, 'dom', 0, 0, tiled=True), axis=0)  7.62 us
    all_to_all x1, starting transfers between devices, local(): best_scores = lax.all_to_all(best, 'rot', 0, 1, tiled=True)  5.83 us
    all_to_all x1, waiting for transfers between devices, local(): lax.all_to_all(jnp.broadcast_to(plain_chunk[None], (chunks, block, width)...  5.18 us
    all_to_all x1, starting transfers between devices, local(): lax.all_to_all(jnp.broadcast_to(plain_chunk[None], (chunks, block, width)...  5.1 us
  transfers between devices with their start and end apart: 4, of which 3 were waited for; matrix products, arithmetic and copies ran while one was open for 26% of the time, Pallas kernels for 0%

profile of v4, /device:TPU:2, one launch (start us, length us, event | category | flops | bytes accessed | tf_op | source)
XLA Modules:
  0.0 88.4 jit_solution(10418232437951178340)
XLA Ops:
  3.6 1.6 %tile.45 = f32[64,4096]{1,0:T(8,128)} reshape(f32[64,64,64]{2,1,0:T(8,128)S(1)} %tile.44) | data formatting | bytes 2097152 | tf_op jit(solution)/shard_map/tile | solution.py:23
  5.3 1.7 %tile.43 = f32[64,4096]{1,0:T(8,128)} reshape(f32[64,64,64]{2,1,0:T(8,128)S(1)} %tile.42) | data formatting | bytes 2097152 | tf_op jit(solution)/shard_map/tile | solution.py:22
  7.0 1.4 %convert_element_type.41 = f32[64,8192]{1,0:T(8,128)S(1)} convert(bf16[64,8192]{1,0:T(8,128)(2,1)} %param.5) | non-fusion elementwise | flops 524288 | bytes 3145728 | tf_op jit(solution)/shard_map/convert_element_type | solution.py:60
  8.6 2.0 %add_multiply_fusion = (f32[64,4096]{1,0:T(8,128)S(1)}, f32[64,4096]{1,0:T(8,128)S(1)}) fusion(f32[64,4096]{1,0:T(8,128)S(1)} %reshape.157, f32[64,4096]{1,0:T(8,128)} %tile.45, f32[64,4096]{1,0:T(8,128)} %tile.43, f32[64,8192]{1,0:T(8,128)S(1)} %convert_element_type.41), kind=kLoop, calls=%fused_computation.17 | loop fusion | flops 2097152 | bytes 7340032 | tf_op jit(solution)/shard_map/mul | solution.py:26
  10.6 0.8 fusion.3
  11.5 1.1 %pad_maximum_fusion = f32[32,24,320]{2,1,0:T(8,128)} fusion(f32[32,24,64]{2,1,0:T(8,128)S(1)} %broadcast_in_dim.90, f32[32,24,256]{2,1,0:T(8,128)S(1)} %bitcast.30), kind=kLoop, calls=%fused_computation.15 | loop fusion | flops 245760 | bytes 1966080 | tf_op jit(solution)/shard_map/concatenate | solution.py:79
  12.6 7.6 %all-to-all-start = ((f32[32,24,320]{2,1,0:T(8,128)}), f32[32,24,320]{2,1,0:T(8,128)S(1)}, u32[]{:S(2)}, u32[]{:S(2)}) async-start(f32[32,24,320]{2,1,0:T(8,128)} %pad_maximum_fusion), calls=%async_computation | async-start | bytes 2359296 | tf_op jit(solution)/shard_map/all_to_all | solution.py:86
  21.5 1.4 %fusion.7 = bf16[64,8192]{1,0:T(8,128)(2,1)S(1)} fusion(f32[64,4096]{1,0:T(8,128)S(1)} %reshape.157, bf16[64,8192]{1,0:T(8,128)(2,1)} %param.5), kind=kLoop, calls=%fused_computation.13 | loop fusion | flops 2097152 | bytes 3145728 | tf_op jit(solution)/shard_map/convert_element_type | solution.py:112
  23.6 1.9 %select_select_fusion.1 = (bf16[64,4096]{1,0:T(8,128)(2,1)}, bf16[64,4096]{1,0:T(8,128)(2,1)}) fusion(pred[4096]{0:T(1024)(128)(4,1)} %get-tuple-element.18, pred[4096]{0:T(1024)(128)(4,1)} %get-tuple-element.19, pred[4096]{0:T(1024)(128)(4,1)} %broadcast_compare_fusion.8, bf16[64,8192]{1,0:T(8,128)(2,1)S(1)} %fusion.7), kind=kLoop, calls=%fused_computation.23 | loop fusion | flops 2097152 | bytes 2109440 | tf_op jit(solution)/shard_map/jit(_where)/select_n | solution.py:120
  25.5 1.8 %select_select_fusion.5 = (bf16[64,4096]{1,0:T(8,128)(2,1)}, bf16[64,4096]{1,0:T(8,128)(2,1)}, bf16[64,4096]{1,0:T(8,128)(2,1)}, bf16[64,4096]{1,0:T(8,128)(2,1)}) fusion(pred[4096]{0:T(1024)(128)(4,1)S(1)} %get-tuple-element.21, pred[4096]{0:T(1024)(128)(4,1)S(1)} %get-tuple-element.23, pred[4096]{0:T(1024)(128)(4,1)S(1)} %get-tuple-element.25, ...), kind=kLoop, calls=%fused_computation.27 | loop fusion | flops 3670016 | bytes 3170304 | tf_op jit(solution)/shard_map/jit(_where)/select_n | solution.py:120
  27.3 10.3 %all-to-all-done = f32[32,24,320]{2,1,0:T(8,128)S(1)} async-done(((f32[32,24,320]{2,1,0:T(8,128)}), f32[32,24,320]{2,1,0:T(8,128)S(1)}, u32[]{:S(2)}, u32[]{:S(2)}) %all-to-all-start) | async-done | bytes 983072 | tf_op jit(solution)/shard_map/all_to_all | solution.py:86
  38.0 0.9 %broadcast_in_dim.91 = f32[32,24,256]{2,1,0:T(8,128)} broadcast(f32[24,256]{1,0:T(8,128)S(1)} %slice_divide_fusion), dimensions={1,2} | broadcast | bytes 811008 | tf_op jit(solution)/shard_map/broadcast_in_dim | solution.py:92
  38.9 5.1 %all-to-all-start.1 = ((f32[32,24,256]{2,1,0:T(8,128)}), f32[32,24,256]{2,1,0:T(8,128)S(1)}, u32[]{:S(2)}, u32[]{:S(2)}) async-start(f32[32,24,256]{2,1,0:T(8,128)} %broadcast_in_dim.91), calls=%async_computation.1 | async-start | bytes 1572864 | tf_op jit(solution)/shard_map/all_to_all | solution.py:91
  44.0 8.1 %maximum_maximum_fusion = bf16[256,8192]{1,0:T(8,128)(2,1)} fusion(bf16[64,4096]{1,0:T(8,128)(2,1)} %get-tuple-element.11, bf16[64,4096]{1,0:T(8,128)(2,1)} %get-tuple-element.10, bf16[64,4096]{1,0:T(8,128)(2,1)} %get-tuple-element.12, bf16[64,4096]{1,0:T(8,128)(2,1)} %get-tuple-element.13, bf16[64,4096]{1,0:T(8,128)(2,1)} %get-tuple-element.7, ...), kind=kLoop, calls=%fused_computation.7 | loop fusion | flops 29360128 | bytes 8388608 | tf_op jit(solution)/shard_map/concatenate | solution.py:123
  52.2 5.2 %all-to-all-done.1 = f32[32,24,256]{2,1,0:T(8,128)S(1)} async-done(((f32[32,24,256]{2,1,0:T(8,128)}), f32[32,24,256]{2,1,0:T(8,128)S(1)}, u32[]{:S(2)}, u32[]{:S(2)}) %all-to-all-start.1) | async-done | bytes 786464 | tf_op jit(solution)/shard_map/all_to_all | solution.py:91
  57.9 8.0 %collective-permute-start = (bf16[6,8192]{1,0:T(8,128)(2,1)S(1)}, bf16[6,8192]{1,0:T(8,128)(2,1)S(1)}, u32[]{:S(2)}, u32[]{:S(2)}) collective-permute-start(bf16[6,8192]{1,0:T(8,128)(2,1)S(1)} %constant_dynamic-slice_fusion), channel_id=1, source_target_pairs={{0,1},{8,2},{16,3},{24,4},{32,5},{40,6},{48,7},{56,9},{64,10},{72,... | collective-permute-start | bytes 294920 | tf_op jit(solution)/shard_map/ppermute | solution.py:109
  65.9 2.0 %subtract_convert_fusion = (bf16[16,24,4096]{2,1,0:T(8,128)(2,1)S(1)}, bf16[16,24,4096]{2,1,0:T(8,128)(2,1)S(1)}) fusion(f32[16,4096]{1,0:T(8,128)S(1)} %tile.49, f32[24,4096]{1,0:T(8,128)S(1)} %get-tuple-element.15, f32[16,4096]{1,0:T(8,128)S(1)} %tile.47, f32[24,4096]{1,0:T(8,128)S(1)} %get-tuple-element.14), kind=kLoop, calls=%fused_computation.6 | loop fusion | flops 12582912 | bytes 7602176 | tf_op jit(solution)/shard_map/convert
  67.9 3.5 %fusion.8 = f32[64,24]{0,1:T(8,128)S(1)} fusion(bf16[4,64,8192,1]{2,1,3,0:T(8,128)(2,1)S(1)} %bitcast.27, bf16[16,24,4096]{2,1,0:T(8,128)(2,1)S(1)} %get-tuple-element.5, bf16[16,24,4096]{2,1,0:T(8,128)(2,1)S(1)} %get-tuple-element.4), kind=kOutput, calls=%fused_computation.14 | convolution fusion | flops 1623292416 | bytes 10491904 | tf_op jit(solution)/shard_map/dot_general | solution.py:125
  71.5 0.7 reshape.171
  72.2 5.8 %all-to-all-start.2 = ((f32[8,1,192]{2,1,0:T(1,128)}), f32[8,1,192]{2,1,0:T(1,128)S(1)}, u32[]{:S(2)}, u32[]{:S(2)}) async-start(f32[8,1,192]{2,1,0:T(1,128)} %reshape.171), calls=%async_computation.2 | async-start | bytes 16384 | tf_op jit(solution)/shard_map/all_to_all | solution.py:129
  78.0 7.7 %all-to-all-done.2 = f32[8,1,192]{2,1,0:T(1,128)S(1)} async-done(((f32[8,1,192]{2,1,0:T(1,128)}), f32[8,1,192]{2,1,0:T(1,128)S(1)}, u32[]{:S(2)}, u32[]{:S(2)}) %all-to-all-start.2) | async-done | bytes 6176 | tf_op jit(solution)/shard_map/all_to_all | solution.py:129
  86.3 0.7 reduce.1
  87.0 0.7 all_to_all.22
  87.7 0.7 dynamic-slice_select_fusion
  (49 shorter events, 6.7 us)
Async XLA Ops:
  0.6 0.7 copy-start
  0.6 2.6 %copy-start.2 = (s32[64]{0:T(128)S(1)}, s32[64]{0:T(128)}, u32[]{:S(2)}) copy-start(s32[64]{0:T(128)} %param.7) | copy-start | bytes 772
  5.2 3.2 %copy-start.3 = (s32[64]{0:T(128)S(1)}, s32[64]{0:T(128)}, u32[]{:S(2)}) copy-start(s32[64]{0:T(128)} %param.6) | copy-start | bytes 772
  12.6 25.0 %all-to-all-start = ((f32[32,24,320]{2,1,0:T(8,128)}), f32[32,24,320]{2,1,0:T(8,128)S(1)}, u32[]{:S(2)}, u32[]{:S(2)}) async-start(f32[32,24,320]{2,1,0:T(8,128)} %pad_maximum_fusion), calls=%async_computation | async-start | bytes 2359296 | tf_op jit(solution)/shard_map/all_to_all | solution.py:86
  38.9 18.4 %all-to-all-start.1 = ((f32[32,24,256]{2,1,0:T(8,128)}), f32[32,24,256]{2,1,0:T(8,128)S(1)}, u32[]{:S(2)}, u32[]{:S(2)}) async-start(f32[32,24,256]{2,1,0:T(8,128)} %broadcast_in_dim.91), calls=%async_computation.1 | async-start | bytes 1572864 | tf_op jit(solution)/shard_map/all_to_all | solution.py:91
  57.8 10.1 %copy-start.1 = (bf16[256,8192]{1,0:T(8,128)(2,1)S(1)}, bf16[256,8192]{1,0:T(8,128)(2,1)}, u32[]{:S(2)}) copy-start(bf16[256,8192]{1,0:T(8,128)(2,1)} %maximum_maximum_fusion) | copy-start | bytes 12582916
  57.9 29.8 %collective-permute-start = (bf16[6,8192]{1,0:T(8,128)(2,1)S(1)}, bf16[6,8192]{1,0:T(8,128)(2,1)S(1)}, u32[]{:S(2)}, u32[]{:S(2)}) collective-permute-start(bf16[6,8192]{1,0:T(8,128)(2,1)S(1)} %constant_dynamic-slice_fusion), channel_id=1, source_target_pairs={{0,1},{8,2},{16,3},{24,4},{32,5},{40,6},{48,7},{56,9},{64,10},{72,... | collective-permute-start | bytes 294920 | tf_op jit(solution)/shard_map/ppermute | solution.py:109
  72.2 13.6 %all-to-all-start.2 = ((f32[8,1,192]{2,1,0:T(1,128)}), f32[8,1,192]{2,1,0:T(1,128)S(1)}, u32[]{:S(2)}, u32[]{:S(2)}) async-start(f32[8,1,192]{2,1,0:T(1,128)} %reshape.171), calls=%async_computation.2 | async-start | bytes 16384 | tf_op jit(solution)/shard_map/all_to_all | solution.py:129

commit v5 on v4

--- a/solution.py
+++ b/solution.py
@@ -11,16 +11,16 @@
 K = 8192
 
 
-def angles(index, total):
-    freqs = jnp.arange(MFREQ, dtype=jnp.int32)
-    phase = freqs[None, :] * index[:, None] % total
+def column_angles(index, total, width):
+    freqs = lax.broadcasted_iota(jnp.int32, (index.shape[0], width), 1) % MFREQ
+    phase = freqs * index[:, None] % total
     return phase.astype(jnp.float32) * (2.0 * math.pi / total)
 
 
 def derotate(real_part, imag_part, rotation, ctf_cols, total):
-    angle = angles(rotation, total)
-    cosine = jnp.tile(jnp.cos(angle), (1, CYCLES))
-    sine = jnp.tile(jnp.sin(angle), (1, CYCLES))
+    angle = column_angles(rotation, total, real_part.shape[1])
+    cosine = jnp.cos(angle)
+    sine = jnp.sin(angle)
     return jnp.concatenate(
         [
             (real_part * cosine + imag_part * sine) * ctf_cols,
@@ -35,9 +35,9 @@
     half = K // 2
     real_part = refs[None, :, :half]
     imag_part = refs[None, :, half:]
-    angle = angles(jnp.arange(turns, dtype=jnp.int32), total)
-    cosine = jnp.tile(jnp.cos(angle), (1, CYCLES))[:, None, :]
-    sine = jnp.tile(jnp.sin(angle), (1, CYCLES))[:, None, :]
+    angle = column_angles(jnp.arange(turns, dtype=jnp.int32), total, half)
+    cosine = jnp.cos(angle)[:, None, :]
+    sine = jnp.sin(angle)[:, None, :]
     turned = jnp.concatenate(
         [real_part * cosine - imag_part * sine, real_part * sine + imag_part * cosine], axis=2
     )

time: 89.4 us -> 89.6 us (level)
  other arithmetic: 23.9 us -> 29.5 us
  local copies, waits for them, and re-layouts: 9.31 us -> 5.29 us
  waiting for transfers between devices: 23.2 us -> 20.3 us
  starting transfers between devices: 26.5 us -> 28.2 us
    all_to_all x1, waiting for transfers between devices: 10.3 us -> 0.46 us  [local(): summed = jnp.sum(lax.all_to_all(payload, 'dom', 0, 0, tiled=True), axis=0)]
    all_to_all x1, waiting for transfers between devices: 5.18 us -> 12.1 us  [local(): lax.all_to_all(jnp.broadcast_to(plain_chunk[None], (chunks, block, width)...]
    concatenate x1, other arithmetic: 8.11 us -> 14.6 us  [local(): stacked = jnp.concatenate(variants, axis=0)]
    another operation x8 -> x0, local copies, waits for them, and re-layouts: 4.01 us -> none  [the longest x2 1.81 us: derotate(): cosine = jnp.tile(jnp.cos(angle), (1, CYCLES))]
    select_n x2, other arithmetic: 3.74 us -> 0.76 us  [local(): jnp.where(step == 0, real_part, jnp.where(step == 1, imag_part, jnp.where...]
    mul x1, other arithmetic: 1.97 us -> 4.56 us  [derotate(): (real_part * cosine + imag_part * sine) * ctf_cols]
    all_to_all x1, starting transfers between devices: 5.1 us -> 6.93 us  [local(): lax.all_to_all(jnp.broadcast_to(plain_chunk[None], (chunks, block, width)...]
  transfers between devices with their start and end apart: 4 -> 4, of which waited for: 3 -> 3; matrix products, arithmetic and copies ran while one was open for 26% -> 29% of each run, Pallas kernels for 0% -> 0%
where the time goes in v5:
time: 89.6 us; the launch traced here: 88.8 us
  other arithmetic  29.5 us (33%)
  starting transfers between devices  28.2 us (31%)
  waiting for transfers between devices  20.3 us (23%)
  local copies, waits for them, and re-layouts  5.29 us (6%)
  matrix products  4.49 us (5%)
  between operations  0.98 us (1%)
    concatenate x1, other arithmetic, local(): stacked = jnp.concatenate(variants, axis=0)  14.6 us
    all_to_all x1, waiting for transfers between devices, local(): lax.all_to_all(jnp.broadcast_to(plain_chunk[None], (chunks, block, width)...  12.1 us
    ppermute x1, starting transfers between devices, local(): got = lax.ppermute(sent, ('dom', 'rot'), pairs)  7.81 us
    all_to_all x1, waiting for transfers between devices, local(): best_scores = lax.all_to_all(best, 'rot', 0, 1, tiled=True)  7.73 us
    all_to_all x1, starting transfers between devices, local(): summed = jnp.sum(lax.all_to_all(payload, 'dom', 0, 0, tiled=True), axis=0)  7.62 us
    all_to_all x1, starting transfers between devices, local(): lax.all_to_all(jnp.broadcast_to(plain_chunk[None], (chunks, block, width)...  6.93 us
    all_to_all x1, starting transfers between devices, local(): best_scores = lax.all_to_all(best, 'rot', 0, 1, tiled=True)  5.86 us
    mul x1, other arithmetic, derotate(): (real_part * cosine + imag_part * sine) * ctf_cols  4.56 us
  transfers between devices with their start and end apart: 4, of which 3 were waited for; matrix products, arithmetic and copies ran while one was open for 29% of the time, Pallas kernels for 0%

profile of v5, /device:TPU:2, one launch (start us, length us, event | category | flops | bytes accessed | tf_op | source)
XLA Modules:
  0.0 88.8 jit_solution(14450706316465829143)
XLA Ops:
  0.7 0.7 compare_select_fusion
  1.4 0.6 gather_fusion
  2.0 0.6 broadcast_in_dim.89
  2.6 0.7 reshape.147
  3.2 1.4 %convert_element_type.34 = f32[64,8192]{1,0:T(8,128)S(1)} convert(bf16[64,8192]{1,0:T(8,128)(2,1)} %param.5) | non-fusion elementwise | flops 524288 | bytes 3145728 | tf_op jit(solution)/shard_map/convert_element_type | solution.py:60
  4.8 4.6 %add_multiply_fusion = (f32[64,4096]{1,0:T(8,128)S(1)}, f32[64,4096]{1,0:T(8,128)S(1)}) fusion(f32[64,4096]{1,0:T(8,128)S(1)} %reshape.147, f32[64,8192]{1,0:T(8,128)S(1)} %convert_element_type.34, s32[64]{0:T(128)S(1)} %copy-done.2, s32[4096]{0:T(1024)S(1)} %get-tuple-element.18, s32[4096]{0:T(1024)S(1)} %get-tuple-element.19, pred[4096]{0:T(1024)(128)(4,1)S(1)} %fusion.29), kind=kLoop, calls=%fused_computation.23 | loop fusion | flops 6029312 | bytes 5280000 | tf_op jit(solution)/shard_map/mul | solution.py:26
  9.4 0.8 fusion.3
  10.3 1.1 %pad_maximum_fusion = f32[32,24,320]{2,1,0:T(8,128)} fusion(f32[32,24,64]{2,1,0:T(8,128)S(1)} %broadcast_in_dim.90, f32[32,24,256]{2,1,0:T(8,128)S(1)} %bitcast.30), kind=kLoop, calls=%fused_computation.18 | loop fusion | flops 245760 | bytes 1966080 | tf_op jit(solution)/shard_map/concatenate | solution.py:79
  11.4 7.6 %all-to-all-start = ((f32[32,24,320]{2,1,0:T(8,128)}), f32[32,24,320]{2,1,0:T(8,128)S(1)}, u32[]{:S(2)}, u32[]{:S(2)}) async-start(f32[32,24,320]{2,1,0:T(8,128)} %pad_maximum_fusion), calls=%async_computation | async-start | bytes 2359296 | tf_op jit(solution)/shard_map/all_to_all | solution.py:86
  19.1 1.4 %fusion.7 = bf16[64,8192]{1,0:T(8,128)(2,1)S(1)} fusion(f32[64,4096]{1,0:T(8,128)S(1)} %reshape.147, bf16[64,8192]{1,0:T(8,128)(2,1)} %param.5), kind=kLoop, calls=%fused_computation.13 | loop fusion | flops 2097152 | bytes 3145728 | tf_op jit(solution)/shard_map/convert_element_type | solution.py:112
  21.4 14.6 %maximum_maximum_fusion = bf16[256,8192]{1,0:T(8,128)(2,1)} fusion(bf16[64,4096]{1,0:T(8,128)(2,1)S(1)} %get-tuple-element.11, bf16[64,4096]{1,0:T(8,128)(2,1)S(1)} %get-tuple-element.10, bf16[64,4096]{1,0:T(8,128)(2,1)S(1)} %get-tuple-element.12, bf16[64,4096]{1,0:T(8,128)(2,1)S(1)} %get-tuple-element.13, bf16[64,4096]{1,0:T(8,128)(2,1)S(1)} %get-tuple-element.7, ...), kind=kLoop, calls=%fused_computation.7 | loop fusion | flops 29360128 | bytes 8388608 | tf_op jit(solution)/shard_map/concatenate | solution.py:123
  36.8 0.9 %broadcast_in_dim.91 = f32[32,24,256]{2,1,0:T(8,128)} broadcast(f32[24,256]{1,0:T(8,128)S(1)} %slice_divide_fusion), dimensions={1,2} | broadcast | bytes 811008 | tf_op jit(solution)/shard_map/broadcast_in_dim | solution.py:92
  37.8 6.9 %all-to-all-start.1 = ((f32[32,24,256]{2,1,0:T(8,128)}), f32[32,24,256]{2,1,0:T(8,128)S(1)}, u32[]{:S(2)}, u32[]{:S(2)}) async-start(f32[32,24,256]{2,1,0:T(8,128)} %broadcast_in_dim.91), calls=%async_computation.1 | async-start | bytes 1572864 | tf_op jit(solution)/shard_map/all_to_all | solution.py:91
  44.7 1.0 %fusion.19 = (f32[16,4096]{1,0:T(8,128)S(1)}, f32[16,4096]{1,0:T(8,128)S(1)}) fusion(s32[4096]{0:T(1024)S(1)} %get-tuple-element.18, s32[4096]{0:T(1024)S(1)} %get-tuple-element.19, pred[4096]{0:T(1024)(128)(4,1)S(1)} %fusion.29), kind=kLoop, calls=%fused_computation.43 | loop fusion | flops 983040 | bytes 561152 | tf_op jit(solution)/shard_map/cos | solution.py:39
  45.7 12.1 %all-to-all-done.1 = f32[32,24,256]{2,1,0:T(8,128)S(1)} async-done(((f32[32,24,256]{2,1,0:T(8,128)}), f32[32,24,256]{2,1,0:T(8,128)S(1)}, u32[]{:S(2)}, u32[]{:S(2)}) %all-to-all-start.1) | async-done | bytes 786464 | tf_op jit(solution)/shard_map/all_to_all | solution.py:91
  58.4 7.8 %collective-permute-start = (bf16[6,8192]{1,0:T(8,128)(2,1)S(1)}, bf16[6,8192]{1,0:T(8,128)(2,1)S(1)}, u32[]{:S(2)}, u32[]{:S(2)}) collective-permute-start(bf16[6,8192]{1,0:T(8,128)(2,1)S(1)} %constant_dynamic-slice_fusion), channel_id=1, source_target_pairs={{0,1},{8,2},{16,3},{24,4},{32,5},{40,6},{48,7},{56,9},{64,10},{72,... | collective-permute-start | bytes 294920 | tf_op jit(solution)/shard_map/ppermute | solution.py:109
  66.2 2.0 %subtract_convert_fusion = (bf16[16,24,4096]{2,1,0:T(8,128)(2,1)S(1)}, bf16[16,24,4096]{2,1,0:T(8,128)(2,1)S(1)}) fusion(f32[16,4096]{1,0:T(8,128)S(1)} %get-tuple-element.17, f32[24,4096]{1,0:T(8,128)S(1)} %get-tuple-element.15, f32[16,4096]{1,0:T(8,128)S(1)} %get-tuple-element.16, f32[24,4096]{1,0:T(8,128)S(1)} %get-tuple-element.14), kind=kLoop, calls=%fused_computation.6 | loop fusion | flops 12582912 | bytes 7602176 | tf_op jit(solution)/shard_map/convert
  68.3 3.5 %fusion.8 = f32[64,24]{0,1:T(8,128)S(1)} fusion(bf16[4,64,8192,1]{2,1,3,0:T(8,128)(2,1)S(1)} %bitcast.27, bf16[16,24,4096]{2,1,0:T(8,128)(2,1)S(1)} %get-tuple-element.5, bf16[16,24,4096]{2,1,0:T(8,128)(2,1)S(1)} %get-tuple-element.4), kind=kOutput, calls=%fused_computation.17 | convolution fusion | flops 1623292416 | bytes 10491904 | tf_op jit(solution)/shard_map/dot_general | solution.py:125
  71.8 0.7 reshape.161
  72.5 5.9 %all-to-all-start.2 = ((f32[8,1,192]{2,1,0:T(1,128)}), f32[8,1,192]{2,1,0:T(1,128)S(1)}, u32[]{:S(2)}, u32[]{:S(2)}) async-start(f32[8,1,192]{2,1,0:T(1,128)} %reshape.161), calls=%async_computation.2 | async-start | bytes 16384 | tf_op jit(solution)/shard_map/all_to_all | solution.py:129
  78.4 7.7 %all-to-all-done.2 = f32[8,1,192]{2,1,0:T(1,128)S(1)} async-done(((f32[8,1,192]{2,1,0:T(1,128)}), f32[8,1,192]{2,1,0:T(1,128)S(1)}, u32[]{:S(2)}, u32[]{:S(2)}) %all-to-all-start.2) | async-done | bytes 6176 | tf_op jit(solution)/shard_map/all_to_all | solution.py:129
  86.6 0.7 reduce.1
  87.4 0.7 all_to_all.22
  88.1 0.7 dynamic-slice_select_fusion
  (41 shorter events, 3.2 us)
Async XLA Ops:
  0.6 0.7 copy-start
  2.0 2.7 %copy-start.3 = (s32[64]{0:T(128)S(1)}, s32[64]{0:T(128)}, u32[]{:S(2)}) copy-start(s32[64]{0:T(128)} %param.6) | copy-start | bytes 772
  2.0 2.9 %copy-start.2 = (s32[64]{0:T(128)S(1)}, s32[64]{0:T(128)}, u32[]{:S(2)}) copy-start(s32[64]{0:T(128)} %param.7) | copy-start | bytes 772
  11.4 25.0 %all-to-all-start = ((f32[32,24,320]{2,1,0:T(8,128)}), f32[32,24,320]{2,1,0:T(8,128)S(1)}, u32[]{:S(2)}, u32[]{:S(2)}) async-start(f32[32,24,320]{2,1,0:T(8,128)} %pad_maximum_fusion), calls=%async_computation | async-start | bytes 2359296 | tf_op jit(solution)/shard_map/all_to_all | solution.py:86
  37.8 20.1 %all-to-all-start.1 = ((f32[32,24,256]{2,1,0:T(8,128)}), f32[32,24,256]{2,1,0:T(8,128)S(1)}, u32[]{:S(2)}, u32[]{:S(2)}) async-start(f32[32,24,256]{2,1,0:T(8,128)} %broadcast_in_dim.91), calls=%async_computation.1 | async-start | bytes 1572864 | tf_op jit(solution)/shard_map/all_to_all | solution.py:91
  58.3 9.9 %copy-start.1 = (bf16[256,8192]{1,0:T(8,128)(2,1)S(1)}, bf16[256,8192]{1,0:T(8,128)(2,1)}, u32[]{:S(2)}) copy-start(bf16[256,8192]{1,0:T(8,128)(2,1)} %maximum_maximum_fusion) | copy-start | bytes 12582916
  58.4 29.7 %collective-permute-start = (bf16[6,8192]{1,0:T(8,128)(2,1)S(1)}, bf16[6,8192]{1,0:T(8,128)(2,1)S(1)}, u32[]{:S(2)}, u32[]{:S(2)}) collective-permute-start(bf16[6,8192]{1,0:T(8,128)(2,1)S(1)} %constant_dynamic-slice_fusion), channel_id=1, source_target_pairs={{0,1},{8,2},{16,3},{24,4},{32,5},{40,6},{48,7},{56,9},{64,10},{72,... | collective-permute-start | bytes 294920 | tf_op jit(solution)/shard_map/ppermute | solution.py:109
  72.5 13.6 %all-to-all-start.2 = ((f32[8,1,192]{2,1,0:T(1,128)}), f32[8,1,192]{2,1,0:T(1,128)S(1)}, u32[]{:S(2)}, u32[]{:S(2)}) async-start(f32[8,1,192]{2,1,0:T(1,128)} %reshape.161), calls=%async_computation.2 | async-start | bytes 16384 | tf_op jit(solution)/shard_map/all_to_all | solution.py:129

commit v6 on v5

--- a/solution.py
+++ b/solution.py
@@ -3,6 +3,7 @@
 import jax
 import jax.numpy as jnp
 from jax import lax
+from jax.experimental import pallas as pl
 from jax.sharding import PartitionSpec as P
 
 CYCLES = 64
@@ -17,17 +18,34 @@
     return phase.astype(jnp.float32) * (2.0 * math.pi / total)
 
 
-def derotate(real_part, imag_part, rotation, ctf_cols, total):
-    angle = column_angles(rotation, total, real_part.shape[1])
-    cosine = jnp.cos(angle)
-    sine = jnp.sin(angle)
-    return jnp.concatenate(
-        [
-            (real_part * cosine + imag_part * sine) * ctf_cols,
-            (imag_part * cosine - real_part * sine) * ctf_cols,
-        ],
-        axis=1,
-    )
+def prologue_kernel(x_ref, cos_ref, sin_ref, ctf_ref, w_ref, mod_ref):
+    half = x_ref.shape[1] // 2
+    lanes = cos_ref.shape[1]
+    cosine = cos_ref[...]
+    sine = sin_ref[...]
+    low = lax.broadcasted_iota(jnp.int32, cosine.shape, 1) < MFREQ
+    for j in range(half // lanes):
+        gain = jnp.where(low, ctf_ref[:, 2 * j : 2 * j + 1], ctf_ref[:, 2 * j + 1 : 2 * j + 2])
+        re_cols = pl.ds(j * lanes, lanes)
+        im_cols = pl.ds(half + j * lanes, lanes)
+        real_part = x_ref[:, re_cols].astype(jnp.float32)
+        imag_part = x_ref[:, im_cols].astype(jnp.float32)
+        w_ref[:, re_cols] = (real_part * cosine + imag_part * sine) * gain
+        w_ref[:, im_cols] = (imag_part * cosine - real_part * sine) * gain
+        mod_ref[:, re_cols] = (real_part * gain).astype(jnp.bfloat16)
+        mod_ref[:, im_cols] = (imag_part * gain).astype(jnp.bfloat16)
+
+
+def derotate_and_modulate(particles, rotation, ctf_rows, total):
+    angle = column_angles(rotation, total, 2 * MFREQ)
+    count = particles.shape[0]
+    return pl.pallas_call(
+        prologue_kernel,
+        out_shape=(
+            jax.ShapeDtypeStruct((count, K), jnp.float32),
+            jax.ShapeDtypeStruct((count, K), jnp.bfloat16),
+        ),
+    )(particles, jnp.cos(angle), jnp.sin(angle), ctf_rows)
 
 
 def rotate_all(refs, turns, total):
@@ -56,10 +74,8 @@
     count = particles.shape[0]
 
     ctf_rows = ctf_table[group]
-    ctf_cols = jnp.repeat(ctf_rows, MFREQ, axis=1)
-    spec = particles.astype(jnp.float32)
     half = K // 2
-    weighted = derotate(spec[:, :half], spec[:, half:], rot_index, ctf_cols, total)
+    weighted, modulated = derotate_and_modulate(particles, rot_index, ctf_rows, total)
     first_class = rot_rank * block
     member = (
         (first_class + jnp.arange(block, dtype=jnp.int32))[:, None] == assign[None, :]
@@ -109,7 +125,6 @@
     got = lax.ppermute(sent, ("dom", "rot"), pairs)
     mine = lax.dynamic_slice_in_dim(refs_block, (dom_rank % owners_per_block) * CLS_DEV, CLS_DEV, 0)
     refs = jnp.where((dom_rank // owners_per_block) == rot_rank, mine, got)
-    modulated = (spec * jnp.concatenate([ctf_cols, ctf_cols], axis=1)).astype(jnp.bfloat16)
     quarter = total // 4
     real_part = modulated[:, :half]
     imag_part = modulated[:, half:]

time: 89.6 us -> 88.6 us (0.989)
  other arithmetic: 29.5 us -> 23.7 us
  Pallas kernels: 0 us -> 3.6 us
  matrix products: 4.49 us -> 6.82 us
  waiting for transfers between devices: 20.3 us -> 21.7 us
  local copies, waits for them, and re-layouts: 5.29 us -> 4.05 us
  starting transfers between devices: 28.2 us -> 27 us
    mul x1 -> x0, other arithmetic: 4.56 us -> none  [derotate(): (real_part * cosine + imag_part * sine) * ctf_cols]
    pallas_call x0 -> x1, Pallas kernels: none -> 3.6 us  [derotate_and_modulate(): pl.pallas_call(prologue_kernel, out_shape=(jax.ShapeDtypeStruct((count, K...]
    convert_element_type x2 -> x0, other arithmetic: 2.76 us -> none  [the longest x1 1.4 us: local(): (spec * jnp.concatenate([ctf_cols, ctf_cols], axis=1)).astype(jnp.bfloat16)]
    dot_general x1, matrix products: 0.83 us -> 2.49 us  [local(): jnp.dot(member, weighted, precision=lax.Precision.HIGHEST, preferred_elem...]
    sin x0 -> x1, other arithmetic: none -> 1.49 us  [derotate_and_modulate(): jnp.sin(angle)]
    all_to_all x1, starting transfers between devices: 6.93 us -> 5.54 us  [local(): lax.all_to_all(jnp.broadcast_to(plain_chunk[None], (chunks, block, width)...]
    all_to_all x1, waiting for transfers between devices: 0.46 us -> 1.85 us  [local(): summed = jnp.sum(lax.all_to_all(payload, 'dom', 0, 0, tiled=True), axis=0)]
  transfers between devices with their start and end apart: 4 -> 4, of which waited for: 3 -> 3; matrix products, arithmetic and copies ran while one was open for 29% -> 27% of each run, Pallas kernels for 0% -> 0%
where the time goes in v6:
time: 88.6 us; the launch traced here: 87.8 us
  starting transfers between devices  27 us (30%)
  other arithmetic  23.7 us (27%)
  waiting for transfers between devices  21.7 us (24%)
  matrix products  6.82 us (8%)
  local copies, waits for them, and re-layouts  4.05 us (5%)
  Pallas kernels  3.6 us (4%)
  between operations  0.95 us (1%)
    concatenate x1, other arithmetic, local(): stacked = jnp.concatenate(variants, axis=0)  14.6 us
    all_to_all x1, waiting for transfers between devices, local(): lax.all_to_all(jnp.broadcast_to(plain_chunk[None], (chunks, block, width)...  12.1 us
    ppermute x1, starting transfers between devices, local(): got = lax.ppermute(sent, ('dom', 'rot'), pairs)  7.99 us
    all_to_all x1, waiting for transfers between devices, local(): best_scores = lax.all_to_all(best, 'rot', 0, 1, tiled=True)  7.73 us
    all_to_all x1, starting transfers between devices, local(): summed = jnp.sum(lax.all_to_all(payload, 'dom', 0, 0, tiled=True), axis=0)  7.62 us
    all_to_all x1, starting transfers between devices, local(): best_scores = lax.all_to_all(best, 'rot', 0, 1, tiled=True)  5.85 us
    all_to_all x1, starting transfers between devices, local(): lax.all_to_all(jnp.broadcast_to(plain_chunk[None], (chunks, block, width)...  5.54 us
    pallas_call x1, Pallas kernels, derotate_and_modulate(): pl.pallas_call(prologue_kernel, out_shape=(jax.ShapeDtypeStruct((count, K...  3.6 us
  transfers between devices with their start and end apart: 4, of which 3 were waited for; matrix products, arithmetic and copies ran while one was open for 27% of the time, Pallas kernels for 0%

profile of v6, /device:TPU:2, one launch (start us, length us, event | category | flops | bytes accessed | tf_op | source)
XLA Modules:
  0.0 87.8 jit_solution(3930750204219153625)
XLA Ops:
  0.7 0.7 compare_select_fusion
  1.4 0.6 gather_fusion
  2.0 0.9 fusion.13
  2.8 1.5 %fusion.15 = (f32[64,128]{1,0:T(8,128)}, f32[64,128]{1,0:T(8,128)}) fusion(s32[64]{0:T(128)} %param.7, s32[128]{0:T(128)S(1)} %get-tuple-element.22, s32[128]{0:T(128)S(1)} %get-tuple-element.23, pred[128]{0:T(512)(128)(4,1)S(1)} %compare_and_fusion), kind=kLoop, calls=%fused_computation.47 | loop fusion | flops 122880 | bytes 66944 | tf_op jit(solution)/shard_map/sin | solution.py:48
  4.3 3.6 %shard_map.68 = (f32[64,8192]{1,0:T(8,128)}, bf16[64,8192]{1,0:T(8,128)(2,1)}) custom-call(bf16[64,8192]{1,0:T(8,128)(2,1)} %x_ref.1, f32[64,128]{1,0:T(8,128)} %get-tuple-element.21.cos_ref, f32[64,128]{1,0:T(8,128)} %get-tuple-element.20.sin_ref, f32[64,64]{1,0:T(8,128)} %copy-done.3), custom_call_target="tpu_custom_call" | custom-call | tf_op jit(solution)/shard_map/pallas_call | solution.py:42
  7.9 2.5 %fusion.26 = f32[24,8192]{1,0:T(8,128)S(1)} fusion(f32[64,8192]{1,0:T(8,128)} %get-tuple-element.4, s32[64]{0:T(128)} %param.6, s32[24]{0:T(128)S(1)} %iota_add_fusion), kind=kOutput, calls=%fused_computation.59 | convolution fusion | flops 150996480 | bytes 2883936 | tf_op jit(solution)/shard_map/dot_general | solution.py:83
  10.5 1.1 %pad_maximum_fusion = f32[32,24,320]{2,1,0:T(8,128)} fusion(f32[32,24,64]{2,1,0:T(8,128)S(1)} %broadcast_in_dim.86, f32[32,24,256]{2,1,0:T(8,128)S(1)} %bitcast.30), kind=kLoop, calls=%fused_computation.9 | loop fusion | flops 245760 | bytes 1966080 | tf_op jit(solution)/shard_map/concatenate | solution.py:95
  11.6 7.6 %all-to-all-start = ((f32[32,24,320]{2,1,0:T(8,128)}), f32[32,24,320]{2,1,0:T(8,128)S(1)}, u32[]{:S(2)}, u32[]{:S(2)}) async-start(f32[32,24,320]{2,1,0:T(8,128)} %pad_maximum_fusion), calls=%async_computation | async-start | bytes 2359296 | tf_op jit(solution)/shard_map/all_to_all | solution.py:102
  19.7 0.5 select_select_fusion.5
  20.2 14.6 %maximum_maximum_fusion = bf16[256,8192]{1,0:T(8,128)(2,1)} fusion(bf16[64,4096]{1,0:T(8,128)(2,1)S(1)} %get-tuple-element.13, bf16[64,4096]{1,0:T(8,128)(2,1)S(1)} %get-tuple-element.12, bf16[64,4096]{1,0:T(8,128)(2,1)S(1)} %get-tuple-element.14, bf16[64,4096]{1,0:T(8,128)(2,1)S(1)} %get-tuple-element.15, bf16[64,4096]{1,0:T(8,128)(2,1)S(1)} %get-tuple-element.9, ...), kind=kLoop, calls=%fused_computation.7 | loop fusion | flops 29360128 | bytes 8388608 | tf_op jit(solution)/shard_map/concatenate | solution.py:138
  34.8 1.8 %all-to-all-done = f32[32,24,320]{2,1,0:T(8,128)S(1)} async-done(((f32[32,24,320]{2,1,0:T(8,128)}), f32[32,24,320]{2,1,0:T(8,128)S(1)}, u32[]{:S(2)}, u32[]{:S(2)}) %all-to-all-start) | async-done | bytes 983072 | tf_op jit(solution)/shard_map/all_to_all | solution.py:102
  37.0 0.9 %broadcast_in_dim.87 = f32[32,24,256]{2,1,0:T(8,128)} broadcast(f32[24,256]{1,0:T(8,128)S(1)} %slice_divide_fusion), dimensions={1,2} | broadcast | bytes 811008 | tf_op jit(solution)/shard_map/broadcast_in_dim | solution.py:108
  38.0 5.5 %all-to-all-start.1 = ((f32[32,24,256]{2,1,0:T(8,128)}), f32[32,24,256]{2,1,0:T(8,128)S(1)}, u32[]{:S(2)}, u32[]{:S(2)}) async-start(f32[32,24,256]{2,1,0:T(8,128)} %broadcast_in_dim.87), calls=%async_computation.1 | async-start | bytes 1572864 | tf_op jit(solution)/shard_map/all_to_all | solution.py:107
  43.5 1.0 %fusion.9 = (f32[16,4096]{1,0:T(8,128)S(1)}, f32[16,4096]{1,0:T(8,128)S(1)}) fusion(s32[4096]{0:T(1024)S(1)} %get-tuple-element.32, s32[4096]{0:T(1024)S(1)} %get-tuple-element.33, pred[4096]{0:T(1024)(128)(4,1)S(1)} %fusion.24), kind=kLoop, calls=%fused_computation.27 | loop fusion | flops 983040 | bytes 561152 | tf_op jit(solution)/shard_map/cos | solution.py:57
  44.6 12.1 %all-to-all-done.1 = f32[32,24,256]{2,1,0:T(8,128)S(1)} async-done(((f32[32,24,256]{2,1,0:T(8,128)}), f32[32,24,256]{2,1,0:T(8,128)S(1)}, u32[]{:S(2)}, u32[]{:S(2)}) %all-to-all-start.1) | async-done | bytes 786464 | tf_op jit(solution)/shard_map/all_to_all | solution.py:107
  57.2 8.0 %collective-permute-start = (bf16[6,8192]{1,0:T(8,128)(2,1)S(1)}, bf16[6,8192]{1,0:T(8,128)(2,1)S(1)}, u32[]{:S(2)}, u32[]{:S(2)}) collective-permute-start(bf16[6,8192]{1,0:T(8,128)(2,1)S(1)} %constant_dynamic-slice_fusion), channel_id=1, source_target_pairs={{0,1},{8,2},{16,3},{24,4},{32,5},{40,6},{48,7},{56,9},{64,10},{72,... | collective-permute-start | bytes 294920 | tf_op jit(solution)/shard_map/ppermute | solution.py:125
  65.2 2.0 %subtract_convert_fusion = (bf16[16,24,4096]{2,1,0:T(8,128)(2,1)S(1)}, bf16[16,24,4096]{2,1,0:T(8,128)(2,1)S(1)}) fusion(f32[16,4096]{1,0:T(8,128)S(1)} %get-tuple-element.19, f32[24,4096]{1,0:T(8,128)S(1)} %get-tuple-element.17, f32[16,4096]{1,0:T(8,128)S(1)} %get-tuple-element.18, f32[24,4096]{1,0:T(8,128)S(1)} %get-tuple-element.16), kind=kLoop, calls=%fused_computation.6 | loop fusion | flops 12582912 | bytes 7602176 | tf_op jit(solution)/shard_map/convert
  67.3 3.5 %fusion.3 = f32[64,24]{0,1:T(8,128)S(1)} fusion(bf16[4,64,8192,1]{2,1,3,0:T(8,128)(2,1)S(1)} %bitcast.28, bf16[16,24,4096]{2,1,0:T(8,128)(2,1)S(1)} %get-tuple-element.7, bf16[16,24,4096]{2,1,0:T(8,128)(2,1)S(1)} %get-tuple-element.6), kind=kOutput, calls=%fused_computation.8 | convolution fusion | flops 1623292416 | bytes 10491904 | tf_op jit(solution)/shard_map/dot_general | solution.py:140
  70.9 0.7 reshape.157
  71.5 5.9 %all-to-all-start.2 = ((f32[8,1,192]{2,1,0:T(1,128)}), f32[8,1,192]{2,1,0:T(1,128)S(1)}, u32[]{:S(2)}, u32[]{:S(2)}) async-start(f32[8,1,192]{2,1,0:T(1,128)} %reshape.157), calls=%async_computation.2 | async-start | bytes 16384 | tf_op jit(solution)/shard_map/all_to_all | solution.py:144
  77.4 7.7 %all-to-all-done.2 = f32[8,1,192]{2,1,0:T(1,128)S(1)} async-done(((f32[8,1,192]{2,1,0:T(1,128)}), f32[8,1,192]{2,1,0:T(1,128)S(1)}, u32[]{:S(2)}, u32[]{:S(2)}) %all-to-all-start.2) | async-done | bytes 6176 | tf_op jit(solution)/shard_map/all_to_all | solution.py:144
  85.6 0.7 reduce.1
  86.4 0.7 all_to_all.22
  87.1 0.7 dynamic-slice_select_fusion
  (40 shorter events, 2.0 us)
Async XLA Ops:
  0.6 0.7 copy-start
  1.9 2.4 %copy-start.3 = (f32[64,64]{1,0:T(8,128)}, f32[64,64]{1,0:T(8,128)S(1)}, u32[]{:S(2)}) copy-start(f32[64,64]{1,0:T(8,128)S(1)} %gather_fusion) | copy-start | bytes 49156
  7.9 11.5 %copy-start.1 = (bf16[64,8192]{1,0:T(8,128)(2,1)S(1)}, bf16[64,8192]{1,0:T(8,128)(2,1)}, u32[]{:S(2)}) copy-start(bf16[64,8192]{1,0:T(8,128)(2,1)} %get-tuple-element.5) | copy-start | bytes 3145732
  11.6 25.0 %all-to-all-start = ((f32[32,24,320]{2,1,0:T(8,128)}), f32[32,24,320]{2,1,0:T(8,128)S(1)}, u32[]{:S(2)}, u32[]{:S(2)}) async-start(f32[32,24,320]{2,1,0:T(8,128)} %pad_maximum_fusion), calls=%async_computation | async-start | bytes 2359296 | tf_op jit(solution)/shard_map/all_to_all | solution.py:102
  38.0 18.7 %all-to-all-start.1 = ((f32[32,24,256]{2,1,0:T(8,128)}), f32[32,24,256]{2,1,0:T(8,128)S(1)}, u32[]{:S(2)}, u32[]{:S(2)}) async-start(f32[32,24,256]{2,1,0:T(8,128)} %broadcast_in_dim.87), calls=%async_computation.1 | async-start | bytes 1572864 | tf_op jit(solution)/shard_map/all_to_all | solution.py:107
  57.2 10.1 %copy-start.2 = (bf16[256,8192]{1,0:T(8,128)(2,1)S(1)}, bf16[256,8192]{1,0:T(8,128)(2,1)}, u32[]{:S(2)}) copy-start(bf16[256,8192]{1,0:T(8,128)(2,1)} %maximum_maximum_fusion) | copy-start | bytes 12582916
  57.2 29.9 %collective-permute-start = (bf16[6,8192]{1,0:T(8,128)(2,1)S(1)}, bf16[6,8192]{1,0:T(8,128)(2,1)S(1)}, u32[]{:S(2)}, u32[]{:S(2)}) collective-permute-start(bf16[6,8192]{1,0:T(8,128)(2,1)S(1)} %constant_dynamic-slice_fusion), channel_id=1, source_target_pairs={{0,1},{8,2},{16,3},{24,4},{32,5},{40,6},{48,7},{56,9},{64,10},{72,... | collective-permute-start | bytes 294920 | tf_op jit(solution)/shard_map/ppermute | solution.py:125
  71.5 13.6 %all-to-all-start.2 = ((f32[8,1,192]{2,1,0:T(1,128)}), f32[8,1,192]{2,1,0:T(1,128)S(1)}, u32[]{:S(2)}, u32[]{:S(2)}) async-start(f32[8,1,192]{2,1,0:T(1,128)} %reshape.157), calls=%async_computation.2 | async-start | bytes 16384 | tf_op jit(solution)/shard_map/all_to_all | solution.py:144

commit v7 on v6

--- a/solution.py
+++ b/solution.py
@@ -94,15 +94,16 @@
     per_chunk = width // MFREQ
     payload = jnp.concatenate(
         [
-            numer.reshape(block, chunks, width).transpose(1, 0, 2),
-            jnp.broadcast_to(denom[None], (chunks, block, CYCLES)),
+            numer.reshape(block, chunks, width).transpose(1, 0, 2).reshape(chunks, block * width),
+            jnp.broadcast_to(denom.reshape(1, block * CYCLES), (chunks, block * CYCLES)),
         ],
-        axis=2,
+        axis=1,
     )
     summed = jnp.sum(lax.all_to_all(payload, "dom", 0, 0, tiled=True), axis=0)
-    numer_chunk = summed[:, :width].reshape(block, per_chunk, MFREQ)
+    numer_chunk = summed[: block * width].reshape(block, per_chunk, MFREQ)
+    denom_all = summed[block * width :].reshape(block, CYCLES)
     first_cycle = (dom_rank * per_chunk) % CYCLES
-    denom_chunk = lax.dynamic_slice_in_dim(summed[:, width:], first_cycle, per_chunk, 1)
+    denom_chunk = lax.dynamic_slice_in_dim(denom_all, first_cycle, per_chunk, 1)
     plain_chunk = (numer_chunk / (denom_chunk[:, :, None] + 1.0)).reshape(block, width)
     plain = lax.all_to_all(
         jnp.broadcast_to(plain_chunk[None], (chunks, block, width)), "dom", 0, 0, tiled=True

time: 88.6 us -> 90.2 us (1.018)
  local copies, waits for them, and re-layouts: 4.05 us -> 6.38 us
  waiting for transfers between devices: 21.7 us -> 19.9 us
  starting transfers between devices: 27 us -> 28.7 us
    all_to_all x0 -> x1, local copies, waits for them, and re-layouts: none -> 1.96 us  [local(): summed = jnp.sum(lax.all_to_all(payload, 'dom', 0, 0, tiled=True), axis=0)]
    all_to_all x1, starting transfers between devices: 5.54 us -> 7.39 us  [local(): lax.all_to_all(jnp.broadcast_to(plain_chunk[None], (chunks, block, width)...]
    all_to_all x1, waiting for transfers between devices: 1.85 us -> 0.01 us  [local(): summed = jnp.sum(lax.all_to_all(payload, 'dom', 0, 0, tiled=True), axis=0)]
    concatenate x1 -> x0, other arithmetic: 1.1 us -> none  [local(): jnp.concatenate([numer.reshape(block, chunks, width).transpose(1, 0, 2),...]
  transfers between devices with their start and end apart: 4 -> 4, of which waited for: 3 -> 2; matrix products, arithmetic and copies ran while one was open for 27% -> 27% of each run, Pallas kernels for 0% -> 0%
where the time goes in v7:
time: 90.2 us; the launch traced here: 89.4 us
  starting transfers between devices  28.7 us (32%)
  other arithmetic  23.1 us (26%)
  waiting for transfers between devices  19.9 us (22%)
  matrix products  6.73 us (7%)
  local copies, waits for them, and re-layouts  6.38 us (7%)
  Pallas kernels  3.6 us (4%)
  between operations  0.98 us (1%)
    concatenate x1, other arithmetic, local(): stacked = jnp.concatenate(variants, axis=0)  14.6 us
    all_to_all x1, waiting for transfers between devices, local(): lax.all_to_all(jnp.broadcast_to(plain_chunk[None], (chunks, block, width)...  12.1 us
    ppermute x1, starting transfers between devices, local(): got = lax.ppermute(sent, ('dom', 'rot'), pairs)  7.81 us
    all_to_all x1, waiting for transfers between devices, local(): best_scores = lax.all_to_all(best, 'rot', 0, 1, tiled=True)  7.73 us
    all_to_all x1, starting transfers between devices, local(): summed = jnp.sum(lax.all_to_all(payload, 'dom', 0, 0, tiled=True), axis=0)  7.62 us
    all_to_all x1, starting transfers between devices, local(): lax.all_to_all(jnp.broadcast_to(plain_chunk[None], (chunks, block, width)...  7.39 us
    all_to_all x1, starting transfers between devices, local(): best_scores = lax.all_to_all(best, 'rot', 0, 1, tiled=True)  5.86 us
    pallas_call x1, Pallas kernels, derotate_and_modulate(): pl.pallas_call(prologue_kernel, out_shape=(jax.ShapeDtypeStruct((count, K...  3.6 us
  transfers between devices with their start and end apart: 4, of which 2 were waited for; matrix products, arithmetic and copies ran while one was open for 27% of the time, Pallas kernels for 0%

profile of v7, /device:TPU:2, one launch (start us, length us, event | category | flops | bytes accessed | tf_op | source)
XLA Modules:
  0.0 89.4 jit_solution(14822614946620215822)
XLA Ops:
  0.7 0.7 compare_select_fusion
  1.4 0.6 gather_fusion
  2.0 0.9 fusion.13
  2.8 1.5 %fusion.15 = (f32[64,128]{1,0:T(8,128)}, f32[64,128]{1,0:T(8,128)}) fusion(s32[64]{0:T(128)} %param.7, s32[128]{0:T(128)S(1)} %get-tuple-element.22, s32[128]{0:T(128)S(1)} %get-tuple-element.23, pred[128]{0:T(512)(128)(4,1)S(1)} %compare_and_fusion), kind=kLoop, calls=%fused_computation.46 | loop fusion | flops 122880 | bytes 66944 | tf_op jit(solution)/shard_map/sin | solution.py:48
  4.3 3.6 %shard_map.68 = (f32[64,8192]{1,0:T(8,128)}, bf16[64,8192]{1,0:T(8,128)(2,1)}) custom-call(bf16[64,8192]{1,0:T(8,128)(2,1)} %x_ref.1, f32[64,128]{1,0:T(8,128)} %get-tuple-element.21.cos_ref, f32[64,128]{1,0:T(8,128)} %get-tuple-element.20.sin_ref, f32[64,64]{1,0:T(8,128)} %copy-done.3), custom_call_target="tpu_custom_call" | custom-call | tf_op jit(solution)/shard_map/pallas_call | solution.py:42
  7.9 2.4 %fusion.26 = f32[24,8192]{1,0:T(8,128)S(1)} fusion(f32[64,8192]{1,0:T(8,128)} %get-tuple-element.4, s32[64]{0:T(128)} %param.6, s32[24]{0:T(128)S(1)} %iota_add_fusion), kind=kOutput, calls=%fused_computation.58 | convolution fusion | flops 150996480 | bytes 2883936 | tf_op jit(solution)/shard_map/dot_general | solution.py:83
  10.8 2.0 %copy.15 = f32[32,1,7680]{2,1,0:T(1,128)} copy(f32[32,1,7680]{2,0,1:T(8,128)S(1)} %maximum_bitcast_fusion.4) | data formatting | bytes 1966080 | tf_op jit(solution)/shard_map/all_to_all | solution.py:102
  12.8 7.6 %all-to-all-start = ((f32[32,1,7680]{2,1,0:T(1,128)}), f32[32,1,7680]{2,1,0:T(1,128)S(1)}, u32[]{:S(2)}, u32[]{:S(2)}) async-start(f32[32,1,7680]{2,1,0:T(1,128)} %copy.15), calls=%async_computation | async-start | bytes 1966080 | tf_op jit(solution)/shard_map/all_to_all | solution.py:102
  20.9 0.5 select_select_fusion.5
  21.4 14.6 %maximum_maximum_fusion = bf16[256,8192]{1,0:T(8,128)(2,1)} fusion(bf16[64,4096]{1,0:T(8,128)(2,1)S(1)} %get-tuple-element.13, bf16[64,4096]{1,0:T(8,128)(2,1)S(1)} %get-tuple-element.12, bf16[64,4096]{1,0:T(8,128)(2,1)S(1)} %get-tuple-element.14, bf16[64,4096]{1,0:T(8,128)(2,1)S(1)} %get-tuple-element.15, bf16[64,4096]{1,0:T(8,128)(2,1)S(1)} %get-tuple-element.9, ...), kind=kLoop, calls=%fused_computation.7 | loop fusion | flops 29360128 | bytes 8388608 | tf_op jit(solution)/shard_map/concatenate | solution.py:139
  35.9 0.6 reduce_sum.18
  36.9 0.9 %broadcast_in_dim.89 = f32[32,24,256]{2,1,0:T(8,128)} broadcast(f32[24,256]{1,0:T(8,128)S(1)} %div.39), dimensions={1,2} | broadcast | bytes 811008 | tf_op jit(solution)/shard_map/broadcast_in_dim | solution.py:109
  37.9 7.4 %all-to-all-start.1 = ((f32[32,24,256]{2,1,0:T(8,128)}), f32[32,24,256]{2,1,0:T(8,128)S(1)}, u32[]{:S(2)}, u32[]{:S(2)}) async-start(f32[32,24,256]{2,1,0:T(8,128)} %broadcast_in_dim.89), calls=%async_computation.1 | async-start | bytes 1572864 | tf_op jit(solution)/shard_map/all_to_all | solution.py:108
  45.3 1.0 %fusion.9 = (f32[16,4096]{1,0:T(8,128)S(1)}, f32[16,4096]{1,0:T(8,128)S(1)}) fusion(s32[4096]{0:T(1024)S(1)} %get-tuple-element.32, s32[4096]{0:T(1024)S(1)} %get-tuple-element.33, pred[4096]{0:T(1024)(128)(4,1)S(1)} %fusion.24), kind=kLoop, calls=%fused_computation.27 | loop fusion | flops 983040 | bytes 561152 | tf_op jit(solution)/shard_map/cos | solution.py:57
  46.3 12.1 %all-to-all-done.1 = f32[32,24,256]{2,1,0:T(8,128)S(1)} async-done(((f32[32,24,256]{2,1,0:T(8,128)}), f32[32,24,256]{2,1,0:T(8,128)S(1)}, u32[]{:S(2)}, u32[]{:S(2)}) %all-to-all-start.1) | async-done | bytes 786464 | tf_op jit(solution)/shard_map/all_to_all | solution.py:108
  59.0 7.8 %collective-permute-start = (bf16[6,8192]{1,0:T(8,128)(2,1)S(1)}, bf16[6,8192]{1,0:T(8,128)(2,1)S(1)}, u32[]{:S(2)}, u32[]{:S(2)}) collective-permute-start(bf16[6,8192]{1,0:T(8,128)(2,1)S(1)} %constant_dynamic-slice_fusion), channel_id=1, source_target_pairs={{0,1},{8,2},{16,3},{24,4},{32,5},{40,6},{48,7},{56,9},{64,10},{72,... | collective-permute-start | bytes 294920 | tf_op jit(solution)/shard_map/ppermute | solution.py:126
  66.8 2.0 %subtract_convert_fusion = (bf16[16,24,4096]{2,1,0:T(8,128)(2,1)S(1)}, bf16[16,24,4096]{2,1,0:T(8,128)(2,1)S(1)}) fusion(f32[16,4096]{1,0:T(8,128)S(1)} %get-tuple-element.19, f32[24,4096]{1,0:T(8,128)S(1)} %get-tuple-element.17, f32[16,4096]{1,0:T(8,128)S(1)} %get-tuple-element.18, f32[24,4096]{1,0:T(8,128)S(1)} %get-tuple-element.16), kind=kLoop, calls=%fused_computation.6 | loop fusion | flops 12582912 | bytes 7602176 | tf_op jit(solution)/shard_map/convert
  68.8 3.5 %fusion.3 = f32[64,24]{0,1:T(8,128)S(1)} fusion(bf16[4,64,8192,1]{2,1,3,0:T(8,128)(2,1)S(1)} %bitcast.30, bf16[16,24,4096]{2,1,0:T(8,128)(2,1)S(1)} %get-tuple-element.7, bf16[16,24,4096]{2,1,0:T(8,128)(2,1)S(1)} %get-tuple-element.6), kind=kOutput, calls=%fused_computation.8 | convolution fusion | flops 1623292416 | bytes 10491904 | tf_op jit(solution)/shard_map/dot_general | solution.py:141
  72.4 0.7 reshape.185
  73.1 5.9 %all-to-all-start.2 = ((f32[8,1,192]{2,1,0:T(1,128)}), f32[8,1,192]{2,1,0:T(1,128)S(1)}, u32[]{:S(2)}, u32[]{:S(2)}) async-start(f32[8,1,192]{2,1,0:T(1,128)} %reshape.185), calls=%async_computation.2 | async-start | bytes 16384 | tf_op jit(solution)/shard_map/all_to_all | solution.py:145
  79.0 7.7 %all-to-all-done.2 = f32[8,1,192]{2,1,0:T(1,128)S(1)} async-done(((f32[8,1,192]{2,1,0:T(1,128)}), f32[8,1,192]{2,1,0:T(1,128)S(1)}, u32[]{:S(2)}, u32[]{:S(2)}) %all-to-all-start.2) | async-done | bytes 6176 | tf_op jit(solution)/shard_map/all_to_all | solution.py:145
  87.2 0.7 reduce.2
  88.0 0.7 all_to_all.26
  88.6 0.7 dynamic-slice_select_fusion
  (46 shorter events, 2.4 us)
Async XLA Ops:
  0.6 0.7 copy-start
  1.9 2.4 %copy-start.3 = (f32[64,64]{1,0:T(8,128)}, f32[64,64]{1,0:T(8,128)S(1)}, u32[]{:S(2)}) copy-start(f32[64,64]{1,0:T(8,128)S(1)} %gather_fusion) | copy-start | bytes 49156
  10.3 10.3 %copy-start.1 = (bf16[64,8192]{1,0:T(8,128)(2,1)S(1)}, bf16[64,8192]{1,0:T(8,128)(2,1)}, u32[]{:S(2)}) copy-start(bf16[64,8192]{1,0:T(8,128)(2,1)} %get-tuple-element.5) | copy-start | bytes 3145732
  12.8 23.2 %all-to-all-start = ((f32[32,1,7680]{2,1,0:T(1,128)}), f32[32,1,7680]{2,1,0:T(1,128)S(1)}, u32[]{:S(2)}, u32[]{:S(2)}) async-start(f32[32,1,7680]{2,1,0:T(1,128)} %copy.15), calls=%async_computation | async-start | bytes 1966080 | tf_op jit(solution)/shard_map/all_to_all | solution.py:102
  37.9 20.6 %all-to-all-start.1 = ((f32[32,24,256]{2,1,0:T(8,128)}), f32[32,24,256]{2,1,0:T(8,128)S(1)}, u32[]{:S(2)}, u32[]{:S(2)}) async-start(f32[32,24,256]{2,1,0:T(8,128)} %broadcast_in_dim.89), calls=%async_computation.1 | async-start | bytes 1572864 | tf_op jit(solution)/shard_map/all_to_all | solution.py:108
  58.9 9.9 %copy-start.2 = (bf16[256,8192]{1,0:T(8,128)(2,1)S(1)}, bf16[256,8192]{1,0:T(8,128)(2,1)}, u32[]{:S(2)}) copy-start(bf16[256,8192]{1,0:T(8,128)(2,1)} %maximum_maximum_fusion) | copy-start | bytes 12582916
  59.0 29.7 %collective-permute-start = (bf16[6,8192]{1,0:T(8,128)(2,1)S(1)}, bf16[6,8192]{1,0:T(8,128)(2,1)S(1)}, u32[]{:S(2)}, u32[]{:S(2)}) collective-permute-start(bf16[6,8192]{1,0:T(8,128)(2,1)S(1)} %constant_dynamic-slice_fusion), channel_id=1, source_target_pairs={{0,1},{8,2},{16,3},{24,4},{32,5},{40,6},{48,7},{56,9},{64,10},{72,... | collective-permute-start | bytes 294920 | tf_op jit(solution)/shard_map/ppermute | solution.py:126
  73.1 13.6 %all-to-all-start.2 = ((f32[8,1,192]{2,1,0:T(1,128)}), f32[8,1,192]{2,1,0:T(1,128)S(1)}, u32[]{:S(2)}, u32[]{:S(2)}) async-start(f32[8,1,192]{2,1,0:T(1,128)} %reshape.185), calls=%async_computation.2 | async-start | bytes 16384 | tf_op jit(solution)/shard_map/all_to_all | solution.py:145

commit v8 on v6

--- a/solution.py
+++ b/solution.py
@@ -4,6 +4,7 @@
 import jax.numpy as jnp
 from jax import lax
 from jax.experimental import pallas as pl
+from jax.experimental.pallas import tpu as pltpu
 from jax.sharding import PartitionSpec as P
 
 CYCLES = 64
@@ -18,9 +19,21 @@
     return phase.astype(jnp.float32) * (2.0 * math.pi / total)
 
 
-def prologue_kernel(x_ref, cos_ref, sin_ref, ctf_ref, w_ref, mod_ref):
+def split_dot(member, value):
+    high = value.astype(jnp.bfloat16)
+    rest = value - high.astype(jnp.float32)
+    mid = rest.astype(jnp.bfloat16)
+    low = (rest - mid.astype(jnp.float32)).astype(jnp.bfloat16)
+    total = jnp.dot(member, high, preferred_element_type=jnp.float32)
+    total = total + jnp.dot(member, mid, preferred_element_type=jnp.float32)
+    return total + jnp.dot(member, low, preferred_element_type=jnp.float32)
+
+
+def prologue_kernel(x_ref, cos_ref, sin_ref, ctf_ref, member_ref, pay_ref, mod_ref, w_ref):
     half = x_ref.shape[1] // 2
     lanes = cos_ref.shape[1]
+    chunks, _, width = pay_ref.shape
+    width -= ctf_ref.shape[1]
     cosine = cos_ref[...]
     sine = sin_ref[...]
     low = lax.broadcasted_iota(jnp.int32, cosine.shape, 1) < MFREQ
@@ -34,18 +47,27 @@
         w_ref[:, im_cols] = (imag_part * cosine - real_part * sine) * gain
         mod_ref[:, re_cols] = (real_part * gain).astype(jnp.bfloat16)
         mod_ref[:, im_cols] = (imag_part * gain).astype(jnp.bfloat16)
+    member = member_ref[...]
+    gains = ctf_ref[...]
+    denom = split_dot(member, gains * gains)
+    numer = split_dot(member, w_ref[...])
+    for x in range(chunks):
+        pay_ref[x, :, :width] = numer[:, x * width : (x + 1) * width]
+        pay_ref[x, :, width:] = denom
 
 
-def derotate_and_modulate(particles, rotation, ctf_rows, total):
+def derotate_and_sum(particles, rotation, ctf_rows, member, chunks, total):
     angle = column_angles(rotation, total, 2 * MFREQ)
     count = particles.shape[0]
+    block = member.shape[0]
     return pl.pallas_call(
         prologue_kernel,
         out_shape=(
-            jax.ShapeDtypeStruct((count, K), jnp.float32),
+            jax.ShapeDtypeStruct((chunks, block, K // chunks + CYCLES), jnp.float32),
             jax.ShapeDtypeStruct((count, K), jnp.bfloat16),
         ),
-    )(particles, jnp.cos(angle), jnp.sin(angle), ctf_rows)
+        scratch_shapes=[pltpu.VMEM((count, K), jnp.float32)],
+    )(particles, jnp.cos(angle), jnp.sin(angle), ctf_rows, member)
 
 
 def rotate_all(refs, turns, total):
@@ -75,30 +97,14 @@
 
     ctf_rows = ctf_table[group]
     half = K // 2
-    weighted, modulated = derotate_and_modulate(particles, rot_index, ctf_rows, total)
     first_class = rot_rank * block
     member = (
         (first_class + jnp.arange(block, dtype=jnp.int32))[:, None] == assign[None, :]
-    ).astype(jnp.float32)
-    numer = jnp.dot(
-        member, weighted, precision=lax.Precision.HIGHEST, preferred_element_type=jnp.float32
-    )
-    denom = jnp.dot(
-        member,
-        ctf_rows * ctf_rows,
-        precision=lax.Precision.HIGHEST,
-        preferred_element_type=jnp.float32,
-    )
+    ).astype(jnp.bfloat16)
     chunks = dom_count
     width = K // chunks
     per_chunk = width // MFREQ
-    payload = jnp.concatenate(
-        [
-            numer.reshape(block, chunks, width).transpose(1, 0, 2),
-            jnp.broadcast_to(denom[None], (chunks, block, CYCLES)),
-        ],
-        axis=2,
-    )
+    payload, modulated = derotate_and_sum(particles, rot_index, ctf_rows, member, chunks, total)
     summed = jnp.sum(lax.all_to_all(payload, "dom", 0, 0, tiled=True), axis=0)
     numer_chunk = summed[:, :width].reshape(block, per_chunk, MFREQ)
     first_cycle = (dom_rank * per_chunk) % CYCLES

time: 88.6 us -> 87.4 us (0.986)
  matrix products: 6.82 us -> 3.47 us
  other arithmetic: 23.7 us -> 25.1 us
  starting transfers between devices: 27 us -> 28.3 us
  waiting for transfers between devices: 21.7 us -> 20.5 us
    dot_general x2 -> x0, matrix products: 3.35 us -> none  [the longest x1 2.49 us: local(): jnp.dot(member, weighted, precision=lax.Precision.HIGHEST, preferred_elem...]
    convert_element_type x0 -> x1, other arithmetic: none -> 1.32 us  [local(): member = ((first_class + jnp.arange(block, dtype=jnp.int32))[:, None] ==...]
    all_to_all x1, waiting for transfers between devices: 1.85 us -> 0.63 us  [local(): summed = jnp.sum(lax.all_to_all(payload, 'dom', 0, 0, tiled=True), axis=0)]
    all_to_all x1, starting transfers between devices: 5.54 us -> 6.75 us  [local(): lax.all_to_all(jnp.broadcast_to(plain_chunk[None], (chunks, block, width)...]
    select_n x2, other arithmetic: 0.77 us -> 1.97 us  [local(): jnp.where(step == 0, real_part, jnp.where(step == 1, imag_part, jnp.where...]
    concatenate x1 -> x0, other arithmetic: 1.1 us -> none  [local(): jnp.concatenate([numer.reshape(block, chunks, width).transpose(1, 0, 2),...]
  transfers between devices with their start and end apart: 4 -> 4, of which waited for: 3 -> 3; matrix products, arithmetic and copies ran while one was open for 27% -> 29% of each run, Pallas kernels for 0% -> 0%
where the time goes in v8:
time: 87.4 us; the launch traced here: 86.5 us
  starting transfers between devices  28.3 us (32%)
  other arithmetic  25.1 us (29%)
  waiting for transfers between devices  20.5 us (23%)
  local copies, waits for them, and re-layouts  4.54 us (5%)
  Pallas kernels  3.66 us (4%)
  matrix products  3.47 us (4%)
  between operations  0.91 us (1%)
    concatenate x1, other arithmetic, local(): stacked = jnp.concatenate(variants, axis=0)  14.6 us
    all_to_all x1, waiting for transfers between devices, local(): lax.all_to_all(jnp.broadcast_to(plain_chunk[None], (chunks, block, width)...  12.1 us
    ppermute x1, starting transfers between devices, local(): got = lax.ppermute(sent, ('dom', 'rot'), pairs)  7.99 us
    all_to_all x1, starting transfers between devices, local(): summed = jnp.sum(lax.all_to_all(payload, 'dom', 0, 0, tiled=True), axis=0)  7.75 us
    all_to_all x1, waiting for transfers between devices, local(): best_scores = lax.all_to_all(best, 'rot', 0, 1, tiled=True)  7.73 us
    all_to_all x1, starting transfers between devices, local(): lax.all_to_all(jnp.broadcast_to(plain_chunk[None], (chunks, block, width)...  6.75 us
    all_to_all x1, starting transfers between devices, local(): best_scores = lax.all_to_all(best, 'rot', 0, 1, tiled=True)  5.86 us
    pallas_call x1, Pallas kernels, derotate_and_sum(): pl.pallas_call(prologue_kernel, out_shape=(jax.ShapeDtypeStruct((chunks,...  3.66 us
  transfers between devices with their start and end apart: 4, of which 3 were waited for; matrix products, arithmetic and copies ran while one was open for 29% of the time, Pallas kernels for 0%

profile of v8, /device:TPU:2, one launch (start us, length us, event | category | flops | bytes accessed | tf_op | source)
XLA Modules:
  0.0 86.5 jit_solution(15269575132374716300)
XLA Ops:
  0.7 0.7 compare_select_fusion
  1.4 1.2 %gather_fusion = f32[64,64]{1,0:T(8,128)} fusion(f32[32,64]{1,0:T(8,128)S(1)} %copy-done, s32[1024]{0:T(1024)S(1)} %pad_clamp_fusion), kind=kCustom, calls=%fused_computation | custom fusion | bytes 33024 | tf_op jit(solution)/shard_map/gather | solution.py:98
  2.5 1.3 %compare_convert_fusion.member_ref = bf16[24,64]{1,0:T(8,128)(2,1)} fusion(s32[64]{0:T(128)} %param.6, s32[24]{0:T(128)S(1)} %iota_add_fusion), kind=kLoop, calls=%fused_computation.55 | loop fusion | flops 3072 | bytes 3424 | tf_op jit(solution)/shard_map/convert_element_type | solution.py:103
  3.9 1.5 %fusion.13 = (f32[64,128]{1,0:T(8,128)}, f32[64,128]{1,0:T(8,128)}) fusion(s32[64]{0:T(128)} %param.7, s32[128]{0:T(128)S(1)} %get-tuple-element.22, s32[128]{0:T(128)S(1)} %get-tuple-element.23, pred[128]{0:T(512)(128)(4,1)S(1)} %compare_and_fusion), kind=kLoop, calls=%fused_computation.43 | loop fusion | flops 122880 | bytes 66944 | tf_op jit(solution)/shard_map/sin | solution.py:70
  5.3 3.7 %shard_map.68 = (f32[32,24,320]{2,1,0:T(8,128)}, bf16[64,8192]{1,0:T(8,128)(2,1)}) custom-call(bf16[64,8192]{1,0:T(8,128)(2,1)} %x_ref.1, f32[64,128]{1,0:T(8,128)} %get-tuple-element.21.cos_ref, f32[64,128]{1,0:T(8,128)} %get-tuple-element.20.sin_ref, f32[64,64]{1,0:T(8,128)} %gather_fusion, bf16[24,64]{1,0:T(8,128)(2,1)} %compare_convert_fusion.member_ref), custom_call_target="tpu_custom_call" | custom-call | tf_op jit(solution)/shard_map/pallas_call | solution.py:63
  9.0 7.8 %all-to-all-start = ((f32[32,24,320]{2,1,0:T(8,128)}), f32[32,24,320]{2,1,0:T(8,128)S(1)}, u32[]{:S(2)}, u32[]{:S(2)}) async-start(f32[32,24,320]{2,1,0:T(8,128)} %get-tuple-element.4), calls=%async_computation | async-start | bytes 2359296 | tf_op jit(solution)/shard_map/all_to_all | solution.py:108
  17.0 1.4 %select_select_fusion.1 = (bf16[64,4096]{1,0:T(8,128)(2,1)S(1)}, bf16[64,4096]{1,0:T(8,128)(2,1)S(1)}) fusion(pred[4096]{0:T(1024)(128)(4,1)S(1)} %get-tuple-element.24, pred[4096]{0:T(1024)(128)(4,1)S(1)} %get-tuple-element.25, pred[4096]{0:T(1024)(128)(4,1)S(1)} %broadcast_compare_fusion.8, bf16[64,8192]{1,0:T(8,128)(2,1)} %get-tuple-element.5), kind=kLoop, calls=%fused_computation.13 | loop fusion | flops 2097152 | bytes 2109440 | tf_op jit(solution)/shard_map/jit(_where)/select_n | solution.py:141
  18.4 0.5 select_select_fusion.5
  19.0 14.6 %maximum_maximum_fusion = bf16[256,8192]{1,0:T(8,128)(2,1)} fusion(bf16[64,4096]{1,0:T(8,128)(2,1)S(1)} %get-tuple-element.13, bf16[64,4096]{1,0:T(8,128)(2,1)S(1)} %get-tuple-element.12, bf16[64,4096]{1,0:T(8,128)(2,1)S(1)} %get-tuple-element.14, bf16[64,4096]{1,0:T(8,128)(2,1)S(1)} %get-tuple-element.15, bf16[64,4096]{1,0:T(8,128)(2,1)S(1)} %get-tuple-element.9, ...), kind=kLoop, calls=%fused_computation.7 | loop fusion | flops 29360128 | bytes 8388608 | tf_op jit(solution)/shard_map/concatenate | solution.py:144
  33.5 0.6 all-to-all-done
  34.5 0.9 %broadcast_in_dim.80 = f32[32,24,256]{2,1,0:T(8,128)} broadcast(f32[24,256]{1,0:T(8,128)S(1)} %slice_divide_fusion), dimensions={1,2} | broadcast | bytes 811008 | tf_op jit(solution)/shard_map/broadcast_in_dim | solution.py:114
  35.5 6.8 %all-to-all-start.1 = ((f32[32,24,256]{2,1,0:T(8,128)}), f32[32,24,256]{2,1,0:T(8,128)S(1)}, u32[]{:S(2)}, u32[]{:S(2)}) async-start(f32[32,24,256]{2,1,0:T(8,128)} %broadcast_in_dim.80), calls=%async_computation.1 | async-start | bytes 1572864 | tf_op jit(solution)/shard_map/all_to_all | solution.py:113
  42.2 1.0 %fusion.9 = (f32[16,4096]{1,0:T(8,128)S(1)}, f32[16,4096]{1,0:T(8,128)S(1)}) fusion(s32[4096]{0:T(1024)S(1)} %get-tuple-element.32, s32[4096]{0:T(1024)S(1)} %get-tuple-element.33, pred[4096]{0:T(1024)(128)(4,1)S(1)} %fusion.22), kind=kLoop, calls=%fused_computation.25 | loop fusion | flops 983040 | bytes 561152 | tf_op jit(solution)/shard_map/cos | solution.py:79
  43.3 12.1 %all-to-all-done.1 = f32[32,24,256]{2,1,0:T(8,128)S(1)} async-done(((f32[32,24,256]{2,1,0:T(8,128)}), f32[32,24,256]{2,1,0:T(8,128)S(1)}, u32[]{:S(2)}, u32[]{:S(2)}) %all-to-all-start.1) | async-done | bytes 786464 | tf_op jit(solution)/shard_map/all_to_all | solution.py:113
  56.0 8.0 %collective-permute-start = (bf16[6,8192]{1,0:T(8,128)(2,1)S(1)}, bf16[6,8192]{1,0:T(8,128)(2,1)S(1)}, u32[]{:S(2)}, u32[]{:S(2)}) collective-permute-start(bf16[6,8192]{1,0:T(8,128)(2,1)S(1)} %constant_dynamic-slice_fusion), channel_id=1, source_target_pairs={{0,1},{8,2},{16,3},{24,4},{32,5},{40,6},{48,7},{56,9},{64,10},{72,... | collective-permute-start | bytes 294920 | tf_op jit(solution)/shard_map/ppermute | solution.py:131
  64.0 2.0 %subtract_convert_fusion = (bf16[16,24,4096]{2,1,0:T(8,128)(2,1)S(1)}, bf16[16,24,4096]{2,1,0:T(8,128)(2,1)S(1)}) fusion(f32[16,4096]{1,0:T(8,128)S(1)} %get-tuple-element.19, f32[24,4096]{1,0:T(8,128)S(1)} %get-tuple-element.17, f32[16,4096]{1,0:T(8,128)S(1)} %get-tuple-element.18, f32[24,4096]{1,0:T(8,128)S(1)} %get-tuple-element.16), kind=kLoop, calls=%fused_computation.6 | loop fusion | flops 12582912 | bytes 7602176 | tf_op jit(solution)/shard_map/convert
  66.0 3.5 %fusion.3 = f32[64,24]{0,1:T(8,128)S(1)} fusion(bf16[4,64,8192,1]{2,1,3,0:T(8,128)(2,1)S(1)} %bitcast.20, bf16[16,24,4096]{2,1,0:T(8,128)(2,1)S(1)} %get-tuple-element.7, bf16[16,24,4096]{2,1,0:T(8,128)(2,1)S(1)} %get-tuple-element.6), kind=kOutput, calls=%fused_computation.8 | convolution fusion | flops 1623292416 | bytes 10491904 | tf_op jit(solution)/shard_map/dot_general | solution.py:146
  69.6 0.7 reshape.152
  70.3 5.9 %all-to-all-start.2 = ((f32[8,1,192]{2,1,0:T(1,128)}), f32[8,1,192]{2,1,0:T(1,128)S(1)}, u32[]{:S(2)}, u32[]{:S(2)}) async-start(f32[8,1,192]{2,1,0:T(1,128)} %reshape.152), calls=%async_computation.2 | async-start | bytes 16384 | tf_op jit(solution)/shard_map/all_to_all | solution.py:150
  76.1 7.7 %all-to-all-done.2 = f32[8,1,192]{2,1,0:T(1,128)S(1)} async-done(((f32[8,1,192]{2,1,0:T(1,128)}), f32[8,1,192]{2,1,0:T(1,128)S(1)}, u32[]{:S(2)}, u32[]{:S(2)}) %all-to-all-start.2) | async-done | bytes 6176 | tf_op jit(solution)/shard_map/all_to_all | solution.py:150
  83.9 0.5 broadcast.286
  84.4 0.7 reduce.1
  85.1 0.7 all_to_all.22
  85.8 0.7 dynamic-slice_select_fusion
  (34 shorter events, 1.2 us)
Async XLA Ops:
  0.6 0.7 copy-start
  9.0 9.4 %copy-start.1 = (bf16[64,8192]{1,0:T(8,128)(2,1)S(1)}, bf16[64,8192]{1,0:T(8,128)(2,1)}, u32[]{:S(2)}) copy-start(bf16[64,8192]{1,0:T(8,128)(2,1)} %get-tuple-element.5) | copy-start | bytes 3145732
  9.0 25.2 %all-to-all-start = ((f32[32,24,320]{2,1,0:T(8,128)}), f32[32,24,320]{2,1,0:T(8,128)S(1)}, u32[]{:S(2)}, u32[]{:S(2)}) async-start(f32[32,24,320]{2,1,0:T(8,128)} %get-tuple-element.4), calls=%async_computation | async-start | bytes 2359296 | tf_op jit(solution)/shard_map/all_to_all | solution.py:108
  35.5 19.9 %all-to-all-start.1 = ((f32[32,24,256]{2,1,0:T(8,128)}), f32[32,24,256]{2,1,0:T(8,128)S(1)}, u32[]{:S(2)}, u32[]{:S(2)}) async-start(f32[32,24,256]{2,1,0:T(8,128)} %broadcast_in_dim.80), calls=%async_computation.1 | async-start | bytes 1572864 | tf_op jit(solution)/shard_map/all_to_all | solution.py:113
  55.9 10.1 %copy-start.2 = (bf16[256,8192]{1,0:T(8,128)(2,1)S(1)}, bf16[256,8192]{1,0:T(8,128)(2,1)}, u32[]{:S(2)}) copy-start(bf16[256,8192]{1,0:T(8,128)(2,1)} %maximum_maximum_fusion) | copy-start | bytes 12582916
  56.0 29.9 %collective-permute-start = (bf16[6,8192]{1,0:T(8,128)(2,1)S(1)}, bf16[6,8192]{1,0:T(8,128)(2,1)S(1)}, u32[]{:S(2)}, u32[]{:S(2)}) collective-permute-start(bf16[6,8192]{1,0:T(8,128)(2,1)S(1)} %constant_dynamic-slice_fusion), channel_id=1, source_target_pairs={{0,1},{8,2},{16,3},{24,4},{32,5},{40,6},{48,7},{56,9},{64,10},{72,... | collective-permute-start | bytes 294920 | tf_op jit(solution)/shard_map/ppermute | solution.py:131
  70.3 13.6 %all-to-all-start.2 = ((f32[8,1,192]{2,1,0:T(1,128)}), f32[8,1,192]{2,1,0:T(1,128)S(1)}, u32[]{:S(2)}, u32[]{:S(2)}) async-start(f32[8,1,192]{2,1,0:T(1,128)} %reshape.152), calls=%async_computation.2 | async-start | bytes 16384 | tf_op jit(solution)/shard_map/all_to_all | solution.py:150

commit v9 on v8

--- a/solution.py
+++ b/solution.py
@@ -29,7 +29,17 @@
     return total + jnp.dot(member, low, preferred_element_type=jnp.float32)
 
 
-def prologue_kernel(x_ref, cos_ref, sin_ref, ctf_ref, member_ref, pay_ref, mod_ref, w_ref):
+def prologue_kernel(
+    x_ref, cos_ref, sin_ref, group_ref, table_ref, assign_ref, pay_ref, mod_ref, w_ref, ctf_ref
+):
+    groups = table_ref.shape[0]
+    count = x_ref.shape[0]
+    block = pay_ref.shape[1]
+    onehot = group_ref[...] == lax.broadcasted_iota(jnp.int32, (count, groups), 1)
+    ctf_ref[...] = split_dot(onehot.astype(jnp.bfloat16), table_ref[...])
+    first_class = lax.axis_index("rot") * block
+    classes = first_class + lax.broadcasted_iota(jnp.int32, (block, count), 0)
+    member = (classes == assign_ref[...]).astype(jnp.bfloat16)
     half = x_ref.shape[1] // 2
     lanes = cos_ref.shape[1]
     chunks, _, width = pay_ref.shape
@@ -47,7 +57,6 @@
         w_ref[:, im_cols] = (imag_part * cosine - real_part * sine) * gain
         mod_ref[:, re_cols] = (real_part * gain).astype(jnp.bfloat16)
         mod_ref[:, im_cols] = (imag_part * gain).astype(jnp.bfloat16)
-    member = member_ref[...]
     gains = ctf_ref[...]
     denom = split_dot(member, gains * gains)
     numer = split_dot(member, w_ref[...])
@@ -56,18 +65,27 @@
         pay_ref[x, :, width:] = denom
 
 
-def derotate_and_sum(particles, rotation, ctf_rows, member, chunks, total):
+def derotate_and_sum(particles, rotation, group, ctf_table, assign, block, chunks, total):
     angle = column_angles(rotation, total, 2 * MFREQ)
     count = particles.shape[0]
-    block = member.shape[0]
     return pl.pallas_call(
         prologue_kernel,
         out_shape=(
             jax.ShapeDtypeStruct((chunks, block, K // chunks + CYCLES), jnp.float32),
             jax.ShapeDtypeStruct((count, K), jnp.bfloat16),
         ),
-        scratch_shapes=[pltpu.VMEM((count, K), jnp.float32)],
-    )(particles, jnp.cos(angle), jnp.sin(angle), ctf_rows, member)
+        scratch_shapes=[
+            pltpu.VMEM((count, K), jnp.float32),
+            pltpu.VMEM((count, ctf_table.shape[1]), jnp.float32),
+        ],
+    )(
+        particles,
+        jnp.cos(angle),
+        jnp.sin(angle),
+        group.reshape(count, 1),
+        ctf_table,
+        assign.reshape(1, count),
+    )
 
 
 def rotate_all(refs, turns, total):
@@ -95,16 +113,13 @@
     total = 8 * rot_count
     count = particles.shape[0]
 
-    ctf_rows = ctf_table[group]
     half = K // 2
-    first_class = rot_rank * block
-    member = (
-        (first_class + jnp.arange(block, dtype=jnp.int32))[:, None] == assign[None, :]
-    ).astype(jnp.bfloat16)
     chunks = dom_count
     width = K // chunks
     per_chunk = width // MFREQ
-    payload, modulated = derotate_and_sum(particles, rot_index, ctf_rows, member, chunks, total)
+    payload, modulated = derotate_and_sum(
+        particles, rot_index, group, ctf_table, assign, block, chunks, total
+    )
     summed = jnp.sum(lax.all_to_all(payload, "dom", 0, 0, tiled=True), axis=0)
     numer_chunk = summed[:, :width].reshape(block, per_chunk, MFREQ)
     first_cycle = (dom_rank * per_chunk) % CYCLES

time: 87.4 us -> 85.8 us (0.982)
  other arithmetic: 25.1 us -> 23.1 us
    reshape x0 -> x1, local copies, waits for them, and re-layouts: none -> 1.36 us  [derotate_and_sum(): group.reshape(count, 1)]
    convert_element_type x1 -> x0, other arithmetic: 1.32 us -> none  [local(): member = ((first_class + jnp.arange(block, dtype=jnp.int32))[:, None] ==...]
    gather x1 -> x0, local copies, waits for them, and re-layouts: 1.19 us -> none  [local(): ctf_rows = ctf_table[group]]
  transfers between devices with their start and end apart: 4 -> 4, of which waited for: 3 -> 3; matrix products, arithmetic and copies ran while one was open for 29% -> 30% of each run, Pallas kernels for 0% -> 0%
where the time goes in v9:
time: 85.8 us; the launch traced here: 85 us
  starting transfers between devices  28.3 us (33%)
  other arithmetic  23.1 us (27%)
  waiting for transfers between devices  20.5 us (24%)
  local copies, waits for them, and re-layouts  4.7 us (5%)
  Pallas kernels  3.99 us (5%)
  matrix products  3.47 us (4%)
  between operations  0.9 us (1%)
    concatenate x1, other arithmetic, local(): stacked = jnp.concatenate(variants, axis=0)  14.6 us
    all_to_all x1, waiting for transfers between devices, local(): lax.all_to_all(jnp.broadcast_to(plain_chunk[None], (chunks, block, width)...  12.1 us
    ppermute x1, starting transfers between devices, local(): got = lax.ppermute(sent, ('dom', 'rot'), pairs)  7.99 us
    all_to_all x1, starting transfers between devices, local(): summed = jnp.sum(lax.all_to_all(payload, 'dom', 0, 0, tiled=True), axis=0)  7.75 us
    all_to_all x1, waiting for transfers between devices, local(): best_scores = lax.all_to_all(best, 'rot', 0, 1, tiled=True)  7.73 us
    all_to_all x1, starting transfers between devices, local(): lax.all_to_all(jnp.broadcast_to(plain_chunk[None], (chunks, block, width)...  6.75 us
    all_to_all x1, starting transfers between devices, local(): best_scores = lax.all_to_all(best, 'rot', 0, 1, tiled=True)  5.85 us
    pallas_call x1, Pallas kernels, derotate_and_sum(): pl.pallas_call(prologue_kernel, out_shape=(jax.ShapeDtypeStruct((chunks,...  3.99 us
  transfers between devices with their start and end apart: 4, of which 3 were waited for; matrix products, arithmetic and copies ran while one was open for 30% of the time, Pallas kernels for 0%

profile of v9, /device:TPU:2, one launch (start us, length us, event | category | flops | bytes accessed | tf_op | source)
XLA Modules:
  0.0 85.0 jit_solution(6446353448886474912)
XLA Ops:
  0.7 1.4 %copy.14.group_ref = s32[64,1]{1,0:T(8,128)} copy(s32[64,1]{0,1:T(1,128)} %bitcast.26) | data formatting | bytes 512 | tf_op jit(solution)/shard_map/reshape | solution.py:85
  2.0 1.5 %fusion.13 = (f32[64,128]{1,0:T(8,128)}, f32[64,128]{1,0:T(8,128)}) fusion(s32[64]{0:T(128)} %param.7, s32[128]{0:T(128)S(1)} %get-tuple-element.22, s32[128]{0:T(128)S(1)} %get-tuple-element.23, pred[128]{0:T(512)(128)(4,1)S(1)} %compare_and_fusion), kind=kLoop, calls=%fused_computation.42 | loop fusion | flops 122880 | bytes 66944 | tf_op jit(solution)/shard_map/sin | solution.py:84
  3.5 4.0 %shard_map.68 = (f32[32,24,320]{2,1,0:T(8,128)}, bf16[64,8192]{1,0:T(8,128)(2,1)}) custom-call(bf16[64,8192]{1,0:T(8,128)(2,1)} %x_ref.1, f32[64,128]{1,0:T(8,128)} %get-tuple-element.21.cos_ref, f32[64,128]{1,0:T(8,128)} %get-tuple-element.20.sin_ref, s32[64,1]{1,0:T(8,128)} %copy.14.group_ref, f32[32,64]{1,0:T(8,128)} %table_ref.1, s32[1,64]{1,0:T(1,128)} %bitcast.27), custom_call_target="tpu_custom_call" | custom-call | tf_op jit(solution)/shard_map/pallas_call | solution.py:71
  7.5 7.8 %all-to-all-start = ((f32[32,24,320]{2,1,0:T(8,128)}), f32[32,24,320]{2,1,0:T(8,128)S(1)}, u32[]{:S(2)}, u32[]{:S(2)}) async-start(f32[32,24,320]{2,1,0:T(8,128)} %get-tuple-element.4), calls=%async_computation | async-start | bytes 2359296 | tf_op jit(solution)/shard_map/all_to_all | solution.py:123
  15.5 1.4 %select_select_fusion.1 = (bf16[64,4096]{1,0:T(8,128)(2,1)S(1)}, bf16[64,4096]{1,0:T(8,128)(2,1)S(1)}) fusion(pred[4096]{0:T(1024)(128)(4,1)S(1)} %get-tuple-element.24, pred[4096]{0:T(1024)(128)(4,1)S(1)} %get-tuple-element.25, pred[4096]{0:T(1024)(128)(4,1)S(1)} %broadcast_compare_fusion.8, bf16[64,8192]{1,0:T(8,128)(2,1)} %get-tuple-element.5), kind=kLoop, calls=%fused_computation.12 | loop fusion | flops 2097152 | bytes 2109440 | tf_op jit(solution)/shard_map/jit(_where)/select_n | solution.py:156
  16.9 0.5 select_select_fusion.5
  17.5 14.6 %maximum_maximum_fusion = bf16[256,8192]{1,0:T(8,128)(2,1)} fusion(bf16[64,4096]{1,0:T(8,128)(2,1)S(1)} %get-tuple-element.13, bf16[64,4096]{1,0:T(8,128)(2,1)S(1)} %get-tuple-element.12, bf16[64,4096]{1,0:T(8,128)(2,1)S(1)} %get-tuple-element.14, bf16[64,4096]{1,0:T(8,128)(2,1)S(1)} %get-tuple-element.15, bf16[64,4096]{1,0:T(8,128)(2,1)S(1)} %get-tuple-element.9, ...), kind=kLoop, calls=%fused_computation.6 | loop fusion | flops 29360128 | bytes 8388608 | tf_op jit(solution)/shard_map/concatenate | solution.py:159
  32.0 0.6 all-to-all-done
  33.0 0.9 %broadcast_in_dim.74 = f32[32,24,256]{2,1,0:T(8,128)} broadcast(f32[24,256]{1,0:T(8,128)S(1)} %slice_divide_fusion), dimensions={1,2} | broadcast | bytes 811008 | tf_op jit(solution)/shard_map/broadcast_in_dim | solution.py:129
  34.0 6.8 %all-to-all-start.1 = ((f32[32,24,256]{2,1,0:T(8,128)}), f32[32,24,256]{2,1,0:T(8,128)S(1)}, u32[]{:S(2)}, u32[]{:S(2)}) async-start(f32[32,24,256]{2,1,0:T(8,128)} %broadcast_in_dim.74), calls=%async_computation.1 | async-start | bytes 1572864 | tf_op jit(solution)/shard_map/all_to_all | solution.py:128
  40.7 1.0 %fusion.9 = (f32[16,4096]{1,0:T(8,128)S(1)}, f32[16,4096]{1,0:T(8,128)S(1)}) fusion(s32[4096]{0:T(1024)S(1)} %get-tuple-element.32, s32[4096]{0:T(1024)S(1)} %get-tuple-element.33, pred[4096]{0:T(1024)(128)(4,1)S(1)} %fusion.22), kind=kLoop, calls=%fused_computation.24 | loop fusion | flops 983040 | bytes 561152 | tf_op jit(solution)/shard_map/cos | solution.py:97
  41.8 12.1 %all-to-all-done.1 = f32[32,24,256]{2,1,0:T(8,128)S(1)} async-done(((f32[32,24,256]{2,1,0:T(8,128)}), f32[32,24,256]{2,1,0:T(8,128)S(1)}, u32[]{:S(2)}, u32[]{:S(2)}) %all-to-all-start.1) | async-done | bytes 786464 | tf_op jit(solution)/shard_map/all_to_all | solution.py:128
  54.0 0.2 fusion.4
  54.2 0.1 divide_convert_fusion
  54.4 8.0 %collective-permute-start = (bf16[6,8192]{1,0:T(8,128)(2,1)S(1)}, bf16[6,8192]{1,0:T(8,128)(2,1)S(1)}, u32[]{:S(2)}, u32[]{:S(2)}) collective-permute-start(bf16[6,8192]{1,0:T(8,128)(2,1)S(1)} %constant_dynamic-slice_fusion), channel_id=1, source_target_pairs={{0,1},{8,2},{16,3},{24,4},{32,5},{40,6},{48,7},{56,9},{64,10},{72,... | collective-permute-start | bytes 294920 | tf_op jit(solution)/shard_map/ppermute | solution.py:146
  62.4 2.0 %subtract_convert_fusion = (bf16[16,24,4096]{2,1,0:T(8,128)(2,1)S(1)}, bf16[16,24,4096]{2,1,0:T(8,128)(2,1)S(1)}) fusion(f32[16,4096]{1,0:T(8,128)S(1)} %get-tuple-element.19, f32[24,4096]{1,0:T(8,128)S(1)} %get-tuple-element.17, f32[16,4096]{1,0:T(8,128)S(1)} %get-tuple-element.18, f32[24,4096]{1,0:T(8,128)S(1)} %get-tuple-element.16), kind=kLoop, calls=%fused_computation.5 | loop fusion | flops 12582912 | bytes 7602176 | tf_op jit(solution)/shard_map/convert
  64.5 3.5 %fusion.3 = f32[64,24]{0,1:T(8,128)S(1)} fusion(bf16[4,64,8192,1]{2,1,3,0:T(8,128)(2,1)S(1)} %bitcast.22, bf16[16,24,4096]{2,1,0:T(8,128)(2,1)S(1)} %get-tuple-element.7, bf16[16,24,4096]{2,1,0:T(8,128)(2,1)S(1)} %get-tuple-element.6), kind=kOutput, calls=%fused_computation.7 | convolution fusion | flops 1623292416 | bytes 10491904 | tf_op jit(solution)/shard_map/dot_general | solution.py:161
  68.1 0.7 reshape.146
  68.8 5.9 %all-to-all-start.2 = ((f32[8,1,192]{2,1,0:T(1,128)}), f32[8,1,192]{2,1,0:T(1,128)S(1)}, u32[]{:S(2)}, u32[]{:S(2)}) async-start(f32[8,1,192]{2,1,0:T(1,128)} %reshape.146), calls=%async_computation.2 | async-start | bytes 16384 | tf_op jit(solution)/shard_map/all_to_all | solution.py:165
  74.6 7.7 %all-to-all-done.2 = f32[8,1,192]{2,1,0:T(1,128)S(1)} async-done(((f32[8,1,192]{2,1,0:T(1,128)}), f32[8,1,192]{2,1,0:T(1,128)S(1)}, u32[]{:S(2)}, u32[]{:S(2)}) %all-to-all-start.2) | async-done | bytes 6176 | tf_op jit(solution)/shard_map/all_to_all | solution.py:165
  82.3 0.5 broadcast.277
  82.9 0.7 reduce.1
  83.6 0.7 all_to_all.22
  84.3 0.7 dynamic-slice_select_fusion
  (28 shorter events, 0.8 us)
Async XLA Ops:
  7.5 9.4 %copy-start = (bf16[64,8192]{1,0:T(8,128)(2,1)S(1)}, bf16[64,8192]{1,0:T(8,128)(2,1)}, u32[]{:S(2)}) copy-start(bf16[64,8192]{1,0:T(8,128)(2,1)} %get-tuple-element.5) | copy-start | bytes 3145732
  7.5 25.2 %all-to-all-start = ((f32[32,24,320]{2,1,0:T(8,128)}), f32[32,24,320]{2,1,0:T(8,128)S(1)}, u32[]{:S(2)}, u32[]{:S(2)}) async-start(f32[32,24,320]{2,1,0:T(8,128)} %get-tuple-element.4), calls=%async_computation | async-start | bytes 2359296 | tf_op jit(solution)/shard_map/all_to_all | solution.py:123
  34.0 19.9 %all-to-all-start.1 = ((f32[32,24,256]{2,1,0:T(8,128)}), f32[32,24,256]{2,1,0:T(8,128)S(1)}, u32[]{:S(2)}, u32[]{:S(2)}) async-start(f32[32,24,256]{2,1,0:T(8,128)} %broadcast_in_dim.74), calls=%async_computation.1 | async-start | bytes 1572864 | tf_op jit(solution)/shard_map/all_to_all | solution.py:128
  54.4 10.1 %copy-start.1 = (bf16[256,8192]{1,0:T(8,128)(2,1)S(1)}, bf16[256,8192]{1,0:T(8,128)(2,1)}, u32[]{:S(2)}) copy-start(bf16[256,8192]{1,0:T(8,128)(2,1)} %maximum_maximum_fusion) | copy-start | bytes 12582916
  54.4 29.9 %collective-permute-start = (bf16[6,8192]{1,0:T(8,128)(2,1)S(1)}, bf16[6,8192]{1,0:T(8,128)(2,1)S(1)}, u32[]{:S(2)}, u32[]{:S(2)}) collective-permute-start(bf16[6,8192]{1,0:T(8,128)(2,1)S(1)} %constant_dynamic-slice_fusion), channel_id=1, source_target_pairs={{0,1},{8,2},{16,3},{24,4},{32,5},{40,6},{48,7},{56,9},{64,10},{72,... | collective-permute-start | bytes 294920 | tf_op jit(solution)/shard_map/ppermute | solution.py:146
  68.8 13.6 %all-to-all-start.2 = ((f32[8,1,192]{2,1,0:T(1,128)}), f32[8,1,192]{2,1,0:T(1,128)S(1)}, u32[]{:S(2)}, u32[]{:S(2)}) async-start(f32[8,1,192]{2,1,0:T(1,128)} %reshape.146), calls=%async_computation.2 | async-start | bytes 16384 | tf_op jit(solution)/shard_map/all_to_all | solution.py:165

commit v10 on v9

--- a/solution.py
+++ b/solution.py
@@ -32,11 +32,10 @@
 def prologue_kernel(
     x_ref, cos_ref, sin_ref, group_ref, table_ref, assign_ref, pay_ref, mod_ref, w_ref, ctf_ref
 ):
-    groups = table_ref.shape[0]
     count = x_ref.shape[0]
     block = pay_ref.shape[1]
-    onehot = group_ref[...] == lax.broadcasted_iota(jnp.int32, (count, groups), 1)
-    ctf_ref[...] = split_dot(onehot.astype(jnp.bfloat16), table_ref[...])
+    for p in range(count):
+        ctf_ref[pl.ds(p, 1), :] = table_ref[pl.ds(group_ref[p], 1), :]
     first_class = lax.axis_index("rot") * block
     classes = first_class + lax.broadcasted_iota(jnp.int32, (block, count), 0)
     member = (classes == assign_ref[...]).astype(jnp.bfloat16)
@@ -68,12 +67,14 @@
 def derotate_and_sum(particles, rotation, group, ctf_table, assign, block, chunks, total):
     angle = column_angles(rotation, total, 2 * MFREQ)
     count = particles.shape[0]
+    vmem = pl.BlockSpec(memory_space=pltpu.VMEM)
     return pl.pallas_call(
         prologue_kernel,
         out_shape=(
             jax.ShapeDtypeStruct((chunks, block, K // chunks + CYCLES), jnp.float32),
             jax.ShapeDtypeStruct((count, K), jnp.bfloat16),
         ),
+        in_specs=[vmem, vmem, vmem, pl.BlockSpec(memory_space=pltpu.SMEM), vmem, vmem],
         scratch_shapes=[
             pltpu.VMEM((count, K), jnp.float32),
             pltpu.VMEM((count, ctf_table.shape[1]), jnp.float32),
@@ -82,7 +83,7 @@
         particles,
         jnp.cos(angle),
         jnp.sin(angle),
-        group.reshape(count, 1),
+        group,
         ctf_table,
         assign.reshape(1, count),
     )

time: 85.8 us -> 84.2 us (0.981)
  local copies, waits for them, and re-layouts: 4.7 us -> 3.34 us
    reshape x1 -> x0, local copies, waits for them, and re-layouts: 1.36 us -> none  [derotate_and_sum(): group.reshape(count, 1)]
where the time goes in v10:
time: 84.2 us; the launch traced here: 83.4 us
  starting transfers between devices  28.4 us (34%)
  other arithmetic  23.1 us (27%)
  waiting for transfers between devices  20.5 us (24%)
  Pallas kernels  3.71 us (4%)
  matrix products  3.47 us (4%)
  local copies, waits for them, and re-layouts  3.34 us (4%)
  between operations  0.9 us (1%)
    concatenate x1, other arithmetic, local(): stacked = jnp.concatenate(variants, axis=0)  14.6 us
    all_to_all x1, waiting for transfers between devices, local(): lax.all_to_all(jnp.broadcast_to(plain_chunk[None], (chunks, block, width)...  12.1 us
    ppermute x1, starting transfers between devices, local(): got = lax.ppermute(sent, ('dom', 'rot'), pairs)  7.99 us
    all_to_all x1, starting transfers between devices, local(): summed = jnp.sum(lax.all_to_all(payload, 'dom', 0, 0, tiled=True), axis=0)  7.75 us
    all_to_all x1, waiting for transfers between devices, local(): best_scores = lax.all_to_all(best, 'rot', 0, 1, tiled=True)  7.73 us
    all_to_all x1, starting transfers between devices, local(): lax.all_to_all(jnp.broadcast_to(plain_chunk[None], (chunks, block, width)...  6.75 us
    all_to_all x1, starting transfers between devices, local(): best_scores = lax.all_to_all(best, 'rot', 0, 1, tiled=True)  5.86 us
    pallas_call x1, Pallas kernels, derotate_and_sum(): pl.pallas_call(prologue_kernel, out_shape=(jax.ShapeDtypeStruct((chunks,...  3.71 us
  transfers between devices with their start and end apart: 4, of which 3 were waited for; matrix products, arithmetic and copies ran while one was open for 30% of the time, Pallas kernels for 0%

profile of v10, /device:TPU:2, one launch (start us, length us, event | category | flops | bytes accessed | tf_op | source)
XLA Modules:
  0.0 83.4 jit_solution(3055423868828102727)
XLA Ops:
  0.7 1.5 %fusion.13 = (f32[64,128]{1,0:T(8,128)}, f32[64,128]{1,0:T(8,128)}) fusion(s32[64]{0:T(128)} %param.7, s32[128]{0:T(128)S(1)} %get-tuple-element.22, s32[128]{0:T(128)S(1)} %get-tuple-element.23, pred[128]{0:T(512)(128)(4,1)S(1)} %compare_and_fusion), kind=kLoop, calls=%fused_computation.42 | loop fusion | flops 122880 | bytes 66944 | tf_op jit(solution)/shard_map/sin | solution.py:85
  2.1 3.7 %shard_map.68 = (f32[32,24,320]{2,1,0:T(8,128)}, bf16[64,8192]{1,0:T(8,128)(2,1)}) custom-call(bf16[64,8192]{1,0:T(8,128)(2,1)} %x_ref.1, f32[64,128]{1,0:T(8,128)} %get-tuple-element.21.cos_ref, f32[64,128]{1,0:T(8,128)} %get-tuple-element.20.sin_ref, s32[64]{0:T(128)} %group_ref.1, f32[32,64]{1,0:T(8,128)} %table_ref.1, s32[1,64]{1,0:T(1,128)} %bitcast.25), custom_call_target="tpu_custom_call" | custom-call | tf_op jit(solution)/shard_map/pallas_call | solution.py:71
  5.9 7.8 %all-to-all-start = ((f32[32,24,320]{2,1,0:T(8,128)}), f32[32,24,320]{2,1,0:T(8,128)S(1)}, u32[]{:S(2)}, u32[]{:S(2)}) async-start(f32[32,24,320]{2,1,0:T(8,128)} %get-tuple-element.4), calls=%async_computation | async-start | bytes 2359296 | tf_op jit(solution)/shard_map/all_to_all | solution.py:124
  13.8 1.4 %select_select_fusion.1 = (bf16[64,4096]{1,0:T(8,128)(2,1)S(1)}, bf16[64,4096]{1,0:T(8,128)(2,1)S(1)}) fusion(pred[4096]{0:T(1024)(128)(4,1)S(1)} %get-tuple-element.24, pred[4096]{0:T(1024)(128)(4,1)S(1)} %get-tuple-element.25, pred[4096]{0:T(1024)(128)(4,1)S(1)} %broadcast_compare_fusion.8, bf16[64,8192]{1,0:T(8,128)(2,1)} %get-tuple-element.5), kind=kLoop, calls=%fused_computation.12 | loop fusion | flops 2097152 | bytes 2109440 | tf_op jit(solution)/shard_map/jit(_where)/select_n | solution.py:157
  15.3 0.5 select_select_fusion.5
  15.8 14.6 %maximum_maximum_fusion = bf16[256,8192]{1,0:T(8,128)(2,1)} fusion(bf16[64,4096]{1,0:T(8,128)(2,1)S(1)} %get-tuple-element.13, bf16[64,4096]{1,0:T(8,128)(2,1)S(1)} %get-tuple-element.12, bf16[64,4096]{1,0:T(8,128)(2,1)S(1)} %get-tuple-element.14, bf16[64,4096]{1,0:T(8,128)(2,1)S(1)} %get-tuple-element.15, bf16[64,4096]{1,0:T(8,128)(2,1)S(1)} %get-tuple-element.9, ...), kind=kLoop, calls=%fused_computation.6 | loop fusion | flops 29360128 | bytes 8388608 | tf_op jit(solution)/shard_map/concatenate | solution.py:160
  30.4 0.6 all-to-all-done
  31.3 0.1 div.38
  31.4 0.9 %broadcast_in_dim.74 = f32[32,24,256]{2,1,0:T(8,128)} broadcast(f32[24,256]{1,0:T(8,128)S(1)} %slice_divide_fusion), dimensions={1,2} | broadcast | bytes 811008 | tf_op jit(solution)/shard_map/broadcast_in_dim | solution.py:130
  32.3 6.8 %all-to-all-start.1 = ((f32[32,24,256]{2,1,0:T(8,128)}), f32[32,24,256]{2,1,0:T(8,128)S(1)}, u32[]{:S(2)}, u32[]{:S(2)}) async-start(f32[32,24,256]{2,1,0:T(8,128)} %broadcast_in_dim.74), calls=%async_computation.1 | async-start | bytes 1572864 | tf_op jit(solution)/shard_map/all_to_all | solution.py:129
  39.1 1.0 %fusion.9 = (f32[16,4096]{1,0:T(8,128)S(1)}, f32[16,4096]{1,0:T(8,128)S(1)}) fusion(s32[4096]{0:T(1024)S(1)} %get-tuple-element.32, s32[4096]{0:T(1024)S(1)} %get-tuple-element.33, pred[4096]{0:T(1024)(128)(4,1)S(1)} %fusion.22), kind=kLoop, calls=%fused_computation.24 | loop fusion | flops 983040 | bytes 561152 | tf_op jit(solution)/shard_map/cos | solution.py:98
  40.1 12.1 %all-to-all-done.1 = f32[32,24,256]{2,1,0:T(8,128)S(1)} async-done(((f32[32,24,256]{2,1,0:T(8,128)}), f32[32,24,256]{2,1,0:T(8,128)S(1)}, u32[]{:S(2)}, u32[]{:S(2)}) %all-to-all-start.1) | async-done | bytes 786464 | tf_op jit(solution)/shard_map/all_to_all | solution.py:129
  52.3 0.2 fusion.4
  52.5 0.1 divide_convert_fusion
  52.8 8.0 %collective-permute-start = (bf16[6,8192]{1,0:T(8,128)(2,1)S(1)}, bf16[6,8192]{1,0:T(8,128)(2,1)S(1)}, u32[]{:S(2)}, u32[]{:S(2)}) collective-permute-start(bf16[6,8192]{1,0:T(8,128)(2,1)S(1)} %constant_dynamic-slice_fusion), channel_id=1, source_target_pairs={{0,1},{8,2},{16,3},{24,4},{32,5},{40,6},{48,7},{56,9},{64,10},{72,... | collective-permute-start | bytes 294920 | tf_op jit(solution)/shard_map/ppermute | solution.py:147
  60.8 2.0 %subtract_convert_fusion = (bf16[16,24,4096]{2,1,0:T(8,128)(2,1)S(1)}, bf16[16,24,4096]{2,1,0:T(8,128)(2,1)S(1)}) fusion(f32[16,4096]{1,0:T(8,128)S(1)} %get-tuple-element.19, f32[24,4096]{1,0:T(8,128)S(1)} %get-tuple-element.17, f32[16,4096]{1,0:T(8,128)S(1)} %get-tuple-element.18, f32[24,4096]{1,0:T(8,128)S(1)} %get-tuple-element.16), kind=kLoop, calls=%fused_computation.5 | loop fusion | flops 12582912 | bytes 7602176 | tf_op jit(solution)/shard_map/convert
  62.9 3.5 %fusion.3 = f32[64,24]{0,1:T(8,128)S(1)} fusion(bf16[4,64,8192,1]{2,1,3,0:T(8,128)(2,1)S(1)} %bitcast.21, bf16[16,24,4096]{2,1,0:T(8,128)(2,1)S(1)} %get-tuple-element.7, bf16[16,24,4096]{2,1,0:T(8,128)(2,1)S(1)} %get-tuple-element.6), kind=kOutput, calls=%fused_computation.7 | convolution fusion | flops 1623292416 | bytes 10491904 | tf_op jit(solution)/shard_map/dot_general | solution.py:162
  66.4 0.7 reshape.142
  67.1 5.9 %all-to-all-start.2 = ((f32[8,1,192]{2,1,0:T(1,128)}), f32[8,1,192]{2,1,0:T(1,128)S(1)}, u32[]{:S(2)}, u32[]{:S(2)}) async-start(f32[8,1,192]{2,1,0:T(1,128)} %reshape.142), calls=%async_computation.2 | async-start | bytes 16384 | tf_op jit(solution)/shard_map/all_to_all | solution.py:166
  73.0 7.7 %all-to-all-done.2 = f32[8,1,192]{2,1,0:T(1,128)S(1)} async-done(((f32[8,1,192]{2,1,0:T(1,128)}), f32[8,1,192]{2,1,0:T(1,128)S(1)}, u32[]{:S(2)}, u32[]{:S(2)}) %all-to-all-start.2) | async-done | bytes 6176 | tf_op jit(solution)/shard_map/all_to_all | solution.py:166
  80.7 0.5 broadcast.277
  81.2 0.7 reduce.1
  82.0 0.7 all_to_all.22
  82.7 0.7 dynamic-slice_select_fusion
  (27 shorter events, 0.7 us)
Async XLA Ops:
  5.9 9.4 %copy-start = (bf16[64,8192]{1,0:T(8,128)(2,1)S(1)}, bf16[64,8192]{1,0:T(8,128)(2,1)}, u32[]{:S(2)}) copy-start(bf16[64,8192]{1,0:T(8,128)(2,1)} %get-tuple-element.5) | copy-start | bytes 3145732
  5.9 25.2 %all-to-all-start = ((f32[32,24,320]{2,1,0:T(8,128)}), f32[32,24,320]{2,1,0:T(8,128)S(1)}, u32[]{:S(2)}, u32[]{:S(2)}) async-start(f32[32,24,320]{2,1,0:T(8,128)} %get-tuple-element.4), calls=%async_computation | async-start | bytes 2359296 | tf_op jit(solution)/shard_map/all_to_all | solution.py:124
  32.3 19.9 %all-to-all-start.1 = ((f32[32,24,256]{2,1,0:T(8,128)}), f32[32,24,256]{2,1,0:T(8,128)S(1)}, u32[]{:S(2)}, u32[]{:S(2)}) async-start(f32[32,24,256]{2,1,0:T(8,128)} %broadcast_in_dim.74), calls=%async_computation.1 | async-start | bytes 1572864 | tf_op jit(solution)/shard_map/all_to_all | solution.py:129
  52.7 10.1 %copy-start.1 = (bf16[256,8192]{1,0:T(8,128)(2,1)S(1)}, bf16[256,8192]{1,0:T(8,128)(2,1)}, u32[]{:S(2)}) copy-start(bf16[256,8192]{1,0:T(8,128)(2,1)} %maximum_maximum_fusion) | copy-start | bytes 12582916
  52.8 29.9 %collective-permute-start = (bf16[6,8192]{1,0:T(8,128)(2,1)S(1)}, bf16[6,8192]{1,0:T(8,128)(2,1)S(1)}, u32[]{:S(2)}, u32[]{:S(2)}) collective-permute-start(bf16[6,8192]{1,0:T(8,128)(2,1)S(1)} %constant_dynamic-slice_fusion), channel_id=1, source_target_pairs={{0,1},{8,2},{16,3},{24,4},{32,5},{40,6},{48,7},{56,9},{64,10},{72,... | collective-permute-start | bytes 294920 | tf_op jit(solution)/shard_map/ppermute | solution.py:147
  67.1 13.6 %all-to-all-start.2 = ((f32[8,1,192]{2,1,0:T(1,128)}), f32[8,1,192]{2,1,0:T(1,128)S(1)}, u32[]{:S(2)}, u32[]{:S(2)}) async-start(f32[8,1,192]{2,1,0:T(1,128)} %reshape.142), calls=%async_computation.2 | async-start | bytes 16384 | tf_op jit(solution)/shard_map/all_to_all | solution.py:166

commit v11 on v10

--- a/solution.py
+++ b/solution.py
@@ -1,6 +1,7 @@
 import math
 
 import jax
+import numpy as np
 import jax.numpy as jnp
 from jax import lax
 from jax.experimental import pallas as pl
@@ -30,12 +31,15 @@
 
 
 def prologue_kernel(
-    x_ref, cos_ref, sin_ref, group_ref, table_ref, assign_ref, pay_ref, mod_ref, w_ref, ctf_ref
+    x_ref, cos_ref, sin_ref, rot_ref, group_ref, table_ref, assign_ref,
+    pay_ref, mod_ref, w_ref, ctf_ref, cos_scr, sin_scr,
 ):
     count = x_ref.shape[0]
     block = pay_ref.shape[1]
     for p in range(count):
         ctf_ref[pl.ds(p, 1), :] = table_ref[pl.ds(group_ref[p], 1), :]
+        cos_scr[pl.ds(p, 1), :] = cos_ref[pl.ds(rot_ref[p], 1), :]
+        sin_scr[pl.ds(p, 1), :] = sin_ref[pl.ds(rot_ref[p], 1), :]
     first_class = lax.axis_index("rot") * block
     classes = first_class + lax.broadcasted_iota(jnp.int32, (block, count), 0)
     member = (classes == assign_ref[...]).astype(jnp.bfloat16)
@@ -43,8 +47,8 @@
     lanes = cos_ref.shape[1]
     chunks, _, width = pay_ref.shape
     width -= ctf_ref.shape[1]
-    cosine = cos_ref[...]
-    sine = sin_ref[...]
+    cosine = cos_scr[...]
+    sine = sin_scr[...]
     low = lax.broadcasted_iota(jnp.int32, cosine.shape, 1) < MFREQ
     for j in range(half // lanes):
         gain = jnp.where(low, ctf_ref[:, 2 * j : 2 * j + 1], ctf_ref[:, 2 * j + 1 : 2 * j + 2])
@@ -65,8 +69,10 @@
 
 
 def derotate_and_sum(particles, rotation, group, ctf_table, assign, block, chunks, total):
-    angle = column_angles(rotation, total, 2 * MFREQ)
+    phase = (np.arange(2 * MFREQ)[None, :] % MFREQ) * np.arange(total)[:, None] % total
+    angle = phase.astype(np.float32) * np.float32(2.0 * math.pi / total)
     count = particles.shape[0]
+    smem = pl.BlockSpec(memory_space=pltpu.SMEM)
     vmem = pl.BlockSpec(memory_space=pltpu.VMEM)
     return pl.pallas_call(
         prologue_kernel,
@@ -74,15 +80,18 @@
             jax.ShapeDtypeStruct((chunks, block, K // chunks + CYCLES), jnp.float32),
             jax.ShapeDtypeStruct((count, K), jnp.bfloat16),
         ),
-        in_specs=[vmem, vmem, vmem, pl.BlockSpec(memory_space=pltpu.SMEM), vmem, vmem],
+        in_specs=[vmem, vmem, vmem, smem, smem, vmem, vmem],
         scratch_shapes=[
             pltpu.VMEM((count, K), jnp.float32),
             pltpu.VMEM((count, ctf_table.shape[1]), jnp.float32),
+            pltpu.VMEM((count, 2 * MFREQ), jnp.float32),
+            pltpu.VMEM((count, 2 * MFREQ), jnp.float32),
         ],
     )(
         particles,
-        jnp.cos(angle),
-        jnp.sin(angle),
+        jnp.asarray(np.cos(angle)),
+        jnp.asarray(np.sin(angle)),
+        rotation,
         group,
         ctf_table,
         assign.reshape(1, count),

time: 84.2 us -> 82.7 us (0.982)
  other arithmetic: 23.1 us -> 21.6 us
    sin x1 -> x0, other arithmetic: 1.5 us -> none  [derotate_and_sum(): jnp.sin(angle)]
  transfers between devices with their start and end apart: 4 -> 4, of which waited for: 3 -> 3; matrix products, arithmetic and copies ran while one was open for 30% -> 31% of each run, Pallas kernels for 0% -> 0%
where the time goes in v11:
time: 82.7 us; the launch traced here: 81.9 us
  starting transfers between devices  28.4 us (34%)
  other arithmetic  21.6 us (26%)
  waiting for transfers between devices  20.5 us (25%)
  Pallas kernels  3.75 us (5%)
  matrix products  3.47 us (4%)
  local copies, waits for them, and re-layouts  3.35 us (4%)
  between operations  0.89 us (1%)
    concatenate x1, other arithmetic, local(): stacked = jnp.concatenate(variants, axis=0)  14.6 us
    all_to_all x1, waiting for transfers between devices, local(): lax.all_to_all(jnp.broadcast_to(plain_chunk[None], (chunks, block, width)...  12.1 us
    ppermute x1, starting transfers between devices, local(): got = lax.ppermute(sent, ('dom', 'rot'), pairs)  7.99 us
    all_to_all x1, starting transfers between devices, local(): summed = jnp.sum(lax.all_to_all(payload, 'dom', 0, 0, tiled=True), axis=0)  7.75 us
    all_to_all x1, waiting for transfers between devices, local(): best_scores = lax.all_to_all(best, 'rot', 0, 1, tiled=True)  7.73 us
    all_to_all x1, starting transfers between devices, local(): lax.all_to_all(jnp.broadcast_to(plain_chunk[None], (chunks, block, width)...  6.77 us
    all_to_all x1, starting transfers between devices, local(): best_scores = lax.all_to_all(best, 'rot', 0, 1, tiled=True)  5.85 us
    pallas_call x1, Pallas kernels, derotate_and_sum(): pl.pallas_call(prologue_kernel, out_shape=(jax.ShapeDtypeStruct((chunks,...  3.75 us
  transfers between devices with their start and end apart: 4, of which 3 were waited for; matrix products, arithmetic and copies ran while one was open for 31% of the time, Pallas kernels for 0%

profile of v11, /device:TPU:2, one launch (start us, length us, event | category | flops | bytes accessed | tf_op | source)
XLA Modules:
  0.0 81.9 jit_solution(11547756414028813019)
XLA Ops:
  0.6 3.7 %shard_map.86 = (f32[32,24,320]{2,1,0:T(8,128)}, bf16[64,8192]{1,0:T(8,128)(2,1)}) custom-call(bf16[64,8192]{1,0:T(8,128)(2,1)} %x_ref.1, f32[64,128]{1,0:T(8,128)} %constant.127.clone.cos_ref, f32[64,128]{1,0:T(8,128)} %constant.128.clone.sin_ref, s32[64]{0:T(128)} %rot_ref.1, s32[64]{0:T(128)} %group_ref.1, f32[32,64]{1,0:T(8,128)} %table_ref.1, ...), custom_call_target="tpu_custom_call" | custom-call | tf_op jit(solution)/shard_map/pallas_call | solution.py:77
  4.4 7.7 %all-to-all-start = ((f32[32,24,320]{2,1,0:T(8,128)}), f32[32,24,320]{2,1,0:T(8,128)S(1)}, u32[]{:S(2)}, u32[]{:S(2)}) async-start(f32[32,24,320]{2,1,0:T(8,128)} %get-tuple-element.4), calls=%async_computation | async-start | bytes 2359296 | tf_op jit(solution)/shard_map/all_to_all | solution.py:133
  12.4 1.4 %select_select_fusion.1 = (bf16[64,4096]{1,0:T(8,128)(2,1)S(1)}, bf16[64,4096]{1,0:T(8,128)(2,1)S(1)}) fusion(pred[4096]{0:T(1024)(128)(4,1)S(1)} %get-tuple-element.20, pred[4096]{0:T(1024)(128)(4,1)S(1)} %get-tuple-element.21, pred[4096]{0:T(1024)(128)(4,1)S(1)} %broadcast_compare_fusion.8, bf16[64,8192]{1,0:T(8,128)(2,1)} %get-tuple-element.5), kind=kLoop, calls=%fused_computation.12 | loop fusion | flops 2097152 | bytes 2109440 | tf_op jit(solution)/shard_map/jit(_where)/select_n | solution.py:166
  13.8 0.5 select_select_fusion.5
  14.3 14.6 %maximum_maximum_fusion = bf16[256,8192]{1,0:T(8,128)(2,1)} fusion(bf16[64,4096]{1,0:T(8,128)(2,1)S(1)} %get-tuple-element.13, bf16[64,4096]{1,0:T(8,128)(2,1)S(1)} %get-tuple-element.12, bf16[64,4096]{1,0:T(8,128)(2,1)S(1)} %get-tuple-element.14, bf16[64,4096]{1,0:T(8,128)(2,1)S(1)} %get-tuple-element.15, bf16[64,4096]{1,0:T(8,128)(2,1)S(1)} %get-tuple-element.9, ...), kind=kLoop, calls=%fused_computation.6 | loop fusion | flops 29360128 | bytes 8388608 | tf_op jit(solution)/shard_map/concatenate | solution.py:169
  28.9 0.6 all-to-all-done
  29.5 0.1 reduce_sum.18
  29.8 0.1 div.38
  29.9 0.9 %broadcast_in_dim.73 = f32[32,24,256]{2,1,0:T(8,128)} broadcast(f32[24,256]{1,0:T(8,128)S(1)} %slice_divide_fusion), dimensions={1,2} | broadcast | bytes 811008 | tf_op jit(solution)/shard_map/broadcast_in_dim | solution.py:139
  30.9 6.8 %all-to-all-start.1 = ((f32[32,24,256]{2,1,0:T(8,128)}), f32[32,24,256]{2,1,0:T(8,128)S(1)}, u32[]{:S(2)}, u32[]{:S(2)}) async-start(f32[32,24,256]{2,1,0:T(8,128)} %broadcast_in_dim.73), calls=%async_computation.1 | async-start | bytes 1572864 | tf_op jit(solution)/shard_map/all_to_all | solution.py:138
  37.6 1.0 %fusion.9 = (f32[16,4096]{1,0:T(8,128)S(1)}, f32[16,4096]{1,0:T(8,128)S(1)}) fusion(s32[4096]{0:T(1024)S(1)} %get-tuple-element.28, s32[4096]{0:T(1024)S(1)} %get-tuple-element.29, pred[4096]{0:T(1024)(128)(4,1)S(1)} %fusion.17), kind=kLoop, calls=%fused_computation.24 | loop fusion | flops 983040 | bytes 561152 | tf_op jit(solution)/shard_map/cos | solution.py:107
  38.7 12.1 %all-to-all-done.1 = f32[32,24,256]{2,1,0:T(8,128)S(1)} async-done(((f32[32,24,256]{2,1,0:T(8,128)}), f32[32,24,256]{2,1,0:T(8,128)S(1)}, u32[]{:S(2)}, u32[]{:S(2)}) %all-to-all-start.1) | async-done | bytes 786464 | tf_op jit(solution)/shard_map/all_to_all | solution.py:138
  50.9 0.2 fusion.4
  51.1 0.1 divide_convert_fusion
  51.4 8.0 %collective-permute-start = (bf16[6,8192]{1,0:T(8,128)(2,1)S(1)}, bf16[6,8192]{1,0:T(8,128)(2,1)S(1)}, u32[]{:S(2)}, u32[]{:S(2)}) collective-permute-start(bf16[6,8192]{1,0:T(8,128)(2,1)S(1)} %constant_dynamic-slice_fusion), channel_id=1, source_target_pairs={{0,1},{8,2},{16,3},{24,4},{32,5},{40,6},{48,7},{56,9},{64,10},{72,... | collective-permute-start | bytes 294920 | tf_op jit(solution)/shard_map/ppermute | solution.py:156
  59.4 2.0 %subtract_convert_fusion = (bf16[16,24,4096]{2,1,0:T(8,128)(2,1)S(1)}, bf16[16,24,4096]{2,1,0:T(8,128)(2,1)S(1)}) fusion(f32[16,4096]{1,0:T(8,128)S(1)} %get-tuple-element.19, f32[24,4096]{1,0:T(8,128)S(1)} %get-tuple-element.17, f32[16,4096]{1,0:T(8,128)S(1)} %get-tuple-element.18, f32[24,4096]{1,0:T(8,128)S(1)} %get-tuple-element.16), kind=kLoop, calls=%fused_computation.5 | loop fusion | flops 12582912 | bytes 7602176 | tf_op jit(solution)/shard_map/convert
  61.4 3.5 %fusion.3 = f32[64,24]{0,1:T(8,128)S(1)} fusion(bf16[4,64,8192,1]{2,1,3,0:T(8,128)(2,1)S(1)} %bitcast.21, bf16[16,24,4096]{2,1,0:T(8,128)(2,1)S(1)} %get-tuple-element.7, bf16[16,24,4096]{2,1,0:T(8,128)(2,1)S(1)} %get-tuple-element.6), kind=kOutput, calls=%fused_computation.7 | convolution fusion | flops 1623292416 | bytes 10491904 | tf_op jit(solution)/shard_map/dot_general | solution.py:171
  65.0 0.7 reshape.141
  65.7 5.9 %all-to-all-start.2 = ((f32[8,1,192]{2,1,0:T(1,128)}), f32[8,1,192]{2,1,0:T(1,128)S(1)}, u32[]{:S(2)}, u32[]{:S(2)}) async-start(f32[8,1,192]{2,1,0:T(1,128)} %reshape.141), calls=%async_computation.2 | async-start | bytes 16384 | tf_op jit(solution)/shard_map/all_to_all | solution.py:175
  71.5 7.7 %all-to-all-done.2 = f32[8,1,192]{2,1,0:T(1,128)S(1)} async-done(((f32[8,1,192]{2,1,0:T(1,128)}), f32[8,1,192]{2,1,0:T(1,128)S(1)}, u32[]{:S(2)}, u32[]{:S(2)}) %all-to-all-start.2) | async-done | bytes 6176 | tf_op jit(solution)/shard_map/all_to_all | solution.py:175
  79.3 0.5 broadcast.254
  79.8 0.7 reduce.1
  80.5 0.7 all_to_all.22
  81.2 0.7 dynamic-slice_select_fusion
  (24 shorter events, 0.6 us)
Async XLA Ops:
  4.4 9.4 %copy-start = (bf16[64,8192]{1,0:T(8,128)(2,1)S(1)}, bf16[64,8192]{1,0:T(8,128)(2,1)}, u32[]{:S(2)}) copy-start(bf16[64,8192]{1,0:T(8,128)(2,1)} %get-tuple-element.5) | copy-start | bytes 3145732
  4.4 25.2 %all-to-all-start = ((f32[32,24,320]{2,1,0:T(8,128)}), f32[32,24,320]{2,1,0:T(8,128)S(1)}, u32[]{:S(2)}, u32[]{:S(2)}) async-start(f32[32,24,320]{2,1,0:T(8,128)} %get-tuple-element.4), calls=%async_computation | async-start | bytes 2359296 | tf_op jit(solution)/shard_map/all_to_all | solution.py:133
  30.9 20.0 %all-to-all-start.1 = ((f32[32,24,256]{2,1,0:T(8,128)}), f32[32,24,256]{2,1,0:T(8,128)S(1)}, u32[]{:S(2)}, u32[]{:S(2)}) async-start(f32[32,24,256]{2,1,0:T(8,128)} %broadcast_in_dim.73), calls=%async_computation.1 | async-start | bytes 1572864 | tf_op jit(solution)/shard_map/all_to_all | solution.py:138
  51.3 10.1 %copy-start.1 = (bf16[256,8192]{1,0:T(8,128)(2,1)S(1)}, bf16[256,8192]{1,0:T(8,128)(2,1)}, u32[]{:S(2)}) copy-start(bf16[256,8192]{1,0:T(8,128)(2,1)} %maximum_maximum_fusion) | copy-start | bytes 12582916
  51.4 29.9 %collective-permute-start = (bf16[6,8192]{1,0:T(8,128)(2,1)S(1)}, bf16[6,8192]{1,0:T(8,128)(2,1)S(1)}, u32[]{:S(2)}, u32[]{:S(2)}) collective-permute-start(bf16[6,8192]{1,0:T(8,128)(2,1)S(1)} %constant_dynamic-slice_fusion), channel_id=1, source_target_pairs={{0,1},{8,2},{16,3},{24,4},{32,5},{40,6},{48,7},{56,9},{64,10},{72,... | collective-permute-start | bytes 294920 | tf_op jit(solution)/shard_map/ppermute | solution.py:156
  65.7 13.6 %all-to-all-start.2 = ((f32[8,1,192]{2,1,0:T(1,128)}), f32[8,1,192]{2,1,0:T(1,128)S(1)}, u32[]{:S(2)}, u32[]{:S(2)}) async-start(f32[8,1,192]{2,1,0:T(1,128)} %reshape.141), calls=%async_computation.2 | async-start | bytes 16384 | tf_op jit(solution)/shard_map/all_to_all | solution.py:175

commit v12 on v11

--- a/solution.py
+++ b/solution.py
@@ -12,12 +12,6 @@
 MFREQ = 64
 CLS_DEV = 6
 K = 8192
-
-
-def column_angles(index, total, width):
-    freqs = lax.broadcasted_iota(jnp.int32, (index.shape[0], width), 1) % MFREQ
-    phase = freqs * index[:, None] % total
-    return phase.astype(jnp.float32) * (2.0 * math.pi / total)
 
 
 def split_dot(member, value):
@@ -103,9 +97,10 @@
     half = K // 2
     real_part = refs[None, :, :half]
     imag_part = refs[None, :, half:]
-    angle = column_angles(jnp.arange(turns, dtype=jnp.int32), total, half)
-    cosine = jnp.cos(angle)[:, None, :]
-    sine = jnp.sin(angle)[:, None, :]
+    phase = (np.arange(half)[None, :] % MFREQ) * np.arange(turns)[:, None] % total
+    angle = phase.astype(np.float32) * np.float32(2.0 * math.pi / total)
+    cosine = jnp.asarray(np.cos(angle))[:, None, :]
+    sine = jnp.asarray(np.sin(angle))[:, None, :]
     turned = jnp.concatenate(
         [real_part * cosine - imag_part * sine, real_part * sine + imag_part * cosine], axis=2
     )

time: 82.7 us -> 84 us (1.016); the launches traced: 81.9 us -> 82.4 us
  waiting for transfers between devices: 20.5 us -> 21.7 us
    all_to_all x1, waiting for transfers between devices: 0.61 us -> 13.9 us  [local(): summed = jnp.sum(lax.all_to_all(payload, 'dom', 0, 0, tiled=True), axis=0)]
    all_to_all x1, waiting for transfers between devices: 12.1 us -> 0.01 us  [local(): lax.all_to_all(jnp.broadcast_to(plain_chunk[None], (chunks, block, width)...]
    all_to_all x1, starting transfers between devices: 5.85 us -> 7.82 us  [local(): best_scores = lax.all_to_all(best, 'rot', 0, 1, tiled=True)]
    all_to_all x1, starting transfers between devices: 6.77 us -> 5.1 us  [local(): lax.all_to_all(jnp.broadcast_to(plain_chunk[None], (chunks, block, width)...]
    select_n x2, other arithmetic: 1.97 us -> 3.25 us  [local(): jnp.where(step == 0, real_part, jnp.where(step == 1, imag_part, jnp.where...]
    cos x1 -> x0, other arithmetic: 1.05 us -> none  [rotate_all(): cosine = jnp.cos(angle)[:, None, :]]
  transfers between devices with their start and end apart: 4 -> 4, of which waited for: 3 -> 2; matrix products, arithmetic and copies ran while one was open for 31% -> 30% of each run, Pallas kernels for 0% -> 0%
where the time goes in v12:
time: 84 us; the launch traced here: 82.4 us
  starting transfers between devices  28.1 us (33%)
  waiting for transfers between devices  21.7 us (26%)
  other arithmetic  21.1 us (25%)
  Pallas kernels  3.76 us (4%)
  matrix products  3.47 us (4%)
  local copies, waits for them, and re-layouts  3.36 us (4%)
  between operations  0.89 us (1%)
    all_to_all x1, waiting for transfers between devices, local(): summed = jnp.sum(lax.all_to_all(payload, 'dom', 0, 0, tiled=True), axis=0)  13.9 us
    concatenate x1, other arithmetic, local(): stacked = jnp.concatenate(variants, axis=0)  13.8 us
    all_to_all x1, starting transfers between devices, local(): best_scores = lax.all_to_all(best, 'rot', 0, 1, tiled=True)  7.82 us
    all_to_all x1, starting transfers between devices, local(): summed = jnp.sum(lax.all_to_all(payload, 'dom', 0, 0, tiled=True), axis=0)  7.75 us
    all_to_all x1, waiting for transfers between devices, local(): best_scores = lax.all_to_all(best, 'rot', 0, 1, tiled=True)  7.73 us
    ppermute x1, starting transfers between devices, local(): got = lax.ppermute(sent, ('dom', 'rot'), pairs)  7.43 us
    all_to_all x1, starting transfers between devices, local(): lax.all_to_all(jnp.broadcast_to(plain_chunk[None], (chunks, block, width)...  5.1 us
    pallas_call x1, Pallas kernels, derotate_and_sum(): pl.pallas_call(prologue_kernel, out_shape=(jax.ShapeDtypeStruct((chunks,...  3.76 us
  transfers between devices with their start and end apart: 4, of which 2 were waited for; matrix products, arithmetic and copies ran while one was open for 30% of the time, Pallas kernels for 0%

profile of v12, /device:TPU:2, one launch (start us, length us, event | category | flops | bytes accessed | tf_op | source)
XLA Modules:
  0.0 82.4 jit_solution(8062477981167376010)
XLA Ops:
  0.6 3.8 %shard_map.104 = (f32[32,24,320]{2,1,0:T(8,128)}, bf16[64,8192]{1,0:T(8,128)(2,1)}) custom-call(bf16[64,8192]{1,0:T(8,128)(2,1)} %x_ref.1, f32[64,128]{1,0:T(8,128)} %constant.118.clone.cos_ref, f32[64,128]{1,0:T(8,128)} %constant.119.clone.sin_ref, s32[64]{0:T(128)} %rot_ref.1, s32[64]{0:T(128)} %group_ref.1, f32[32,64]{1,0:T(8,128)} %table_ref.1, ...), custom_call_target="tpu_custom_call" | custom-call | tf_op jit(solution)/shard_map/pallas_call | solution.py:71
  4.4 7.8 %all-to-all-start = ((f32[32,24,320]{2,1,0:T(8,128)}), f32[32,24,320]{2,1,0:T(8,128)S(1)}, u32[]{:S(2)}, u32[]{:S(2)}) async-start(f32[32,24,320]{2,1,0:T(8,128)} %get-tuple-element.4), calls=%async_computation | async-start | bytes 2359296 | tf_op jit(solution)/shard_map/all_to_all | solution.py:128
  12.3 1.4 %select_select_fusion.1 = (bf16[64,4096]{1,0:T(8,128)(2,1)S(1)}, bf16[64,4096]{1,0:T(8,128)(2,1)S(1)}) fusion(pred[4096]{0:T(1024)(128)(4,1)S(1)} %get-tuple-element.18, pred[4096]{0:T(1024)(128)(4,1)S(1)} %get-tuple-element.19, pred[4096]{0:T(1024)(128)(4,1)S(1)} %broadcast_compare_fusion.8, bf16[64,8192]{1,0:T(8,128)(2,1)} %get-tuple-element.5), kind=kLoop, calls=%fused_computation.12 | loop fusion | flops 2097152 | bytes 2109440 | tf_op jit(solution)/shard_map/jit(_where)/select_n | solution.py:161
  13.8 1.8 %select_select_fusion.5 = (bf16[64,4096]{1,0:T(8,128)(2,1)}, bf16[64,4096]{1,0:T(8,128)(2,1)}, bf16[64,4096]{1,0:T(8,128)(2,1)}, bf16[64,4096]{1,0:T(8,128)(2,1)}) fusion(pred[4096]{0:T(1024)(128)(4,1)S(1)} %get-tuple-element.21, pred[4096]{0:T(1024)(128)(4,1)S(1)} %get-tuple-element.23, pred[4096]{0:T(1024)(128)(4,1)S(1)} %get-tuple-element.25, ...), kind=kLoop, calls=%fused_computation.16 | loop fusion | flops 3670016 | bytes 3170304 | tf_op jit(solution)/shard_map/jit(_where)/select_n | solution.py:161
  15.6 13.9 %all-to-all-done = f32[32,24,320]{2,1,0:T(8,128)S(1)} async-done(((f32[32,24,320]{2,1,0:T(8,128)}), f32[32,24,320]{2,1,0:T(8,128)S(1)}, u32[]{:S(2)}, u32[]{:S(2)}) %all-to-all-start) | async-done | bytes 983072 | tf_op jit(solution)/shard_map/all_to_all | solution.py:128
  29.5 0.1 reduce_sum.18
  29.7 0.1 div.37
  29.8 0.1 div.38
  29.9 0.9 %broadcast_in_dim.72 = f32[32,24,256]{2,1,0:T(8,128)} broadcast(f32[24,256]{1,0:T(8,128)S(1)} %slice_divide_fusion), dimensions={1,2} | broadcast | bytes 811008 | tf_op jit(solution)/shard_map/broadcast_in_dim | solution.py:134
  30.9 5.1 %all-to-all-start.1 = ((f32[32,24,256]{2,1,0:T(8,128)}), f32[32,24,256]{2,1,0:T(8,128)S(1)}, u32[]{:S(2)}, u32[]{:S(2)}) async-start(f32[32,24,256]{2,1,0:T(8,128)} %broadcast_in_dim.72), calls=%async_computation.1 | async-start | bytes 1572864 | tf_op jit(solution)/shard_map/all_to_all | solution.py:133
  36.0 13.8 %maximum_maximum_fusion = bf16[256,8192]{1,0:T(8,128)(2,1)} fusion(bf16[64,4096]{1,0:T(8,128)(2,1)S(1)} %get-tuple-element.13, bf16[64,4096]{1,0:T(8,128)(2,1)S(1)} %get-tuple-element.12, bf16[64,4096]{1,0:T(8,128)(2,1)} %get-tuple-element.14, bf16[64,4096]{1,0:T(8,128)(2,1)} %get-tuple-element.15, bf16[64,4096]{1,0:T(8,128)(2,1)} %get-tuple-element.9, ...), kind=kLoop, calls=%fused_computation.6 | loop fusion | flops 29360128 | bytes 8388608 | tf_op jit(solution)/shard_map/concatenate | solution.py:164
  49.9 0.2 fusion.4
  50.1 0.1 divide_convert_fusion
  50.4 7.4 %collective-permute-start = (bf16[6,8192]{1,0:T(8,128)(2,1)S(1)}, bf16[6,8192]{1,0:T(8,128)(2,1)S(1)}, u32[]{:S(2)}, u32[]{:S(2)}) collective-permute-start(bf16[6,8192]{1,0:T(8,128)(2,1)S(1)} %constant_dynamic-slice_fusion), channel_id=1, source_target_pairs={{0,1},{8,2},{16,3},{24,4},{32,5},{40,6},{48,7},{56,9},{64,10},{72,... | collective-permute-start | bytes 294920 | tf_op jit(solution)/shard_map/ppermute | solution.py:151
  57.8 2.0 %subtract_convert_fusion = (bf16[16,24,4096]{2,1,0:T(8,128)(2,1)S(1)}, bf16[16,24,4096]{2,1,0:T(8,128)(2,1)S(1)}) fusion(f32[16,4096]{1,0:T(8,128)S(1)} %copy-done.2, f32[24,4096]{1,0:T(8,128)S(1)} %get-tuple-element.17, f32[16,4096]{1,0:T(8,128)S(1)} %copy-done.3, f32[24,4096]{1,0:T(8,128)S(1)} %get-tuple-element.16), kind=kLoop, calls=%fused_computation.5 | loop fusion | flops 12582912 | bytes 7602176 | tf_op jit(solution)/shard_map/convert
  59.9 3.5 %fusion.3 = f32[64,24]{0,1:T(8,128)S(1)} fusion(bf16[4,64,8192,1]{2,1,3,0:T(8,128)(2,1)S(1)} %bitcast.21, bf16[16,24,4096]{2,1,0:T(8,128)(2,1)S(1)} %get-tuple-element.7, bf16[16,24,4096]{2,1,0:T(8,128)(2,1)S(1)} %get-tuple-element.6), kind=kOutput, calls=%fused_computation.7 | convolution fusion | flops 1623292416 | bytes 10491904 | tf_op jit(solution)/shard_map/dot_general | solution.py:166
  63.4 0.1 copy.15
  63.4 0.7 reshape.55
  64.1 7.8 %all-to-all-start.2 = ((f32[8,1,192]{2,1,0:T(1,128)}), f32[8,1,192]{2,1,0:T(1,128)S(1)}, u32[]{:S(2)}, u32[]{:S(2)}) async-start(f32[8,1,192]{2,1,0:T(1,128)} %reshape.55), calls=%async_computation.2 | async-start | bytes 16384 | tf_op jit(solution)/shard_map/all_to_all | solution.py:170
  72.0 7.7 %all-to-all-done.2 = f32[8,1,192]{2,1,0:T(1,128)S(1)} async-done(((f32[8,1,192]{2,1,0:T(1,128)}), f32[8,1,192]{2,1,0:T(1,128)S(1)}, u32[]{:S(2)}, u32[]{:S(2)}) %all-to-all-start.2) | async-done | bytes 6176 | tf_op jit(solution)/shard_map/all_to_all | solution.py:170
  79.7 0.5 broadcast.147
  80.2 0.7 reduce.1
  81.0 0.7 all_to_all.22
  81.6 0.7 dynamic-slice_select_fusion
  (25 shorter events, 0.5 us)
Async XLA Ops:
  4.4 9.4 %copy-start = (bf16[64,8192]{1,0:T(8,128)(2,1)S(1)}, bf16[64,8192]{1,0:T(8,128)(2,1)}, u32[]{:S(2)}) copy-start(bf16[64,8192]{1,0:T(8,128)(2,1)} %get-tuple-element.5) | copy-start | bytes 3145732
  4.4 25.2 %all-to-all-start = ((f32[32,24,320]{2,1,0:T(8,128)}), f32[32,24,320]{2,1,0:T(8,128)S(1)}, u32[]{:S(2)}, u32[]{:S(2)}) async-start(f32[32,24,320]{2,1,0:T(8,128)} %get-tuple-element.4), calls=%async_computation | async-start | bytes 2359296 | tf_op jit(solution)/shard_map/all_to_all | solution.py:128
  30.9 19.0 %all-to-all-start.1 = ((f32[32,24,256]{2,1,0:T(8,128)}), f32[32,24,256]{2,1,0:T(8,128)S(1)}, u32[]{:S(2)}, u32[]{:S(2)}) async-start(f32[32,24,256]{2,1,0:T(8,128)} %broadcast_in_dim.72), calls=%async_computation.1 | async-start | bytes 1572864 | tf_op jit(solution)/shard_map/all_to_all | solution.py:133
  49.8 8.0 %copy-start.2 = (f32[16,4096]{1,0:T(8,128)S(1)}, f32[16,4096]{1,0:T(8,128)}, u32[]{:S(2)}) copy-start(f32[16,4096]{1,0:T(8,128)} %constant.121.clone) | copy-start | bytes 786436
  49.8 8.0 %copy-start.3 = (f32[16,4096]{1,0:T(8,128)S(1)}, f32[16,4096]{1,0:T(8,128)}, u32[]{:S(2)}) copy-start(f32[16,4096]{1,0:T(8,128)} %constant.120.clone) | copy-start | bytes 786436
  50.3 9.6 %copy-start.1 = (bf16[256,8192]{1,0:T(8,128)(2,1)S(1)}, bf16[256,8192]{1,0:T(8,128)(2,1)}, u32[]{:S(2)}) copy-start(bf16[256,8192]{1,0:T(8,128)(2,1)} %maximum_maximum_fusion) | copy-start | bytes 12582916
  50.4 31.3 %collective-permute-start = (bf16[6,8192]{1,0:T(8,128)(2,1)S(1)}, bf16[6,8192]{1,0:T(8,128)(2,1)S(1)}, u32[]{:S(2)}, u32[]{:S(2)}) collective-permute-start(bf16[6,8192]{1,0:T(8,128)(2,1)S(1)} %constant_dynamic-slice_fusion), channel_id=1, source_target_pairs={{0,1},{8,2},{16,3},{24,4},{32,5},{40,6},{48,7},{56,9},{64,10},{72,... | collective-permute-start | bytes 294920 | tf_op jit(solution)/shard_map/ppermute | solution.py:151
  64.1 15.5 %all-to-all-start.2 = ((f32[8,1,192]{2,1,0:T(1,128)}), f32[8,1,192]{2,1,0:T(1,128)S(1)}, u32[]{:S(2)}, u32[]{:S(2)}) async-start(f32[8,1,192]{2,1,0:T(1,128)} %reshape.55), calls=%async_computation.2 | async-start | bytes 16384 | tf_op jit(solution)/shard_map/all_to_all | solution.py:170

commit v13 on v11

--- a/solution.py
+++ b/solution.py
@@ -153,7 +153,8 @@
     sent = lax.dynamic_slice_in_dim(
         refs_block, jnp.minimum(dom_rank // others, owners_per_block - 1) * CLS_DEV, CLS_DEV, 0
     )
-    got = lax.ppermute(sent, ("dom", "rot"), pairs)
+    flat = (CLS_DEV * 8, K // 8)
+    got = lax.ppermute(sent.reshape(flat), ("dom", "rot"), pairs).reshape(sent.shape)
     mine = lax.dynamic_slice_in_dim(refs_block, (dom_rank % owners_per_block) * CLS_DEV, CLS_DEV, 0)
     refs = jnp.where((dom_rank // owners_per_block) == rot_rank, mine, got)
     quarter = total // 4

time: 82.7 us -> 83 us (level)
  no operation moved by 1% of the time
where the time goes in v13:
time: 83 us; the launch traced here: 82.3 us
  starting transfers between devices  28.4 us (34%)
  other arithmetic  21.6 us (26%)
  waiting for transfers between devices  20.5 us (25%)
  Pallas kernels  3.75 us (5%)
  local copies, waits for them, and re-layouts  3.66 us (4%)
  matrix products  3.47 us (4%)
  between operations  0.9 us (1%)
    concatenate x1, other arithmetic, local(): stacked = jnp.concatenate(variants, axis=0)  14.6 us
    all_to_all x1, waiting for transfers between devices, local(): lax.all_to_all(jnp.broadcast_to(plain_chunk[None], (chunks, block, width)...  12.1 us
    ppermute x1, starting transfers between devices, local(): lax.ppermute(sent.reshape(flat), ('dom', 'rot'), pairs).reshape(sent.shape)  7.99 us
    all_to_all x1, starting transfers between devices, local(): summed = jnp.sum(lax.all_to_all(payload, 'dom', 0, 0, tiled=True), axis=0)  7.75 us
    all_to_all x1, waiting for transfers between devices, local(): best_scores = lax.all_to_all(best, 'rot', 0, 1, tiled=True)  7.73 us
    all_to_all x1, starting transfers between devices, local(): lax.all_to_all(jnp.broadcast_to(plain_chunk[None], (chunks, block, width)...  6.77 us
    all_to_all x1, starting transfers between devices, local(): best_scores = lax.all_to_all(best, 'rot', 0, 1, tiled=True)  5.86 us
    pallas_call x1, Pallas kernels, derotate_and_sum(): pl.pallas_call(prologue_kernel, out_shape=(jax.ShapeDtypeStruct((chunks,...  3.75 us
  transfers between devices with their start and end apart: 4, of which 3 were waited for; matrix products, arithmetic and copies ran while one was open for 31% of the time, Pallas kernels for 0%

profile of v13, /device:TPU:2, one launch (start us, length us, event | category | flops | bytes accessed | tf_op | source)
XLA Modules:
  0.0 82.3 jit_solution(16836448766380081067)
XLA Ops:
  0.6 3.7 %shard_map.86 = (f32[32,24,320]{2,1,0:T(8,128)}, bf16[64,8192]{1,0:T(8,128)(2,1)}) custom-call(bf16[64,8192]{1,0:T(8,128)(2,1)} %x_ref.1, f32[64,128]{1,0:T(8,128)} %constant.127.clone.cos_ref, f32[64,128]{1,0:T(8,128)} %constant.128.clone.sin_ref, s32[64]{0:T(128)} %rot_ref.1, s32[64]{0:T(128)} %group_ref.1, f32[32,64]{1,0:T(8,128)} %table_ref.1, ...), custom_call_target="tpu_custom_call" | custom-call | tf_op jit(solution)/shard_map/pallas_call | solution.py:77
  4.4 7.7 %all-to-all-start = ((f32[32,24,320]{2,1,0:T(8,128)}), f32[32,24,320]{2,1,0:T(8,128)S(1)}, u32[]{:S(2)}, u32[]{:S(2)}) async-start(f32[32,24,320]{2,1,0:T(8,128)} %get-tuple-element.4), calls=%async_computation | async-start | bytes 2359296 | tf_op jit(solution)/shard_map/all_to_all | solution.py:133
  12.4 1.4 %select_select_fusion.1 = (bf16[64,4096]{1,0:T(8,128)(2,1)S(1)}, bf16[64,4096]{1,0:T(8,128)(2,1)S(1)}) fusion(pred[4096]{0:T(1024)(128)(4,1)S(1)} %get-tuple-element.20, pred[4096]{0:T(1024)(128)(4,1)S(1)} %get-tuple-element.21, pred[4096]{0:T(1024)(128)(4,1)S(1)} %broadcast_compare_fusion.8, bf16[64,8192]{1,0:T(8,128)(2,1)} %get-tuple-element.5), kind=kLoop, calls=%fused_computation.12 | loop fusion | flops 2097152 | bytes 2109440 | tf_op jit(solution)/shard_map/jit(_where)/select_n | solution.py:167
  13.8 0.5 select_select_fusion.5
  14.3 14.6 %maximum_maximum_fusion = bf16[256,8192]{1,0:T(8,128)(2,1)} fusion(bf16[64,4096]{1,0:T(8,128)(2,1)S(1)} %get-tuple-element.13, bf16[64,4096]{1,0:T(8,128)(2,1)S(1)} %get-tuple-element.12, bf16[64,4096]{1,0:T(8,128)(2,1)S(1)} %get-tuple-element.14, bf16[64,4096]{1,0:T(8,128)(2,1)S(1)} %get-tuple-element.15, bf16[64,4096]{1,0:T(8,128)(2,1)S(1)} %get-tuple-element.9, ...), kind=kLoop, calls=%fused_computation.6 | loop fusion | flops 29360128 | bytes 8388608 | tf_op jit(solution)/shard_map/concatenate | solution.py:170
  28.9 0.6 all-to-all-done
  29.9 0.9 %broadcast_in_dim.73 = f32[32,24,256]{2,1,0:T(8,128)} broadcast(f32[24,256]{1,0:T(8,128)S(1)} %slice_divide_fusion), dimensions={1,2} | broadcast | bytes 811008 | tf_op jit(solution)/shard_map/broadcast_in_dim | solution.py:139
  30.9 6.8 %all-to-all-start.1 = ((f32[32,24,256]{2,1,0:T(8,128)}), f32[32,24,256]{2,1,0:T(8,128)S(1)}, u32[]{:S(2)}, u32[]{:S(2)}) async-start(f32[32,24,256]{2,1,0:T(8,128)} %broadcast_in_dim.73), calls=%async_computation.1 | async-start | bytes 1572864 | tf_op jit(solution)/shard_map/all_to_all | solution.py:138
  37.6 1.0 %fusion.9 = (f32[16,4096]{1,0:T(8,128)S(1)}, f32[16,4096]{1,0:T(8,128)S(1)}) fusion(s32[4096]{0:T(1024)S(1)} %get-tuple-element.28, s32[4096]{0:T(1024)S(1)} %get-tuple-element.29, pred[4096]{0:T(1024)(128)(4,1)S(1)} %fusion.17), kind=kLoop, calls=%fused_computation.24 | loop fusion | flops 983040 | bytes 561152 | tf_op jit(solution)/shard_map/cos | solution.py:107
  38.7 12.1 %all-to-all-done.1 = f32[32,24,256]{2,1,0:T(8,128)S(1)} async-done(((f32[32,24,256]{2,1,0:T(8,128)}), f32[32,24,256]{2,1,0:T(8,128)S(1)}, u32[]{:S(2)}, u32[]{:S(2)}) %all-to-all-start.1) | async-done | bytes 786464 | tf_op jit(solution)/shard_map/all_to_all | solution.py:138
  50.9 0.2 fusion.4
  51.1 0.1 divide_convert_fusion
  51.4 0.2 reshape.145
  51.5 8.0 %collective-permute-start = (bf16[48,1024]{1,0:T(8,128)(2,1)S(1)}, bf16[48,1024]{1,0:T(8,128)(2,1)S(1)}, u32[]{:S(2)}, u32[]{:S(2)}) collective-permute-start(bf16[48,1024]{1,0:T(8,128)(2,1)S(1)} %reshape.145), channel_id=1, source_target_pairs={{0,1},{8,2},{16,3},{24,4},{32,5},{40,6},{48,7},{56,9},{64,10},{72,... | collective-permute-start | bytes 294920 | tf_op jit(solution)/shard_map/ppermute | solution.py:157
  59.5 2.0 %subtract_convert_fusion = (bf16[16,24,4096]{2,1,0:T(8,128)(2,1)S(1)}, bf16[16,24,4096]{2,1,0:T(8,128)(2,1)S(1)}) fusion(f32[16,4096]{1,0:T(8,128)S(1)} %get-tuple-element.19, f32[24,4096]{1,0:T(8,128)S(1)} %get-tuple-element.17, f32[16,4096]{1,0:T(8,128)S(1)} %get-tuple-element.18, f32[24,4096]{1,0:T(8,128)S(1)} %get-tuple-element.16), kind=kLoop, calls=%fused_computation.5 | loop fusion | flops 12582912 | bytes 7602176 | tf_op jit(solution)/shard_map/convert
  61.6 3.5 %fusion.3 = f32[64,24]{0,1:T(8,128)S(1)} fusion(bf16[4,64,8192,1]{2,1,3,0:T(8,128)(2,1)S(1)} %bitcast.21, bf16[16,24,4096]{2,1,0:T(8,128)(2,1)S(1)} %get-tuple-element.7, bf16[16,24,4096]{2,1,0:T(8,128)(2,1)S(1)} %get-tuple-element.6), kind=kOutput, calls=%fused_computation.7 | convolution fusion | flops 1623292416 | bytes 10491904 | tf_op jit(solution)/shard_map/dot_general | solution.py:172
  65.1 0.7 reshape.149
  65.8 5.9 %all-to-all-start.2 = ((f32[8,1,192]{2,1,0:T(1,128)}), f32[8,1,192]{2,1,0:T(1,128)S(1)}, u32[]{:S(2)}, u32[]{:S(2)}) async-start(f32[8,1,192]{2,1,0:T(1,128)} %reshape.149), calls=%async_computation.2 | async-start | bytes 16384 | tf_op jit(solution)/shard_map/all_to_all | solution.py:176
  71.7 7.7 %all-to-all-done.2 = f32[8,1,192]{2,1,0:T(1,128)S(1)} async-done(((f32[8,1,192]{2,1,0:T(1,128)}), f32[8,1,192]{2,1,0:T(1,128)S(1)}, u32[]{:S(2)}, u32[]{:S(2)}) %all-to-all-start.2) | async-done | bytes 6176 | tf_op jit(solution)/shard_map/all_to_all | solution.py:176
  79.4 0.5 broadcast.254
  79.9 0.7 reduce.1
  80.7 0.7 all_to_all.22
  81.4 0.1 reshape.146
  81.5 0.7 dynamic-slice_select_fusion
  (26 shorter events, 0.8 us)
Async XLA Ops:
  4.4 9.4 %copy-start = (bf16[64,8192]{1,0:T(8,128)(2,1)S(1)}, bf16[64,8192]{1,0:T(8,128)(2,1)}, u32[]{:S(2)}) copy-start(bf16[64,8192]{1,0:T(8,128)(2,1)} %get-tuple-element.5) | copy-start | bytes 3145732
  4.4 25.2 %all-to-all-start = ((f32[32,24,320]{2,1,0:T(8,128)}), f32[32,24,320]{2,1,0:T(8,128)S(1)}, u32[]{:S(2)}, u32[]{:S(2)}) async-start(f32[32,24,320]{2,1,0:T(8,128)} %get-tuple-element.4), calls=%async_computation | async-start | bytes 2359296 | tf_op jit(solution)/shard_map/all_to_all | solution.py:133
  30.9 20.0 %all-to-all-start.1 = ((f32[32,24,256]{2,1,0:T(8,128)}), f32[32,24,256]{2,1,0:T(8,128)S(1)}, u32[]{:S(2)}, u32[]{:S(2)}) async-start(f32[32,24,256]{2,1,0:T(8,128)} %broadcast_in_dim.73), calls=%async_computation.1 | async-start | bytes 1572864 | tf_op jit(solution)/shard_map/all_to_all | solution.py:138
  51.5 10.0 %copy-start.1 = (bf16[256,8192]{1,0:T(8,128)(2,1)S(1)}, bf16[256,8192]{1,0:T(8,128)(2,1)}, u32[]{:S(2)}) copy-start(bf16[256,8192]{1,0:T(8,128)(2,1)} %maximum_maximum_fusion) | copy-start | bytes 12582916
  51.5 29.8 %collective-permute-start = (bf16[48,1024]{1,0:T(8,128)(2,1)S(1)}, bf16[48,1024]{1,0:T(8,128)(2,1)S(1)}, u32[]{:S(2)}, u32[]{:S(2)}) collective-permute-start(bf16[48,1024]{1,0:T(8,128)(2,1)S(1)} %reshape.145), channel_id=1, source_target_pairs={{0,1},{8,2},{16,3},{24,4},{32,5},{40,6},{48,7},{56,9},{64,10},{72,... | collective-permute-start | bytes 294920 | tf_op jit(solution)/shard_map/ppermute | solution.py:157
  65.8 13.6 %all-to-all-start.2 = ((f32[8,1,192]{2,1,0:T(1,128)}), f32[8,1,192]{2,1,0:T(1,128)S(1)}, u32[]{:S(2)}, u32[]{:S(2)}) async-start(f32[8,1,192]{2,1,0:T(1,128)} %reshape.149), calls=%async_computation.2 | async-start | bytes 16384 | tf_op jit(solution)/shard_map/all_to_all | solution.py:176

commit v14 on v11

--- a/solution.py
+++ b/solution.py
@@ -32,7 +32,7 @@
 
 def prologue_kernel(
     x_ref, cos_ref, sin_ref, rot_ref, group_ref, table_ref, assign_ref,
-    pay_ref, mod_ref, w_ref, ctf_ref, cos_scr, sin_scr,
+    pay_ref, w_ref, ctf_ref, cos_scr, sin_scr,
 ):
     count = x_ref.shape[0]
     block = pay_ref.shape[1]
@@ -58,8 +58,6 @@
         imag_part = x_ref[:, im_cols].astype(jnp.float32)
         w_ref[:, re_cols] = (real_part * cosine + imag_part * sine) * gain
         w_ref[:, im_cols] = (imag_part * cosine - real_part * sine) * gain
-        mod_ref[:, re_cols] = (real_part * gain).astype(jnp.bfloat16)
-        mod_ref[:, im_cols] = (imag_part * gain).astype(jnp.bfloat16)
     gains = ctf_ref[...]
     denom = split_dot(member, gains * gains)
     numer = split_dot(member, w_ref[...])
@@ -76,10 +74,7 @@
     vmem = pl.BlockSpec(memory_space=pltpu.VMEM)
     return pl.pallas_call(
         prologue_kernel,
-        out_shape=(
-            jax.ShapeDtypeStruct((chunks, block, K // chunks + CYCLES), jnp.float32),
-            jax.ShapeDtypeStruct((count, K), jnp.bfloat16),
-        ),
+        out_shape=jax.ShapeDtypeStruct((chunks, block, K // chunks + CYCLES), jnp.float32),
         in_specs=[vmem, vmem, vmem, smem, smem, vmem, vmem],
         scratch_shapes=[
             pltpu.VMEM((count, K), jnp.float32),
@@ -127,9 +122,12 @@
     chunks = dom_count
     width = K // chunks
     per_chunk = width // MFREQ
-    payload, modulated = derotate_and_sum(
+    payload = derotate_and_sum(
         particles, rot_index, group, ctf_table, assign, block, chunks, total
     )
+    ctf_cols = jnp.repeat(ctf_table[group], MFREQ, axis=1)
+    gain_cols = jnp.concatenate([ctf_cols, ctf_cols], axis=1)
+    modulated = (particles.astype(jnp.float32) * gain_cols).astype(jnp.bfloat16)
     summed = jnp.sum(lax.all_to_all(payload, "dom", 0, 0, tiled=True), axis=0)
     numer_chunk = summed[:, :width].reshape(block, per_chunk, MFREQ)
     first_cycle = (dom_rank * per_chunk) % CYCLES

time: 82.7 us -> 86.3 us (1.044)
  local copies, waits for them, and re-layouts: 3.35 us -> 6.18 us
  other arithmetic: 21.6 us -> 22.5 us
    convert_element_type x0 -> x1, other arithmetic: none -> 2.03 us  [local(): modulated = (particles.astype(jnp.float32) * gain_cols).astype(jnp.bfloat16)]
    reshape x0 -> x1, local copies, waits for them, and re-layouts: none -> 1.63 us  [local(): ctf_cols = jnp.repeat(ctf_table[group], MFREQ, axis=1)]
    select_n x2, other arithmetic: 1.97 us -> 0.77 us  [local(): jnp.where(step == 0, real_part, jnp.where(step == 1, imag_part, jnp.where...]
  transfers between devices with their start and end apart: 4 -> 4, of which waited for: 3 -> 2; matrix products, arithmetic and copies ran while one was open for 31% -> 34% of each run, Pallas kernels for 0% -> 0%
where the time goes in v14:
time: 86.3 us; the launch traced here: 85.5 us
  starting transfers between devices  28.8 us (33%)
  other arithmetic  22.5 us (26%)
  waiting for transfers between devices  19.9 us (23%)
  local copies, waits for them, and re-layouts  6.18 us (7%)
  Pallas kernels  3.76 us (4%)
  matrix products  3.47 us (4%)
  between operations  0.94 us (1%)
    concatenate x1, other arithmetic, local(): stacked = jnp.concatenate(variants, axis=0)  14.6 us
    all_to_all x1, waiting for transfers between devices, local(): lax.all_to_all(jnp.broadcast_to(plain_chunk[None], (chunks, block, width)...  12.1 us
    ppermute x1, starting transfers between devices, local(): got = lax.ppermute(sent, ('dom', 'rot'), pairs)  7.99 us
    all_to_all x1, waiting for transfers between devices, local(): best_scores = lax.all_to_all(best, 'rot', 0, 1, tiled=True)  7.73 us
    all_to_all x1, starting transfers between devices, local(): summed = jnp.sum(lax.all_to_all(payload, 'dom', 0, 0, tiled=True), axis=0)  7.62 us
    all_to_all x1, starting transfers between devices, local(): lax.all_to_all(jnp.broadcast_to(plain_chunk[None], (chunks, block, width)...  7.38 us
    all_to_all x1, starting transfers between devices, local(): best_scores = lax.all_to_all(best, 'rot', 0, 1, tiled=True)  5.85 us
    pallas_call x1, Pallas kernels, derotate_and_sum(): pl.pallas_call(prologue_kernel, out_shape=jax.ShapeDtypeStruct((chunks, b...  3.76 us
  transfers between devices with their start and end apart: 4, of which 2 were waited for; matrix products, arithmetic and copies ran while one was open for 34% of the time, Pallas kernels for 0%

profile of v14, /device:TPU:2, one launch (start us, length us, event | category | flops | bytes accessed | tf_op | source)
XLA Modules:
  0.0 85.5 jit_solution(1432370290936381059)
XLA Ops:
  0.7 3.8 %shard_map.86 = f32[32,24,320]{2,1,0:T(8,128)} custom-call(bf16[64,8192]{1,0:T(8,128)(2,1)} %x_ref.1, f32[64,128]{1,0:T(8,128)} %constant.130.clone.cos_ref, f32[64,128]{1,0:T(8,128)} %constant.131.clone.sin_ref, s32[64]{0:T(128)} %rot_ref.1, s32[64]{0:T(128)} %group_ref.1, f32[32,64]{1,0:T(8,128)} %table_ref.1, s32[1,64]{1,0:T(1,128)} %bitcast.25), custom_call_target="tpu_custom_call" | custom-call | tf_op jit(solution)/shard_map/pallas_call | solution.py:75
  4.4 7.6 %all-to-all-start = ((f32[32,24,320]{2,1,0:T(8,128)}), f32[32,24,320]{2,1,0:T(8,128)S(1)}, u32[]{:S(2)}, u32[]{:S(2)}) async-start(f32[32,24,320]{2,1,0:T(8,128)} %shard_map.86), calls=%async_computation | async-start | bytes 2359296 | tf_op jit(solution)/shard_map/all_to_all | solution.py:131
  12.3 0.6 gather_fusion
  12.9 0.6 broadcast_in_dim.81
  13.5 1.6 %reshape.142 = f32[64,4096]{1,0:T(8,128)} reshape(f32[64,64,64]{2,1,0:T(8,128)S(1)} %broadcast_in_dim.81) | data formatting | bytes 2097152 | tf_op jit(solution)/shard_map/reshape | solution.py:128
  15.1 2.0 %fusion.3 = bf16[64,8192]{1,0:T(8,128)(2,1)S(1)} fusion(f32[64,4096]{1,0:T(8,128)} %reshape.142, bf16[64,8192]{1,0:T(8,128)(2,1)} %x_ref.1), kind=kLoop, calls=%fused_computation.9 | loop fusion | flops 2097152 | bytes 3145728 | tf_op jit(solution)/shard_map/convert_element_type | solution.py:130
  17.2 0.2 select_select_fusion.1
  17.4 0.5 select_select_fusion.5
  17.9 14.6 %maximum_maximum_fusion = bf16[256,8192]{1,0:T(8,128)(2,1)} fusion(bf16[64,4096]{1,0:T(8,128)(2,1)S(1)} %get-tuple-element.9, bf16[64,4096]{1,0:T(8,128)(2,1)S(1)} %get-tuple-element.8, bf16[64,4096]{1,0:T(8,128)(2,1)S(1)} %get-tuple-element.10, bf16[64,4096]{1,0:T(8,128)(2,1)S(1)} %get-tuple-element.11, bf16[64,4096]{1,0:T(8,128)(2,1)S(1)} %get-tuple-element.5, ...), kind=kLoop, calls=%fused_computation.7 | loop fusion | flops 29360128 | bytes 8388608 | tf_op jit(solution)/shard_map/concatenate | solution.py:167
  32.9 0.9 %broadcast_in_dim.79 = f32[32,24,256]{2,1,0:T(8,128)} broadcast(f32[24,256]{1,0:T(8,128)S(1)} %slice_divide_fusion), dimensions={1,2} | broadcast | bytes 811008 | tf_op jit(solution)/shard_map/broadcast_in_dim | solution.py:137
  33.9 7.4 %all-to-all-start.1 = ((f32[32,24,256]{2,1,0:T(8,128)}), f32[32,24,256]{2,1,0:T(8,128)S(1)}, u32[]{:S(2)}, u32[]{:S(2)}) async-start(f32[32,24,256]{2,1,0:T(8,128)} %broadcast_in_dim.79), calls=%async_computation.1 | async-start | bytes 1572864 | tf_op jit(solution)/shard_map/all_to_all | solution.py:136
  41.2 1.0 %fusion.10 = (f32[16,4096]{1,0:T(8,128)S(1)}, f32[16,4096]{1,0:T(8,128)S(1)}) fusion(s32[4096]{0:T(1024)S(1)} %get-tuple-element.24, s32[4096]{0:T(1024)S(1)} %get-tuple-element.25, pred[4096]{0:T(1024)(128)(4,1)S(1)} %fusion.18), kind=kLoop, calls=%fused_computation.27 | loop fusion | flops 983040 | bytes 561152 | tf_op jit(solution)/shard_map/cos | solution.py:102
  42.3 12.1 %all-to-all-done.1 = f32[32,24,256]{2,1,0:T(8,128)S(1)} async-done(((f32[32,24,256]{2,1,0:T(8,128)}), f32[32,24,256]{2,1,0:T(8,128)S(1)}, u32[]{:S(2)}, u32[]{:S(2)}) %all-to-all-start.1) | async-done | bytes 786464 | tf_op jit(solution)/shard_map/all_to_all | solution.py:136
  54.5 0.2 fusion.5
  55.0 8.0 %collective-permute-start = (bf16[6,8192]{1,0:T(8,128)(2,1)S(1)}, bf16[6,8192]{1,0:T(8,128)(2,1)S(1)}, u32[]{:S(2)}, u32[]{:S(2)}) collective-permute-start(bf16[6,8192]{1,0:T(8,128)(2,1)S(1)} %constant_dynamic-slice_fusion), channel_id=1, source_target_pairs={{0,1},{8,2},{16,3},{24,4},{32,5},{40,6},{48,7},{56,9},{64,10},{72,... | collective-permute-start | bytes 294920 | tf_op jit(solution)/shard_map/ppermute | solution.py:154
  63.0 2.0 %subtract_convert_fusion = (bf16[16,24,4096]{2,1,0:T(8,128)(2,1)S(1)}, bf16[16,24,4096]{2,1,0:T(8,128)(2,1)S(1)}) fusion(f32[16,4096]{1,0:T(8,128)S(1)} %get-tuple-element.15, f32[24,4096]{1,0:T(8,128)S(1)} %get-tuple-element.13, f32[16,4096]{1,0:T(8,128)S(1)} %get-tuple-element.14, f32[24,4096]{1,0:T(8,128)S(1)} %get-tuple-element.12), kind=kLoop, calls=%fused_computation.6 | loop fusion | flops 12582912 | bytes 7602176 | tf_op jit(solution)/shard_map/convert
  65.0 3.5 %fusion.4 = f32[64,24]{0,1:T(8,128)S(1)} fusion(bf16[4,64,8192,1]{2,1,3,0:T(8,128)(2,1)S(1)} %bitcast.21, bf16[16,24,4096]{2,1,0:T(8,128)(2,1)S(1)} %get-tuple-element.3, bf16[16,24,4096]{2,1,0:T(8,128)(2,1)S(1)} %get-tuple-element.2), kind=kOutput, calls=%fused_computation.10 | convolution fusion | flops 1623292416 | bytes 10491904 | tf_op jit(solution)/shard_map/dot_general | solution.py:169
  68.6 0.7 reshape.154
  69.3 5.9 %all-to-all-start.2 = ((f32[8,1,192]{2,1,0:T(1,128)}), f32[8,1,192]{2,1,0:T(1,128)S(1)}, u32[]{:S(2)}, u32[]{:S(2)}) async-start(f32[8,1,192]{2,1,0:T(1,128)} %reshape.154), calls=%async_computation.2 | async-start | bytes 16384 | tf_op jit(solution)/shard_map/all_to_all | solution.py:173
  75.1 7.7 %all-to-all-done.2 = f32[8,1,192]{2,1,0:T(1,128)S(1)} async-done(((f32[8,1,192]{2,1,0:T(1,128)}), f32[8,1,192]{2,1,0:T(1,128)S(1)}, u32[]{:S(2)}, u32[]{:S(2)}) %all-to-all-start.2) | async-done | bytes 6176 | tf_op jit(solution)/shard_map/all_to_all | solution.py:173
  82.9 0.5 broadcast.258
  83.4 0.7 reduce.1
  84.1 0.7 all_to_all.22
  84.8 0.7 dynamic-slice_select_fusion
  (32 shorter events, 1.0 us)
Async XLA Ops:
  0.6 11.5 %copy-start.2 = (s32[64]{0:T(128)S(1)}, s32[64]{0:T(128)}, u32[]{:S(2)}) copy-start(s32[64]{0:T(128)} %group_ref.1) | copy-start | bytes 772
  0.6 11.6 %copy-start = (f32[32,64]{1,0:T(8,128)S(1)}, f32[32,64]{1,0:T(8,128)}, u32[]{:S(2)}) copy-start(f32[32,64]{1,0:T(8,128)} %table_ref.1) | copy-start | bytes 24580
  4.4 28.1 %all-to-all-start = ((f32[32,24,320]{2,1,0:T(8,128)}), f32[32,24,320]{2,1,0:T(8,128)S(1)}, u32[]{:S(2)}, u32[]{:S(2)}) async-start(f32[32,24,320]{2,1,0:T(8,128)} %shard_map.86), calls=%async_computation | async-start | bytes 2359296 | tf_op jit(solution)/shard_map/all_to_all | solution.py:131
  33.9 20.6 %all-to-all-start.1 = ((f32[32,24,256]{2,1,0:T(8,128)}), f32[32,24,256]{2,1,0:T(8,128)S(1)}, u32[]{:S(2)}, u32[]{:S(2)}) async-start(f32[32,24,256]{2,1,0:T(8,128)} %broadcast_in_dim.79), calls=%async_computation.1 | async-start | bytes 1572864 | tf_op jit(solution)/shard_map/all_to_all | solution.py:136
  54.9 10.1 %copy-start.1 = (bf16[256,8192]{1,0:T(8,128)(2,1)S(1)}, bf16[256,8192]{1,0:T(8,128)(2,1)}, u32[]{:S(2)}) copy-start(bf16[256,8192]{1,0:T(8,128)(2,1)} %maximum_maximum_fusion) | copy-start | bytes 12582916
  55.0 29.9 %collective-permute-start = (bf16[6,8192]{1,0:T(8,128)(2,1)S(1)}, bf16[6,8192]{1,0:T(8,128)(2,1)S(1)}, u32[]{:S(2)}, u32[]{:S(2)}) collective-permute-start(bf16[6,8192]{1,0:T(8,128)(2,1)S(1)} %constant_dynamic-slice_fusion), channel_id=1, source_target_pairs={{0,1},{8,2},{16,3},{24,4},{32,5},{40,6},{48,7},{56,9},{64,10},{72,... | collective-permute-start | bytes 294920 | tf_op jit(solution)/shard_map/ppermute | solution.py:154
  69.3 13.6 %all-to-all-start.2 = ((f32[8,1,192]{2,1,0:T(1,128)}), f32[8,1,192]{2,1,0:T(1,128)S(1)}, u32[]{:S(2)}, u32[]{:S(2)}) async-start(f32[8,1,192]{2,1,0:T(1,128)} %reshape.154), calls=%async_computation.2 | async-start | bytes 16384 | tf_op jit(solution)/shard_map/all_to_all | solution.py:173

commit v15 on v11

--- a/solution.py
+++ b/solution.py
@@ -98,18 +98,45 @@
     )
 
 
-def rotate_all(refs, turns, total):
-    count = refs.shape[0]
+def score_kernel(x_ref, refs_ref, cos_ref, sin_ref, out_ref, turned_scr, found_scr):
+    block = refs_ref.shape[0]
+    turns, half = cos_ref.shape
+    count = out_ref.shape[0]
+    real_part = refs_ref[:, :half]
+    imag_part = refs_ref[:, half:]
+    for r in range(turns):
+        cosine = cos_ref[pl.ds(r, 1), :]
+        sine = sin_ref[pl.ds(r, 1), :]
+        rows = pl.ds(r * block, block)
+        turned_scr[rows, :half] = (real_part * cosine - imag_part * sine).astype(jnp.bfloat16)
+        turned_scr[rows, half:] = (real_part * sine + imag_part * cosine).astype(jnp.bfloat16)
+    found = lax.dot_general(
+        x_ref[...], turned_scr[...], (((1,), (1,)), ((), ())), preferred_element_type=jnp.float32
+    )
+    best = found[:count]
+    for u in range(1, x_ref.shape[0] // count):
+        best = jnp.maximum(best, found[u * count : (u + 1) * count])
+    found_scr[...] = best
+    top = found_scr[:, pl.ds(0, block)]
+    for r in range(1, turns):
+        top = jnp.maximum(top, found_scr[:, pl.ds(r * block, block)])
+    out_ref[...] = top * (1.0 / math.sqrt(K))
+
+
+def score_all(stacked, refs, turns, total):
+    block = refs.shape[0]
     half = K // 2
-    real_part = refs[None, :, :half]
-    imag_part = refs[None, :, half:]
-    angle = column_angles(jnp.arange(turns, dtype=jnp.int32), total, half)
-    cosine = jnp.cos(angle)[:, None, :]
-    sine = jnp.sin(angle)[:, None, :]
-    turned = jnp.concatenate(
-        [real_part * cosine - imag_part * sine, real_part * sine + imag_part * cosine], axis=2
-    )
-    return turned.reshape(turns * count, K).astype(jnp.bfloat16)
+    phase = (np.arange(half)[None, :] % MFREQ) * np.arange(turns)[:, None] % total
+    angle = phase.astype(np.float32) * np.float32(2.0 * math.pi / total)
+    count = stacked.shape[0] // 4
+    return pl.pallas_call(
+        score_kernel,
+        out_shape=jax.ShapeDtypeStruct((count, block), jnp.float32),
+        scratch_shapes=[
+            pltpu.VMEM((turns * block, K), jnp.bfloat16),
+            pltpu.VMEM((count, turns * block), jnp.float32),
+        ],
+    )(stacked, refs, jnp.asarray(np.cos(angle)), jnp.asarray(np.sin(angle)))
 
 
 def local(particles, assign, rot_index, group, ctf_table):
@@ -167,11 +194,7 @@
         im_u = jnp.where(step == 0, imag_part, jnp.where(step == 1, -real_part, jnp.where(step == 2, -imag_part, real_part)))
         variants.append(jnp.concatenate([re_u, im_u], axis=1))
     stacked = jnp.concatenate(variants, axis=0)
-    turned = rotate_all(refs_block.astype(jnp.float32), quarter, total)
-    found = lax.dot_general(
-        stacked, turned, (((1,), (1,)), ((), ())), preferred_element_type=jnp.float32
-    )
-    best = jnp.max(found.reshape(4, count, quarter, block), axis=(0, 2)) * (1.0 / math.sqrt(K))
+    best = score_all(stacked, refs_block.astype(jnp.float32), quarter, total)
     best_scores = lax.all_to_all(best, "rot", 0, 1, tiled=True)
 
     return (refs, best_scores)

time: 82.7 us -> 103 us (1.25)
  waiting for transfers between devices: 20.5 us -> 34.3 us
  Pallas kernels: 3.75 us -> 9.43 us
  other arithmetic: 21.6 us -> 26.9 us
  matrix products: 3.47 us -> 0 us
  starting transfers between devices: 28.4 us -> 26.4 us
    all_to_all x1, waiting for transfers between devices: 0.61 us -> 14.5 us  [local(): summed = jnp.sum(lax.all_to_all(payload, 'dom', 0, 0, tiled=True), axis=0)]
    pallas_call x0 -> x1, Pallas kernels: none -> 5.69 us  [score_all(): pl.pallas_call(score_kernel, out_shape=jax.ShapeDtypeStruct((count, block...]
    concatenate x1, other arithmetic: 14.6 us -> 20 us  [local(): stacked = jnp.concatenate(variants, axis=0)]
    dot_general x1 -> x0, matrix products: 3.47 us -> none  [local(): lax.dot_general(stacked, turned, (((1,), (1,)), ((), ())), preferred_elem...]
    another operation x1 -> x0, other arithmetic: 2.04 us -> none
    select_n x2, other arithmetic: 1.97 us -> 3.96 us  [local(): jnp.where(step == 0, real_part, jnp.where(step == 1, imag_part, jnp.where...]
    all_to_all x1, starting transfers between devices: 6.77 us -> 5.1 us  [local(): lax.all_to_all(jnp.broadcast_to(plain_chunk[None], (chunks, block, width)...]
    cos x1 -> x0, other arithmetic: 1.05 us -> none  [rotate_all(): cosine = jnp.cos(angle)[:, None, :]]
  transfers between devices with their start and end apart: 4 -> 4, of which waited for: 3 -> 3; matrix products, arithmetic and copies ran while one was open for 31% -> 26% of each run, Pallas kernels for 0% -> 6%
where the time goes in v15:
time: 103 us; the launch traced here: 102 us
  waiting for transfers between devices  34.3 us (33%)
  other arithmetic  26.9 us (26%)
  starting transfers between devices  26.4 us (26%)
  Pallas kernels  9.43 us (9%)
  local copies, waits for them, and re-layouts  3.96 us (4%)
    concatenate x1, other arithmetic, local(): stacked = jnp.concatenate(variants, axis=0)  20 us
    all_to_all x1, waiting for transfers between devices, local(): summed = jnp.sum(lax.all_to_all(payload, 'dom', 0, 0, tiled=True), axis=0)  14.5 us
    all_to_all x1, waiting for transfers between devices, local(): lax.all_to_all(jnp.broadcast_to(plain_chunk[None], (chunks, block, width)...  12 us
    all_to_all x1, starting transfers between devices, local(): summed = jnp.sum(lax.all_to_all(payload, 'dom', 0, 0, tiled=True), axis=0)  7.75 us
    all_to_all x1, waiting for transfers between devices, local(): best_scores = lax.all_to_all(best, 'rot', 0, 1, tiled=True)  7.73 us
    ppermute x1, starting transfers between devices, local(): got = lax.ppermute(sent, ('dom', 'rot'), pairs)  7.73 us
    all_to_all x1, starting transfers between devices, local(): best_scores = lax.all_to_all(best, 'rot', 0, 1, tiled=True)  5.83 us
    pallas_call x1, Pallas kernels, score_all(): pl.pallas_call(score_kernel, out_shape=jax.ShapeDtypeStruct((count, block...  5.69 us
  transfers between devices with their start and end apart: 4, of which 3 were waited for; matrix products, arithmetic and copies ran while one was open for 26% of the time, Pallas kernels for 6%

profile of v15, /device:TPU:2, one launch (start us, length us, event | category | flops | bytes accessed | tf_op | source)
XLA Modules:
  0.0 101.8 jit_solution(10451392667527667758)
XLA Ops:
  0.6 3.7 %shard_map.104 = (f32[32,24,320]{2,1,0:T(8,128)}, bf16[64,8192]{1,0:T(8,128)(2,1)}) custom-call(bf16[64,8192]{1,0:T(8,128)(2,1)} %x_ref.1, f32[64,128]{1,0:T(8,128)} %constant.114.clone.cos_ref, f32[64,128]{1,0:T(8,128)} %constant.115.clone.sin_ref, s32[64]{0:T(128)} %rot_ref.1, s32[64]{0:T(128)} %group_ref.1, f32[32,64]{1,0:T(8,128)} %table_ref.1, ...), custom_call_target="tpu_custom_call" | custom-call | tf_op jit(solution)/shard_map/pallas_call | solution.py:77
  4.4 7.8 %all-to-all-start = ((f32[32,24,320]{2,1,0:T(8,128)}), f32[32,24,320]{2,1,0:T(8,128)S(1)}, u32[]{:S(2)}, u32[]{:S(2)}) async-start(f32[32,24,320]{2,1,0:T(8,128)} %get-tuple-element.4), calls=%async_computation | async-start | bytes 2359296 | tf_op jit(solution)/shard_map/all_to_all | solution.py:160
  12.3 2.7 %select_select_fusion.5 = (bf16[64,4096]{1,0:T(8,128)(2,1)S(1)}, bf16[64,4096]{1,0:T(8,128)(2,1)S(1)}, bf16[64,4096]{1,0:T(8,128)(2,1)}, bf16[64,4096]{1,0:T(8,128)(2,1)}) fusion(pred[4096]{0:T(1024)(128)(4,1)S(1)} %get-tuple-element.19, pred[4096]{0:T(1024)(128)(4,1)S(1)} %get-tuple-element.21, pred[4096]{0:T(1024)(128)(4,1)S(1)} %get-tuple-element.23, ...), kind=kLoop, calls=%fused_computation.9 | loop fusion | flops 3670016 | bytes 3170304 | tf_op jit(solution)/shard_map/jit(_where)/select_n | solution.py:193
  15.1 14.5 %all-to-all-done = f32[32,24,320]{2,1,0:T(8,128)S(1)} async-done(((f32[32,24,320]{2,1,0:T(8,128)}), f32[32,24,320]{2,1,0:T(8,128)S(1)}, u32[]{:S(2)}, u32[]{:S(2)}) %all-to-all-start) | async-done | bytes 983072 | tf_op jit(solution)/shard_map/all_to_all | solution.py:160
  29.5 0.1 reduce_sum.18
  29.6 0.1 dynamic-slice_add_fusion
  29.7 0.1 div.37
  29.8 0.1 div.38
  29.9 0.9 broadcast_in_dim.68
  30.9 5.1 %all-to-all-start.1 = ((f32[32,24,256]{2,1,0:T(8,128)}), f32[32,24,256]{2,1,0:T(8,128)S(1)}, u32[]{:S(2)}, u32[]{:S(2)}) async-start(f32[32,24,256]{2,1,0:T(8,128)} %broadcast_in_dim.68), calls=%async_computation.1 | async-start | bytes 1572864 | tf_op jit(solution)/shard_map/all_to_all | solution.py:165
  36.0 1.2 %select_select_fusion.1 = (bf16[64,4096]{1,0:T(8,128)(2,1)}, bf16[64,4096]{1,0:T(8,128)(2,1)}) fusion(pred[4096]{0:T(1024)(128)(4,1)S(1)} %get-tuple-element.16, pred[4096]{0:T(1024)(128)(4,1)S(1)} %get-tuple-element.17, pred[4096]{0:T(1024)(128)(4,1)S(1)} %broadcast_compare_fusion.8, bf16[64,8192]{1,0:T(8,128)(2,1)S(1)} %copy-done), kind=kLoop, calls=%fused_computation.5 | loop fusion | flops 2097152 | bytes 2109440 | tf_op jit(solution)/shard_map/jit(_where)/select_n | solution.py:193
  37.2 12.0 %all-to-all-done.1 = f32[32,24,256]{2,1,0:T(8,128)S(1)} async-done(((f32[32,24,256]{2,1,0:T(8,128)}), f32[32,24,256]{2,1,0:T(8,128)S(1)}, u32[]{:S(2)}, u32[]{:S(2)}) %all-to-all-start.1) | async-done | bytes 786464 | tf_op jit(solution)/shard_map/all_to_all | solution.py:165
  49.3 0.2 fusion
  49.5 1.0 %fusion.7 = (f32[24,8192]{1,0:T(8,128)}, bf16[24,8192]{1,0:T(8,128)(2,1)S(1)}) fusion(f32[24,8192]{1,0:T(8,128)S(1)} %bitcast.10, f32[24]{0:T(128)S(1)} %add_sqrt_fusion), kind=kLoop, calls=%fused_computation.41 | loop fusion | flops 589824 | bytes 1966176 | tf_op jit(solution)/shard_map/convert_element_type | solution.py:197
  50.6 7.7 %collective-permute-start = (bf16[6,8192]{1,0:T(8,128)(2,1)S(1)}, bf16[6,8192]{1,0:T(8,128)(2,1)S(1)}, u32[]{:S(2)}, u32[]{:S(2)}) collective-permute-start(bf16[6,8192]{1,0:T(8,128)(2,1)S(1)} %constant_dynamic-slice_fusion), channel_id=1, source_target_pairs={{0,1},{8,2},{16,3},{24,4},{32,5},{40,6},{48,7},{56,9},{64,10},{72,... | collective-permute-start | bytes 294920 | tf_op jit(solution)/shard_map/ppermute | solution.py:183
  58.4 20.0 %maximum_maximum_fusion.x_ref = bf16[256,8192]{1,0:T(8,128)(2,1)} fusion(bf16[64,4096]{1,0:T(8,128)(2,1)S(1)} %copy-done.2, bf16[64,4096]{1,0:T(8,128)(2,1)S(1)} %copy-done.1, bf16[64,4096]{1,0:T(8,128)(2,1)} %get-tuple-element.14, bf16[64,4096]{1,0:T(8,128)(2,1)} %get-tuple-element.15, bf16[64,4096]{1,0:T(8,128)(2,1)S(1)} %get-tuple-element.9, ...), kind=kLoop, calls=%fused_computation | loop fusion | flops 29360128 | bytes 8388608 | tf_op jit(solution)/shard_map/concatenate | solution.py:196
  78.4 5.7 %shard_map.105 = f32[64,24]{1,0:T(8,128)} custom-call(bf16[256,8192]{1,0:T(8,128)(2,1)} %maximum_maximum_fusion.x_ref, f32[24,8192]{1,0:T(8,128)} %get-tuple-element.6.refs_ref, f32[16,4096]{1,0:T(8,128)} %constant.116.clone.cos_ref, f32[16,4096]{1,0:T(8,128)} %constant.117.clone.sin_ref), custom_call_target="tpu_custom_call" | custom-call | tf_op jit(solution)/shard_map/pallas_call | solution.py:132
  84.1 1.4 %reshape.30 = f32[8,1,192]{2,1,0:T(1,128)} reshape(f32[8,8,24]{2,1,0:T(8,128)} %bitcast.11) | data formatting | bytes 12288
  85.6 5.8 %all-to-all-start.2 = ((f32[8,1,192]{2,1,0:T(1,128)}), f32[8,1,192]{2,1,0:T(1,128)S(1)}, u32[]{:S(2)}, u32[]{:S(2)}) async-start(f32[8,1,192]{2,1,0:T(1,128)} %reshape.30), calls=%async_computation.2 | async-start | bytes 16384 | tf_op jit(solution)/shard_map/all_to_all | solution.py:198
  91.4 7.7 %all-to-all-done.2 = f32[8,1,192]{2,1,0:T(1,128)S(1)} async-done(((f32[8,1,192]{2,1,0:T(1,128)}), f32[8,1,192]{2,1,0:T(1,128)S(1)}, u32[]{:S(2)}, u32[]{:S(2)}) %all-to-all-start.2) | async-done | bytes 6176 | tf_op jit(solution)/shard_map/all_to_all | solution.py:198
  99.1 0.5 broadcast.132
  99.6 0.7 reduce.1
  100.4 0.7 all_to_all.25
  101.1 0.7 dynamic-slice_select_fusion
  (19 shorter events, 0.3 us)
Async XLA Ops:
  4.4 31.6 %copy-start = (bf16[64,8192]{1,0:T(8,128)(2,1)S(1)}, bf16[64,8192]{1,0:T(8,128)(2,1)}, u32[]{:S(2)}) copy-start(bf16[64,8192]{1,0:T(8,128)(2,1)} %get-tuple-element.5) | copy-start | bytes 3145732
  4.4 25.2 %all-to-all-start = ((f32[32,24,320]{2,1,0:T(8,128)}), f32[32,24,320]{2,1,0:T(8,128)S(1)}, u32[]{:S(2)}, u32[]{:S(2)}) async-start(f32[32,24,320]{2,1,0:T(8,128)} %get-tuple-element.4), calls=%async_computation | async-start | bytes 2359296 | tf_op jit(solution)/shard_map/all_to_all | solution.py:160
  30.9 18.4 %all-to-all-start.1 = ((f32[32,24,256]{2,1,0:T(8,128)}), f32[32,24,256]{2,1,0:T(8,128)S(1)}, u32[]{:S(2)}, u32[]{:S(2)}) async-start(f32[32,24,256]{2,1,0:T(8,128)} %broadcast_in_dim.68), calls=%async_computation.1 | async-start | bytes 1572864 | tf_op jit(solution)/shard_map/all_to_all | solution.py:165
  49.3 9.1 %copy-start.1 = (bf16[64,4096]{1,0:T(8,128)(2,1)S(1)}, bf16[64,4096]{1,0:T(8,128)(2,1)}, u32[]{:S(2)}) copy-start(bf16[64,4096]{1,0:T(8,128)(2,1)} %get-tuple-element.12) | copy-start | bytes 1572868
  49.3 9.1 %copy-start.2 = (bf16[64,4096]{1,0:T(8,128)(2,1)S(1)}, bf16[64,4096]{1,0:T(8,128)(2,1)}, u32[]{:S(2)}) copy-start(bf16[64,4096]{1,0:T(8,128)(2,1)} %get-tuple-element.13) | copy-start | bytes 1572868
  50.6 50.4 %collective-permute-start = (bf16[6,8192]{1,0:T(8,128)(2,1)S(1)}, bf16[6,8192]{1,0:T(8,128)(2,1)S(1)}, u32[]{:S(2)}, u32[]{:S(2)}) collective-permute-start(bf16[6,8192]{1,0:T(8,128)(2,1)S(1)} %constant_dynamic-slice_fusion), channel_id=1, source_target_pairs={{0,1},{8,2},{16,3},{24,4},{32,5},{40,6},{48,7},{56,9},{64,10},{72,... | collective-permute-start | bytes 294920 | tf_op jit(solution)/shard_map/ppermute | solution.py:183
  85.6 13.6 %all-to-all-start.2 = ((f32[8,1,192]{2,1,0:T(1,128)}), f32[8,1,192]{2,1,0:T(1,128)S(1)}, u32[]{:S(2)}, u32[]{:S(2)}) async-start(f32[8,1,192]{2,1,0:T(1,128)} %reshape.30), calls=%async_computation.2 | async-start | bytes 16384 | tf_op jit(solution)/shard_map/all_to_all | solution.py:198

commit v16 on v11

--- a/solution.py
+++ b/solution.py
@@ -146,16 +146,19 @@
     others = rot_count - 1
     pairs = []
     for plane in range(rot_count):
-        for sender in range(owners_per_block * others):
-            owner = plane * owners_per_block + sender // others
-            target = (plane + 1 + sender % others) % rot_count
+        first_owner = plane * owners_per_block
+        senders = [x for x in range(dom_count) if x // owners_per_block != plane]
+        for owner in range(first_owner, first_owner + owners_per_block):
+            pairs.append((owner * rot_count + plane, owner * rot_count + plane))
+        for idx, sender in enumerate(senders[: owners_per_block * others]):
+            owner = first_owner + idx // others
+            target = (plane + 1 + idx % others) % rot_count
             pairs.append((sender * rot_count + plane, owner * rot_count + target))
-    sent = lax.dynamic_slice_in_dim(
-        refs_block, jnp.minimum(dom_rank // others, owners_per_block - 1) * CLS_DEV, CLS_DEV, 0
-    )
-    got = lax.ppermute(sent, ("dom", "rot"), pairs)
-    mine = lax.dynamic_slice_in_dim(refs_block, (dom_rank % owners_per_block) * CLS_DEV, CLS_DEV, 0)
-    refs = jnp.where((dom_rank // owners_per_block) == rot_rank, mine, got)
+    own_plane = (dom_rank // owners_per_block) == rot_rank
+    idx = jnp.where(dom_rank > rot_rank * owners_per_block, dom_rank - owners_per_block, dom_rank)
+    slot = jnp.where(own_plane, dom_rank % owners_per_block, jnp.minimum(idx // others, owners_per_block - 1))
+    sent = lax.dynamic_slice_in_dim(refs_block, slot * CLS_DEV, CLS_DEV, 0)
+    refs = lax.ppermute(sent, ("dom", "rot"), pairs)
     quarter = total // 4
     real_part = modulated[:, :half]
     imag_part = modulated[:, half:]

time: 82.7 us -> 81.5 us (0.985)
  blocking collectives: 0 us -> 20.4 us
  starting transfers between devices: 28.4 us -> 15.5 us
  waiting for transfers between devices: 20.5 us -> 12.7 us
    all_to_all x0 -> x1, blocking collectives: none -> 20.4 us  [local(): best_scores = lax.all_to_all(best, 'rot', 0, 1, tiled=True)]
    all_to_all x1 -> x0, waiting for transfers between devices: 7.73 us -> none  [local(): best_scores = lax.all_to_all(best, 'rot', 0, 1, tiled=True)]
    ppermute x1, starting transfers between devices: 7.99 us -> 0.98 us  [local(): refs = lax.ppermute(sent, ('dom', 'rot'), pairs)]
    all_to_all x1 -> x0, starting transfers between devices: 5.85 us -> none  [local(): best_scores = lax.all_to_all(best, 'rot', 0, 1, tiled=True)]
  transfers between devices with their start and end apart: 4 -> 3, of which waited for: 3 -> 2; matrix products, arithmetic and copies ran while one was open for 31% -> 30% of each run, Pallas kernels for 0% -> 0%
where the time goes in v16:
time: 81.5 us; the launch traced here: 81.1 us
  other arithmetic  20.9 us (26%)
  blocking collectives  20.4 us (25%)
  starting transfers between devices  15.5 us (19%)
  waiting for transfers between devices  12.7 us (16%)
  Pallas kernels  3.74 us (5%)
  matrix products  3.47 us (4%)
  local copies, waits for them, and re-layouts  3.41 us (4%)
  between operations  0.94 us (1%)
    all_to_all x1, blocking collectives, local(): best_scores = lax.all_to_all(best, 'rot', 0, 1, tiled=True)  20.4 us
    concatenate x1, other arithmetic, local(): stacked = jnp.concatenate(variants, axis=0)  14.6 us
    all_to_all x1, waiting for transfers between devices, local(): lax.all_to_all(jnp.broadcast_to(plain_chunk[None], (chunks, block, width)...  12.1 us
    all_to_all x1, starting transfers between devices, local(): summed = jnp.sum(lax.all_to_all(payload, 'dom', 0, 0, tiled=True), axis=0)  7.75 us
    all_to_all x1, starting transfers between devices, local(): lax.all_to_all(jnp.broadcast_to(plain_chunk[None], (chunks, block, width)...  6.79 us
    pallas_call x1, Pallas kernels, derotate_and_sum(): pl.pallas_call(prologue_kernel, out_shape=(jax.ShapeDtypeStruct((chunks,...  3.74 us
    dot_general x1, matrix products, local(): lax.dot_general(stacked, turned, (((1,), (1,)), ((), ())), preferred_elem...  3.47 us
    another operation x1, other arithmetic  2.03 us
  transfers between devices with their start and end apart: 3, of which 2 were waited for; matrix products, arithmetic and copies ran while one was open for 30% of the time, Pallas kernels for 0%

profile of v16, /device:TPU:2, one launch (start us, length us, event | category | flops | bytes accessed | tf_op | source)
XLA Modules:
  0.0 81.1 jit_solution(13372809698317459717)
XLA Ops:
  0.6 3.7 %shard_map.86 = (f32[32,24,320]{2,1,0:T(8,128)}, bf16[64,8192]{1,0:T(8,128)(2,1)}) custom-call(bf16[64,8192]{1,0:T(8,128)(2,1)} %x_ref.1, f32[64,128]{1,0:T(8,128)} %constant.129.clone.cos_ref, f32[64,128]{1,0:T(8,128)} %constant.130.clone.sin_ref, s32[64]{0:T(128)} %rot_ref.1, s32[64]{0:T(128)} %group_ref.1, f32[32,64]{1,0:T(8,128)} %table_ref.1, ...), custom_call_target="tpu_custom_call" | custom-call | tf_op jit(solution)/shard_map/pallas_call | solution.py:77
  4.4 7.8 %all-to-all-start = ((f32[32,24,320]{2,1,0:T(8,128)}), f32[32,24,320]{2,1,0:T(8,128)S(1)}, u32[]{:S(2)}, u32[]{:S(2)}) async-start(f32[32,24,320]{2,1,0:T(8,128)} %get-tuple-element.4), calls=%async_computation | async-start | bytes 2359296 | tf_op jit(solution)/shard_map/all_to_all | solution.py:133
  12.4 1.4 %select_select_fusion.1 = (bf16[64,4096]{1,0:T(8,128)(2,1)S(1)}, bf16[64,4096]{1,0:T(8,128)(2,1)S(1)}) fusion(pred[4096]{0:T(1024)(128)(4,1)S(1)} %get-tuple-element.20, pred[4096]{0:T(1024)(128)(4,1)S(1)} %get-tuple-element.21, pred[4096]{0:T(1024)(128)(4,1)S(1)} %broadcast_compare_fusion.8, bf16[64,8192]{1,0:T(8,128)(2,1)} %get-tuple-element.5), kind=kLoop, calls=%fused_computation.12 | loop fusion | flops 2097152 | bytes 2109440 | tf_op jit(solution)/shard_map/jit(_where)/select_n | solution.py:169
  13.8 0.5 select_select_fusion.5
  14.4 14.6 %maximum_maximum_fusion = bf16[256,8192]{1,0:T(8,128)(2,1)} fusion(bf16[64,4096]{1,0:T(8,128)(2,1)S(1)} %get-tuple-element.13, bf16[64,4096]{1,0:T(8,128)(2,1)S(1)} %get-tuple-element.12, bf16[64,4096]{1,0:T(8,128)(2,1)S(1)} %get-tuple-element.14, bf16[64,4096]{1,0:T(8,128)(2,1)S(1)} %get-tuple-element.15, bf16[64,4096]{1,0:T(8,128)(2,1)S(1)} %get-tuple-element.9, ...), kind=kLoop, calls=%fused_computation.6 | loop fusion | flops 29360128 | bytes 8388608 | tf_op jit(solution)/shard_map/concatenate | solution.py:172
  28.9 0.6 all-to-all-done
  29.5 0.1 reduce_sum.18
  29.7 0.1 div.34
  29.8 0.1 div.35
  29.9 0.9 %broadcast_in_dim.73 = f32[32,24,256]{2,1,0:T(8,128)} broadcast(f32[24,256]{1,0:T(8,128)S(1)} %slice_divide_fusion), dimensions={1,2} | broadcast | bytes 811008 | tf_op jit(solution)/shard_map/broadcast_in_dim | solution.py:139
  30.8 6.8 %all-to-all-start.1 = ((f32[32,24,256]{2,1,0:T(8,128)}), f32[32,24,256]{2,1,0:T(8,128)S(1)}, u32[]{:S(2)}, u32[]{:S(2)}) async-start(f32[32,24,256]{2,1,0:T(8,128)} %broadcast_in_dim.73), calls=%async_computation.1 | async-start | bytes 1572864 | tf_op jit(solution)/shard_map/all_to_all | solution.py:138
  37.7 1.0 %fusion.9 = (f32[16,4096]{1,0:T(8,128)S(1)}, f32[16,4096]{1,0:T(8,128)S(1)}) fusion(s32[4096]{0:T(1024)S(1)} %get-tuple-element.28, s32[4096]{0:T(1024)S(1)} %get-tuple-element.29, pred[4096]{0:T(1024)(128)(4,1)S(1)} %fusion.17), kind=kLoop, calls=%fused_computation.24 | loop fusion | flops 983040 | bytes 561152 | tf_op jit(solution)/shard_map/cos | solution.py:107
  38.7 12.1 %all-to-all-done.1 = f32[32,24,256]{2,1,0:T(8,128)S(1)} async-done(((f32[32,24,256]{2,1,0:T(8,128)}), f32[32,24,256]{2,1,0:T(8,128)S(1)}, u32[]{:S(2)}, u32[]{:S(2)}) %all-to-all-start.1) | async-done | bytes 786464 | tf_op jit(solution)/shard_map/all_to_all | solution.py:138
  50.9 0.2 fusion.4
  51.1 0.1 divide_convert_fusion
  51.4 1.0 %collective-permute-start = (bf16[6,8192]{1,0:T(8,128)(2,1)S(1)}, bf16[6,8192]{1,0:T(8,128)(2,1)S(1)}, u32[]{:S(2)}, u32[]{:S(2)}) collective-permute-start(bf16[6,8192]{1,0:T(8,128)(2,1)S(1)} %constant_dynamic-slice_fusion), channel_id=1, source_target_pairs={{0,0},{8,8},{16,16},{24,24},{32,1},{40,2},{48,3},{56,4},{64,5},{72... | collective-permute-start | bytes 294920 | tf_op jit(solution)/shard_map/ppermute | solution.py:161
  52.4 2.0 %subtract_convert_fusion = (bf16[16,24,4096]{2,1,0:T(8,128)(2,1)S(1)}, bf16[16,24,4096]{2,1,0:T(8,128)(2,1)S(1)}) fusion(f32[16,4096]{1,0:T(8,128)S(1)} %get-tuple-element.19, f32[24,4096]{1,0:T(8,128)S(1)} %get-tuple-element.17, f32[16,4096]{1,0:T(8,128)S(1)} %get-tuple-element.18, f32[24,4096]{1,0:T(8,128)S(1)} %get-tuple-element.16), kind=kLoop, calls=%fused_computation.5 | loop fusion | flops 12582912 | bytes 7602176 | tf_op jit(solution)/shard_map/convert
  54.4 3.5 %fusion.3 = f32[64,24]{0,1:T(8,128)S(1)} fusion(bf16[4,64,8192,1]{2,1,3,0:T(8,128)(2,1)S(1)} %bitcast.21, bf16[16,24,4096]{2,1,0:T(8,128)(2,1)S(1)} %get-tuple-element.7, bf16[16,24,4096]{2,1,0:T(8,128)(2,1)S(1)} %get-tuple-element.6), kind=kOutput, calls=%fused_computation.7 | convolution fusion | flops 1623292416 | bytes 10491904 | tf_op jit(solution)/shard_map/dot_general | solution.py:174
  58.0 0.1 reshape.141
  58.1 20.4 %all_to_all.26 = f32[8,1,192]{2,1,0:T(1,128)S(1)} all-to-all(f32[8,1,192]{2,1,0:T(1,128)S(1)} %reshape.141), channel_id=1, replica_groups=mesh['dom'=32,'rot'=8] {'rot'}, dimensions={0} | all-to-all | bytes 12288 | tf_op jit(solution)/shard_map/all_to_all | solution.py:178
  78.5 0.5 broadcast.254
  79.0 0.7 reduce.1
  79.8 0.7 all_to_all.22
  80.4 0.7 copy.18
  (23 shorter events, 0.6 us)
Async XLA Ops:
  4.4 9.5 %copy-start = (bf16[64,8192]{1,0:T(8,128)(2,1)S(1)}, bf16[64,8192]{1,0:T(8,128)(2,1)}, u32[]{:S(2)}) copy-start(bf16[64,8192]{1,0:T(8,128)(2,1)} %get-tuple-element.5) | copy-start | bytes 3145732
  4.4 25.2 %all-to-all-start = ((f32[32,24,320]{2,1,0:T(8,128)}), f32[32,24,320]{2,1,0:T(8,128)S(1)}, u32[]{:S(2)}, u32[]{:S(2)}) async-start(f32[32,24,320]{2,1,0:T(8,128)} %get-tuple-element.4), calls=%async_computation | async-start | bytes 2359296 | tf_op jit(solution)/shard_map/all_to_all | solution.py:133
  30.8 20.0 %all-to-all-start.1 = ((f32[32,24,256]{2,1,0:T(8,128)}), f32[32,24,256]{2,1,0:T(8,128)S(1)}, u32[]{:S(2)}, u32[]{:S(2)}) async-start(f32[32,24,256]{2,1,0:T(8,128)} %broadcast_in_dim.73), calls=%async_computation.1 | async-start | bytes 1572864 | tf_op jit(solution)/shard_map/all_to_all | solution.py:138
  51.3 3.1 %copy-start.1 = (bf16[256,8192]{1,0:T(8,128)(2,1)S(1)}, bf16[256,8192]{1,0:T(8,128)(2,1)}, u32[]{:S(2)}) copy-start(bf16[256,8192]{1,0:T(8,128)(2,1)} %maximum_maximum_fusion) | copy-start | bytes 12582916
  51.4 29.0 %collective-permute-start = (bf16[6,8192]{1,0:T(8,128)(2,1)S(1)}, bf16[6,8192]{1,0:T(8,128)(2,1)S(1)}, u32[]{:S(2)}, u32[]{:S(2)}) collective-permute-start(bf16[6,8192]{1,0:T(8,128)(2,1)S(1)} %constant_dynamic-slice_fusion), channel_id=1, source_target_pairs={{0,0},{8,8},{16,16},{24,24},{32,1},{40,2},{48,3},{56,4},{64,5},{72... | collective-permute-start | bytes 294920 | tf_op jit(solution)/shard_map/ppermute | solution.py:161

commit v17 on v16

--- a/solution.py
+++ b/solution.py
@@ -35,7 +35,7 @@
     pay_ref, mod_ref, w_ref, ctf_ref, cos_scr, sin_scr,
 ):
     count = x_ref.shape[0]
-    block = pay_ref.shape[1]
+    block = pay_ref.shape[1] - 8
     for p in range(count):
         ctf_ref[pl.ds(p, 1), :] = table_ref[pl.ds(group_ref[p], 1), :]
         cos_scr[pl.ds(p, 1), :] = cos_ref[pl.ds(rot_ref[p], 1), :]
@@ -46,7 +46,6 @@
     half = x_ref.shape[1] // 2
     lanes = cos_ref.shape[1]
     chunks, _, width = pay_ref.shape
-    width -= ctf_ref.shape[1]
     cosine = cos_scr[...]
     sine = sin_scr[...]
     low = lax.broadcasted_iota(jnp.int32, cosine.shape, 1) < MFREQ
@@ -61,11 +60,15 @@
         mod_ref[:, re_cols] = (real_part * gain).astype(jnp.bfloat16)
         mod_ref[:, im_cols] = (imag_part * gain).astype(jnp.bfloat16)
     gains = ctf_ref[...]
-    denom = split_dot(member, gains * gains)
+    denom_t = split_dot(member, gains * gains).T
     numer = split_dot(member, w_ref[...])
+    per_chunk = width // MFREQ
+    cycles = gains.shape[1]
     for x in range(chunks):
-        pay_ref[x, :, :width] = numer[:, x * width : (x + 1) * width]
-        pay_ref[x, :, width:] = denom
+        pay_ref[x, :block, :] = numer[:, x * width : (x + 1) * width]
+        first = (x * per_chunk) % cycles
+        pay_ref[x, block:, :] = jnp.zeros((pay_ref.shape[1] - block, width), jnp.float32)
+        pay_ref[x, block : block + per_chunk, :block] = denom_t[first : first + per_chunk, :]
 
 
 def derotate_and_sum(particles, rotation, group, ctf_table, assign, block, chunks, total):
@@ -77,7 +80,7 @@
     return pl.pallas_call(
         prologue_kernel,
         out_shape=(
-            jax.ShapeDtypeStruct((chunks, block, K // chunks + CYCLES), jnp.float32),
+            jax.ShapeDtypeStruct((chunks, block + 8, K // chunks), jnp.float32),
             jax.ShapeDtypeStruct((count, K), jnp.bfloat16),
         ),
         in_specs=[vmem, vmem, vmem, smem, smem, vmem, vmem],
@@ -131,9 +134,8 @@
         particles, rot_index, group, ctf_table, assign, block, chunks, total
     )
     summed = jnp.sum(lax.all_to_all(payload, "dom", 0, 0, tiled=True), axis=0)
-    numer_chunk = summed[:, :width].reshape(block, per_chunk, MFREQ)
-    first_cycle = (dom_rank * per_chunk) % CYCLES
-    denom_chunk = lax.dynamic_slice_in_dim(summed[:, width:], first_cycle, per_chunk, 1)
+    numer_chunk = summed[:block].reshape(block, per_chunk, MFREQ)
+    denom_chunk = summed[block : block + per_chunk, :block].T
     plain_chunk = (numer_chunk / (denom_chunk[:, :, None] + 1.0)).reshape(block, width)
     plain = lax.all_to_all(
         jnp.broadcast_to(plain_chunk[None], (chunks, block, width)), "dom", 0, 0, tiled=True

time: 81.5 us -> 81.9 us (level)
    select_n x2, other arithmetic: 1.96 us -> 3.27 us  [local(): jnp.where(step == 0, real_part, jnp.where(step == 1, imag_part, jnp.where...]
  transfers between devices with their start and end apart: 3 -> 3, of which waited for: 2 -> 1; matrix products, arithmetic and copies ran while one was open for 30% -> 31% of each run, Pallas kernels for 0% -> 0%
where the time goes in v17:
time: 81.9 us; the launch traced here: 81.5 us
  other arithmetic  21.4 us (26%)
  blocking collectives  20.4 us (25%)
  starting transfers between devices  16.1 us (20%)
  waiting for transfers between devices  12.1 us (15%)
  Pallas kernels  3.68 us (4%)
  local copies, waits for them, and re-layouts  3.49 us (4%)
  matrix products  3.47 us (4%)
  between operations  0.82 us (1%)
    all_to_all x1, blocking collectives, local(): best_scores = lax.all_to_all(best, 'rot', 0, 1, tiled=True)  20.4 us
    concatenate x1, other arithmetic, local(): stacked = jnp.concatenate(variants, axis=0)  13.8 us
    all_to_all x1, waiting for transfers between devices, local(): lax.all_to_all(jnp.broadcast_to(plain_chunk[None], (chunks, block, width)...  12.1 us
    all_to_all x1, starting transfers between devices, local(): summed = jnp.sum(lax.all_to_all(payload, 'dom', 0, 0, tiled=True), axis=0)  7.75 us
    all_to_all x1, starting transfers between devices, local(): lax.all_to_all(jnp.broadcast_to(plain_chunk[None], (chunks, block, width)...  7.38 us
    pallas_call x1, Pallas kernels, derotate_and_sum(): pl.pallas_call(prologue_kernel, out_shape=(jax.ShapeDtypeStruct((chunks,...  3.68 us
    dot_general x1, matrix products, local(): lax.dot_general(stacked, turned, (((1,), (1,)), ((), ())), preferred_elem...  3.47 us
    select_n x2, other arithmetic, local(): jnp.where(step == 0, real_part, jnp.where(step == 1, imag_part, jnp.where...  3.27 us
  transfers between devices with their start and end apart: 3, of which 1 were waited for; matrix products, arithmetic and copies ran while one was open for 31% of the time, Pallas kernels for 0%

profile of v17, /device:TPU:2, one launch (start us, length us, event | category | flops | bytes accessed | tf_op | source)
XLA Modules:
  0.0 81.5 jit_solution(17316931958988143473)
XLA Ops:
  0.6 3.7 %shard_map.86 = (f32[32,32,256]{2,1,0:T(8,128)}, bf16[64,8192]{1,0:T(8,128)(2,1)}) custom-call(bf16[64,8192]{1,0:T(8,128)(2,1)} %x_ref.1, f32[64,128]{1,0:T(8,128)} %constant.125.clone.cos_ref, f32[64,128]{1,0:T(8,128)} %constant.126.clone.sin_ref, s32[64]{0:T(128)} %rot_ref.1, s32[64]{0:T(128)} %group_ref.1, f32[32,64]{1,0:T(8,128)} %table_ref.1, ...), custom_call_target="tpu_custom_call" | custom-call | tf_op jit(solution)/shard_map/pallas_call | solution.py:80
  4.3 7.7 %all-to-all-start = ((f32[32,32,256]{2,1,0:T(8,128)}), f32[32,32,256]{2,1,0:T(8,128)S(1)}, u32[]{:S(2)}, u32[]{:S(2)}) async-start(f32[32,32,256]{2,1,0:T(8,128)} %get-tuple-element.4), calls=%async_computation | async-start | bytes 2097152 | tf_op jit(solution)/shard_map/all_to_all | solution.py:136
  12.2 1.4 %select_select_fusion.1 = (bf16[64,4096]{1,0:T(8,128)(2,1)S(1)}, bf16[64,4096]{1,0:T(8,128)(2,1)S(1)}) fusion(pred[4096]{0:T(1024)(128)(4,1)S(1)} %get-tuple-element.20, pred[4096]{0:T(1024)(128)(4,1)S(1)} %get-tuple-element.21, pred[4096]{0:T(1024)(128)(4,1)S(1)} %broadcast_compare_fusion.8, bf16[64,8192]{1,0:T(8,128)(2,1)} %get-tuple-element.5), kind=kLoop, calls=%fused_computation.12 | loop fusion | flops 2097152 | bytes 2109440 | tf_op jit(solution)/shard_map/jit(_where)/select_n | solution.py:171
  13.7 1.8 %select_select_fusion.5 = (bf16[64,4096]{1,0:T(8,128)(2,1)}, bf16[64,4096]{1,0:T(8,128)(2,1)}, bf16[64,4096]{1,0:T(8,128)(2,1)}, bf16[64,4096]{1,0:T(8,128)(2,1)}) fusion(pred[4096]{0:T(1024)(128)(4,1)S(1)} %get-tuple-element.23, pred[4096]{0:T(1024)(128)(4,1)S(1)} %get-tuple-element.25, pred[4096]{0:T(1024)(128)(4,1)S(1)} %get-tuple-element.27, ...), kind=kLoop, calls=%fused_computation.16 | loop fusion | flops 3670016 | bytes 3170304 | tf_op jit(solution)/shard_map/jit(_where)/select_n | solution.py:171
  15.5 13.8 %maximum_maximum_fusion = bf16[256,8192]{1,0:T(8,128)(2,1)} fusion(bf16[64,4096]{1,0:T(8,128)(2,1)S(1)} %get-tuple-element.13, bf16[64,4096]{1,0:T(8,128)(2,1)S(1)} %get-tuple-element.12, bf16[64,4096]{1,0:T(8,128)(2,1)} %get-tuple-element.14, bf16[64,4096]{1,0:T(8,128)(2,1)} %get-tuple-element.15, bf16[64,4096]{1,0:T(8,128)(2,1)} %get-tuple-element.9, ...), kind=kLoop, calls=%fused_computation.6 | loop fusion | flops 29360128 | bytes 8388608 | tf_op jit(solution)/shard_map/concatenate | solution.py:174
  29.4 0.1 copy.16
  29.5 0.1 div.34
  29.6 0.1 div.35
  29.7 0.9 %broadcast_in_dim.73 = f32[32,24,256]{2,1,0:T(8,128)} broadcast(f32[24,256]{1,0:T(8,128)S(1)} %slice_divide_fusion), dimensions={1,2} | broadcast | bytes 811008 | tf_op jit(solution)/shard_map/broadcast_in_dim | solution.py:141
  30.7 7.4 %all-to-all-start.1 = ((f32[32,24,256]{2,1,0:T(8,128)}), f32[32,24,256]{2,1,0:T(8,128)S(1)}, u32[]{:S(2)}, u32[]{:S(2)}) async-start(f32[32,24,256]{2,1,0:T(8,128)} %broadcast_in_dim.73), calls=%async_computation.1 | async-start | bytes 1572864 | tf_op jit(solution)/shard_map/all_to_all | solution.py:140
  38.0 1.0 %fusion.9 = (f32[16,4096]{1,0:T(8,128)S(1)}, f32[16,4096]{1,0:T(8,128)S(1)}) fusion(s32[4096]{0:T(1024)S(1)} %get-tuple-element.28, s32[4096]{0:T(1024)S(1)} %get-tuple-element.29, pred[4096]{0:T(1024)(128)(4,1)S(1)} %fusion.17), kind=kLoop, calls=%fused_computation.24 | loop fusion | flops 983040 | bytes 561152 | tf_op jit(solution)/shard_map/cos | solution.py:110
  39.1 12.1 %all-to-all-done.1 = f32[32,24,256]{2,1,0:T(8,128)S(1)} async-done(((f32[32,24,256]{2,1,0:T(8,128)}), f32[32,24,256]{2,1,0:T(8,128)S(1)}, u32[]{:S(2)}, u32[]{:S(2)}) %all-to-all-start.1) | async-done | bytes 786464 | tf_op jit(solution)/shard_map/all_to_all | solution.py:140
  51.3 0.2 fusion.4
  51.5 0.1 divide_convert_fusion
  51.8 1.0 %collective-permute-start = (bf16[6,8192]{1,0:T(8,128)(2,1)S(1)}, bf16[6,8192]{1,0:T(8,128)(2,1)S(1)}, u32[]{:S(2)}, u32[]{:S(2)}) collective-permute-start(bf16[6,8192]{1,0:T(8,128)(2,1)S(1)} %constant_dynamic-slice_fusion), channel_id=1, source_target_pairs={{0,0},{8,8},{16,16},{24,24},{32,1},{40,2},{48,3},{56,4},{64,5},{72... | collective-permute-start | bytes 294920 | tf_op jit(solution)/shard_map/ppermute | solution.py:163
  52.8 2.0 %subtract_convert_fusion = (bf16[16,24,4096]{2,1,0:T(8,128)(2,1)S(1)}, bf16[16,24,4096]{2,1,0:T(8,128)(2,1)S(1)}) fusion(f32[16,4096]{1,0:T(8,128)S(1)} %get-tuple-element.19, f32[24,4096]{1,0:T(8,128)S(1)} %get-tuple-element.17, f32[16,4096]{1,0:T(8,128)S(1)} %get-tuple-element.18, f32[24,4096]{1,0:T(8,128)S(1)} %get-tuple-element.16), kind=kLoop, calls=%fused_computation.5 | loop fusion | flops 12582912 | bytes 7602176 | tf_op jit(solution)/shard_map/convert
  54.8 3.5 %fusion.3 = f32[64,24]{0,1:T(8,128)S(1)} fusion(bf16[4,64,8192,1]{2,1,3,0:T(8,128)(2,1)S(1)} %bitcast.23, bf16[16,24,4096]{2,1,0:T(8,128)(2,1)S(1)} %get-tuple-element.7, bf16[16,24,4096]{2,1,0:T(8,128)(2,1)S(1)} %get-tuple-element.6), kind=kOutput, calls=%fused_computation.7 | convolution fusion | flops 1623292416 | bytes 10491904 | tf_op jit(solution)/shard_map/dot_general | solution.py:176
  58.3 0.1 copy.18
  58.4 0.1 reshape.141
  58.5 20.4 %all_to_all.26 = f32[8,1,192]{2,1,0:T(1,128)S(1)} all-to-all(f32[8,1,192]{2,1,0:T(1,128)S(1)} %reshape.141), channel_id=1, replica_groups=mesh['dom'=32,'rot'=8] {'rot'}, dimensions={0} | all-to-all | bytes 12288 | tf_op jit(solution)/shard_map/all_to_all | solution.py:180
  78.9 0.5 broadcast.255
  79.4 0.7 reduce.1
  80.1 0.7 all_to_all.22
  80.8 0.7 copy.23
  (23 shorter events, 0.5 us)
Async XLA Ops:
  4.3 9.3 %copy-start = (bf16[64,8192]{1,0:T(8,128)(2,1)S(1)}, bf16[64,8192]{1,0:T(8,128)(2,1)}, u32[]{:S(2)}) copy-start(bf16[64,8192]{1,0:T(8,128)(2,1)} %get-tuple-element.5) | copy-start | bytes 3145732
  4.3 25.0 %all-to-all-start = ((f32[32,32,256]{2,1,0:T(8,128)}), f32[32,32,256]{2,1,0:T(8,128)S(1)}, u32[]{:S(2)}, u32[]{:S(2)}) async-start(f32[32,32,256]{2,1,0:T(8,128)} %get-tuple-element.4), calls=%async_computation | async-start | bytes 2097152 | tf_op jit(solution)/shard_map/all_to_all | solution.py:136
  30.7 20.6 %all-to-all-start.1 = ((f32[32,24,256]{2,1,0:T(8,128)}), f32[32,24,256]{2,1,0:T(8,128)S(1)}, u32[]{:S(2)}, u32[]{:S(2)}) async-start(f32[32,24,256]{2,1,0:T(8,128)} %broadcast_in_dim.73), calls=%async_computation.1 | async-start | bytes 1572864 | tf_op jit(solution)/shard_map/all_to_all | solution.py:140
  51.7 3.1 %copy-start.1 = (bf16[256,8192]{1,0:T(8,128)(2,1)S(1)}, bf16[256,8192]{1,0:T(8,128)(2,1)}, u32[]{:S(2)}) copy-start(bf16[256,8192]{1,0:T(8,128)(2,1)} %maximum_maximum_fusion) | copy-start | bytes 12582916
  51.8 29.0 %collective-permute-start = (bf16[6,8192]{1,0:T(8,128)(2,1)S(1)}, bf16[6,8192]{1,0:T(8,128)(2,1)S(1)}, u32[]{:S(2)}, u32[]{:S(2)}) collective-permute-start(bf16[6,8192]{1,0:T(8,128)(2,1)S(1)} %constant_dynamic-slice_fusion), channel_id=1, source_target_pairs={{0,0},{8,8},{16,16},{24,24},{32,1},{40,2},{48,3},{56,4},{64,5},{72... | collective-permute-start | bytes 294920 | tf_op jit(solution)/shard_map/ppermute | solution.py:163

commit v18 on v16

--- a/solution.py
+++ b/solution.py
@@ -158,7 +158,6 @@
     idx = jnp.where(dom_rank > rot_rank * owners_per_block, dom_rank - owners_per_block, dom_rank)
     slot = jnp.where(own_plane, dom_rank % owners_per_block, jnp.minimum(idx // others, owners_per_block - 1))
     sent = lax.dynamic_slice_in_dim(refs_block, slot * CLS_DEV, CLS_DEV, 0)
-    refs = lax.ppermute(sent, ("dom", "rot"), pairs)
     quarter = total // 4
     real_part = modulated[:, :half]
     imag_part = modulated[:, half:]
@@ -175,6 +174,8 @@
         stacked, turned, (((1,), (1,)), ((), ())), preferred_element_type=jnp.float32
     )
     best = jnp.max(found.reshape(4, count, quarter, block), axis=(0, 2)) * (1.0 / math.sqrt(K))
+    sent, best = lax.optimization_barrier((sent, best))
+    refs = lax.ppermute(sent, ("dom", "rot"), pairs)
     best_scores = lax.all_to_all(best, "rot", 0, 1, tiled=True)
 
     return (refs, best_scores)

time: 81.5 us -> 81.2 us (level)
  transfers between devices with their start and end apart: 3 -> 3, of which waited for: 2 -> 2; matrix products, arithmetic and copies ran while one was open for 30% -> 24% of each run, Pallas kernels for 0% -> 0%
where the time goes in v18:
time: 81.2 us; the launch traced here: 80.7 us
  other arithmetic  20.9 us (26%)
  blocking collectives  20.3 us (25%)
  starting transfers between devices  15.2 us (19%)
  waiting for transfers between devices  12.7 us (16%)
  Pallas kernels  3.74 us (5%)
  local copies, waits for them, and re-layouts  3.49 us (4%)
  matrix products  3.47 us (4%)
  between operations  0.94 us (1%)
    all_to_all x1, blocking collectives, local(): best_scores = lax.all_to_all(best, 'rot', 0, 1, tiled=True)  20.3 us
    concatenate x1, other arithmetic, local(): stacked = jnp.concatenate(variants, axis=0)  14.6 us
    all_to_all x1, waiting for transfers between devices, local(): lax.all_to_all(jnp.broadcast_to(plain_chunk[None], (chunks, block, width)...  12.1 us
    all_to_all x1, starting transfers between devices, local(): summed = jnp.sum(lax.all_to_all(payload, 'dom', 0, 0, tiled=True), axis=0)  7.75 us
    all_to_all x1, starting transfers between devices, local(): lax.all_to_all(jnp.broadcast_to(plain_chunk[None], (chunks, block, width)...  6.8 us
    pallas_call x1, Pallas kernels, derotate_and_sum(): pl.pallas_call(prologue_kernel, out_shape=(jax.ShapeDtypeStruct((chunks,...  3.74 us
    dot_general x1, matrix products, local(): lax.dot_general(stacked, turned, (((1,), (1,)), ((), ())), preferred_elem...  3.47 us
    another operation x1, other arithmetic  2.03 us
  transfers between devices with their start and end apart: 3, of which 2 were waited for; matrix products, arithmetic and copies ran while one was open for 24% of the time, Pallas kernels for 0%

profile of v18, /device:TPU:2, one launch (start us, length us, event | category | flops | bytes accessed | tf_op | source)
XLA Modules:
  0.0 80.7 jit_solution(6638376046698509899)
XLA Ops:
  0.6 3.7 %shard_map.86 = (f32[32,24,320]{2,1,0:T(8,128)}, bf16[64,8192]{1,0:T(8,128)(2,1)}) custom-call(bf16[64,8192]{1,0:T(8,128)(2,1)} %x_ref.1, f32[64,128]{1,0:T(8,128)} %constant.129.clone.cos_ref, f32[64,128]{1,0:T(8,128)} %constant.130.clone.sin_ref, s32[64]{0:T(128)} %rot_ref.1, s32[64]{0:T(128)} %group_ref.1, f32[32,64]{1,0:T(8,128)} %table_ref.1, ...), custom_call_target="tpu_custom_call" | custom-call | tf_op jit(solution)/shard_map/pallas_call | solution.py:77
  4.4 7.7 %all-to-all-start = ((f32[32,24,320]{2,1,0:T(8,128)}), f32[32,24,320]{2,1,0:T(8,128)S(1)}, u32[]{:S(2)}, u32[]{:S(2)}) async-start(f32[32,24,320]{2,1,0:T(8,128)} %get-tuple-element.6), calls=%async_computation | async-start | bytes 2359296 | tf_op jit(solution)/shard_map/all_to_all | solution.py:133
  12.4 1.4 %select_select_fusion.1 = (bf16[64,4096]{1,0:T(8,128)(2,1)S(1)}, bf16[64,4096]{1,0:T(8,128)(2,1)S(1)}) fusion(pred[4096]{0:T(1024)(128)(4,1)S(1)} %get-tuple-element.24, pred[4096]{0:T(1024)(128)(4,1)S(1)} %get-tuple-element.25, pred[4096]{0:T(1024)(128)(4,1)S(1)} %broadcast_compare_fusion.8, bf16[64,8192]{1,0:T(8,128)(2,1)} %get-tuple-element.7), kind=kLoop, calls=%fused_computation.12 | loop fusion | flops 2097152 | bytes 2109440 | tf_op jit(solution)/shard_map/jit(_where)/select_n | solution.py:168
  13.8 0.5 select_select_fusion.5
  14.4 14.6 %maximum_maximum_fusion = bf16[256,8192]{1,0:T(8,128)(2,1)} fusion(bf16[64,4096]{1,0:T(8,128)(2,1)S(1)} %get-tuple-element.17, bf16[64,4096]{1,0:T(8,128)(2,1)S(1)} %get-tuple-element.16, bf16[64,4096]{1,0:T(8,128)(2,1)S(1)} %get-tuple-element.18, bf16[64,4096]{1,0:T(8,128)(2,1)S(1)} %get-tuple-element.19, bf16[64,4096]{1,0:T(8,128)(2,1)S(1)} %get-tuple-element.13, ...), kind=kLoop, calls=%fused_computation.6 | loop fusion | flops 29360128 | bytes 8388608 | tf_op jit(solution)/shard_map/concatenate | solution.py:171
  28.9 0.6 all-to-all-done
  29.5 0.1 reduce_sum.18
  29.7 0.1 div.34
  29.8 0.1 div.35
  29.9 0.9 %broadcast_in_dim.73 = f32[32,24,256]{2,1,0:T(8,128)} broadcast(f32[24,256]{1,0:T(8,128)S(1)} %slice_divide_fusion), dimensions={1,2} | broadcast | bytes 811008 | tf_op jit(solution)/shard_map/broadcast_in_dim | solution.py:139
  30.8 6.8 %all-to-all-start.1 = ((f32[32,24,256]{2,1,0:T(8,128)}), f32[32,24,256]{2,1,0:T(8,128)S(1)}, u32[]{:S(2)}, u32[]{:S(2)}) async-start(f32[32,24,256]{2,1,0:T(8,128)} %broadcast_in_dim.73), calls=%async_computation.1 | async-start | bytes 1572864 | tf_op jit(solution)/shard_map/all_to_all | solution.py:138
  37.7 1.0 %fusion.9 = (f32[16,4096]{1,0:T(8,128)S(1)}, f32[16,4096]{1,0:T(8,128)S(1)}) fusion(s32[4096]{0:T(1024)S(1)} %get-tuple-element.32, s32[4096]{0:T(1024)S(1)} %get-tuple-element.33, pred[4096]{0:T(1024)(128)(4,1)S(1)} %fusion.17), kind=kLoop, calls=%fused_computation.24 | loop fusion | flops 983040 | bytes 561152 | tf_op jit(solution)/shard_map/cos | solution.py:107
  38.7 12.1 %all-to-all-done.1 = f32[32,24,256]{2,1,0:T(8,128)S(1)} async-done(((f32[32,24,256]{2,1,0:T(8,128)}), f32[32,24,256]{2,1,0:T(8,128)S(1)}, u32[]{:S(2)}, u32[]{:S(2)}) %all-to-all-start.1) | async-done | bytes 786464 | tf_op jit(solution)/shard_map/all_to_all | solution.py:138
  50.9 0.2 fusion.4
  51.1 0.1 divide_convert_fusion
  51.4 2.0 %subtract_convert_fusion = (bf16[16,24,4096]{2,1,0:T(8,128)(2,1)S(1)}, bf16[16,24,4096]{2,1,0:T(8,128)(2,1)S(1)}) fusion(f32[16,4096]{1,0:T(8,128)S(1)} %get-tuple-element.23, f32[24,4096]{1,0:T(8,128)S(1)} %get-tuple-element.21, f32[16,4096]{1,0:T(8,128)S(1)} %get-tuple-element.22, f32[24,4096]{1,0:T(8,128)S(1)} %get-tuple-element.20), kind=kLoop, calls=%fused_computation.5 | loop fusion | flops 12582912 | bytes 7602176 | tf_op jit(solution)/shard_map/convert
  53.5 3.5 %fusion.3 = f32[64,24]{0,1:T(8,128)S(1)} fusion(bf16[4,64,8192,1]{2,1,3,0:T(8,128)(2,1)S(1)} %bitcast.21, bf16[16,24,4096]{2,1,0:T(8,128)(2,1)S(1)} %get-tuple-element.11, bf16[16,24,4096]{2,1,0:T(8,128)(2,1)S(1)} %get-tuple-element.10), kind=kOutput, calls=%fused_computation.7 | convolution fusion | flops 1623292416 | bytes 10491904 | tf_op jit(solution)/shard_map/dot_general | solution.py:173
  57.0 0.7 collective-permute-start
  57.7 0.1 reshape.138
  57.8 20.3 %all_to_all.29 = f32[8,1,192]{2,1,0:T(1,128)S(1)} all-to-all(f32[8,1,192]{2,1,0:T(1,128)S(1)} %reshape.138), channel_id=1, replica_groups=mesh['dom'=32,'rot'=8] {'rot'}, dimensions={0} | all-to-all | bytes 12288 | tf_op jit(solution)/shard_map/all_to_all | solution.py:179
  78.1 0.5 broadcast.251
  78.6 0.7 reduce.1
  79.4 0.7 all_to_all.25
  80.1 0.7 copy.18
  (23 shorter events, 0.6 us)
Async XLA Ops:
  4.4 9.5 %copy-start = (bf16[64,8192]{1,0:T(8,128)(2,1)S(1)}, bf16[64,8192]{1,0:T(8,128)(2,1)}, u32[]{:S(2)}) copy-start(bf16[64,8192]{1,0:T(8,128)(2,1)} %get-tuple-element.7) | copy-start | bytes 3145732
  4.4 25.2 %all-to-all-start = ((f32[32,24,320]{2,1,0:T(8,128)}), f32[32,24,320]{2,1,0:T(8,128)S(1)}, u32[]{:S(2)}, u32[]{:S(2)}) async-start(f32[32,24,320]{2,1,0:T(8,128)} %get-tuple-element.6), calls=%async_computation | async-start | bytes 2359296 | tf_op jit(solution)/shard_map/all_to_all | solution.py:133
  30.8 20.0 %all-to-all-start.1 = ((f32[32,24,256]{2,1,0:T(8,128)}), f32[32,24,256]{2,1,0:T(8,128)S(1)}, u32[]{:S(2)}, u32[]{:S(2)}) async-start(f32[32,24,256]{2,1,0:T(8,128)} %broadcast_in_dim.73), calls=%async_computation.1 | async-start | bytes 1572864 | tf_op jit(solution)/shard_map/all_to_all | solution.py:138
  51.3 2.2 %copy-start.1 = (bf16[256,8192]{1,0:T(8,128)(2,1)S(1)}, bf16[256,8192]{1,0:T(8,128)(2,1)}, u32[]{:S(2)}) copy-start(bf16[256,8192]{1,0:T(8,128)(2,1)} %maximum_maximum_fusion) | copy-start | bytes 12582916
  57.0 23.1 %collective-permute-start = (bf16[6,8192]{1,0:T(8,128)(2,1)S(1)}, bf16[6,8192]{1,0:T(8,128)(2,1)S(1)}, u32[]{:S(2)}, u32[]{:S(2)}) collective-permute-start(bf16[6,8192]{1,0:T(8,128)(2,1)S(1)} %constant_dynamic-slice_fusion), channel_id=1, source_target_pairs={{0,0},{8,8},{16,16},{24,24},{32,1},{40,2},{48,3},{56,4},{64,5},{72... | collective-permute-start | bytes 294920 | tf_op jit(solution)/shard_map/ppermute | solution.py:178

commit v19 on v18

--- a/solution.py
+++ b/solution.py
@@ -131,6 +131,7 @@
         particles, rot_index, group, ctf_table, assign, block, chunks, total
     )
     summed = jnp.sum(lax.all_to_all(payload, "dom", 0, 0, tiled=True), axis=0)
+    modulated, summed = lax.optimization_barrier((modulated, summed))
     numer_chunk = summed[:, :width].reshape(block, per_chunk, MFREQ)
     first_cycle = (dom_rank * per_chunk) % CYCLES
     denom_chunk = lax.dynamic_slice_in_dim(summed[:, width:], first_cycle, per_chunk, 1)

time: 81.2 us -> 84.2 us (1.037); the launches traced: 80.7 us -> 82.6 us
  waiting for transfers between devices: 12.7 us -> 16.1 us
  starting transfers between devices: 15.2 us -> 13.5 us
  blocking collectives: 20.3 us -> 21.7 us
  other arithmetic: 20.9 us -> 19.7 us
    all_to_all x1, waiting for transfers between devices: 0.59 us -> 16.1 us  [local(): summed = jnp.sum(lax.all_to_all(payload, 'dom', 0, 0, tiled=True), axis=0)]
    all_to_all x1, waiting for transfers between devices: 12.1 us -> 0.01 us  [local(): lax.all_to_all(jnp.broadcast_to(plain_chunk[None], (chunks, block, width)...]
    all_to_all x1, starting transfers between devices: 6.8 us -> 5.11 us  [local(): lax.all_to_all(jnp.broadcast_to(plain_chunk[None], (chunks, block, width)...]
    all_to_all x1, blocking collectives: 20.3 us -> 21.7 us  [local(): best_scores = lax.all_to_all(best, 'rot', 0, 1, tiled=True)]
    select_n x2, other arithmetic: 1.96 us -> 0.77 us  [local(): jnp.where(step == 0, real_part, jnp.where(step == 1, imag_part, jnp.where...]
  transfers between devices with their start and end apart: 3 -> 3, of which waited for: 2 -> 1; matrix products, arithmetic and copies ran while one was open for 24% -> 22% of each run, Pallas kernels for 0% -> 0%
where the time goes in v19:
time: 84.2 us; the launch traced here: 82.6 us
  blocking collectives  21.7 us (26%)
  other arithmetic  19.7 us (23%)
  waiting for transfers between devices  16.1 us (19%)
  starting transfers between devices  13.5 us (16%)
  Pallas kernels  3.75 us (4%)
  local copies, waits for them, and re-layouts  3.48 us (4%)
  matrix products  3.47 us (4%)
  between operations  0.9 us (1%)
    all_to_all x1, blocking collectives, local(): best_scores = lax.all_to_all(best, 'rot', 0, 1, tiled=True)  21.7 us
    all_to_all x1, waiting for transfers between devices, local(): summed = jnp.sum(lax.all_to_all(payload, 'dom', 0, 0, tiled=True), axis=0)  16.1 us
    concatenate x1, other arithmetic, local(): stacked = jnp.concatenate(variants, axis=0)  14.6 us
    all_to_all x1, starting transfers between devices, local(): summed = jnp.sum(lax.all_to_all(payload, 'dom', 0, 0, tiled=True), axis=0)  7.75 us
    all_to_all x1, starting transfers between devices, local(): lax.all_to_all(jnp.broadcast_to(plain_chunk[None], (chunks, block, width)...  5.11 us
    pallas_call x1, Pallas kernels, derotate_and_sum(): pl.pallas_call(prologue_kernel, out_shape=(jax.ShapeDtypeStruct((chunks,...  3.75 us
    dot_general x1, matrix products, local(): lax.dot_general(stacked, turned, (((1,), (1,)), ((), ())), preferred_elem...  3.47 us
    another operation x1, other arithmetic  2.03 us
  transfers between devices with their start and end apart: 3, of which 1 were waited for; matrix products, arithmetic and copies ran while one was open for 22% of the time, Pallas kernels for 0%

profile of v19, /device:TPU:2, one launch (start us, length us, event | category | flops | bytes accessed | tf_op | source)
XLA Modules:
  0.0 82.6 jit_solution(134358378342284231)
XLA Ops:
  0.6 3.7 %shard_map.86 = (f32[32,24,320]{2,1,0:T(8,128)}, bf16[64,8192]{1,0:T(8,128)(2,1)}) custom-call(bf16[64,8192]{1,0:T(8,128)(2,1)} %x_ref.1, f32[64,128]{1,0:T(8,128)} %constant.129.clone.cos_ref, f32[64,128]{1,0:T(8,128)} %constant.130.clone.sin_ref, s32[64]{0:T(128)} %rot_ref.1, s32[64]{0:T(128)} %group_ref.1, f32[32,64]{1,0:T(8,128)} %table_ref.1, ...), custom_call_target="tpu_custom_call" | custom-call | tf_op jit(solution)/shard_map/pallas_call | solution.py:77
  4.4 7.8 %all-to-all-start = ((f32[32,24,320]{2,1,0:T(8,128)}), f32[32,24,320]{2,1,0:T(8,128)S(1)}, u32[]{:S(2)}, u32[]{:S(2)}) async-start(f32[32,24,320]{2,1,0:T(8,128)} %get-tuple-element.9), calls=%async_computation | async-start | bytes 2359296 | tf_op jit(solution)/shard_map/all_to_all | solution.py:133
  12.4 1.0 %fusion.9 = (f32[16,4096]{1,0:T(8,128)S(1)}, f32[16,4096]{1,0:T(8,128)S(1)}) fusion(s32[4096]{0:T(1024)S(1)} %get-tuple-element.36, s32[4096]{0:T(1024)S(1)} %get-tuple-element.37, pred[4096]{0:T(1024)(128)(4,1)S(1)} %fusion.17), kind=kLoop, calls=%fused_computation.24 | loop fusion | flops 983040 | bytes 561152 | tf_op jit(solution)/shard_map/cos | solution.py:107
  13.4 16.1 %all-to-all-done = f32[32,24,320]{2,1,0:T(8,128)S(1)} async-done(((f32[32,24,320]{2,1,0:T(8,128)}), f32[32,24,320]{2,1,0:T(8,128)S(1)}, u32[]{:S(2)}, u32[]{:S(2)}) %all-to-all-start) | async-done | bytes 983072 | tf_op jit(solution)/shard_map/all_to_all | solution.py:133
  29.5 0.1 reduce_sum.18
  29.7 0.1 div.34
  29.8 0.1 div.35
  29.9 0.9 %broadcast_in_dim.73 = f32[32,24,256]{2,1,0:T(8,128)} broadcast(f32[24,256]{1,0:T(8,128)S(1)} %slice_divide_fusion), dimensions={1,2} | broadcast | bytes 811008 | tf_op jit(solution)/shard_map/broadcast_in_dim | solution.py:140
  30.9 5.1 %all-to-all-start.1 = ((f32[32,24,256]{2,1,0:T(8,128)}), f32[32,24,256]{2,1,0:T(8,128)S(1)}, u32[]{:S(2)}, u32[]{:S(2)}) async-start(f32[32,24,256]{2,1,0:T(8,128)} %broadcast_in_dim.73), calls=%async_computation.1 | async-start | bytes 1572864 | tf_op jit(solution)/shard_map/all_to_all | solution.py:139
  36.0 0.2 select_select_fusion.1
  36.2 0.5 select_select_fusion.5
  36.8 14.6 %maximum_maximum_fusion = bf16[256,8192]{1,0:T(8,128)(2,1)} fusion(bf16[64,4096]{1,0:T(8,128)(2,1)S(1)} %get-tuple-element.21, bf16[64,4096]{1,0:T(8,128)(2,1)S(1)} %get-tuple-element.20, bf16[64,4096]{1,0:T(8,128)(2,1)S(1)} %get-tuple-element.22, bf16[64,4096]{1,0:T(8,128)(2,1)S(1)} %get-tuple-element.23, bf16[64,4096]{1,0:T(8,128)(2,1)S(1)} %get-tuple-element.17, ...), kind=kLoop, calls=%fused_computation.6 | loop fusion | flops 29360128 | bytes 8388608 | tf_op jit(solution)/shard_map/concatenate | solution.py:172
  51.4 0.2 fusion.4
  51.6 0.1 divide_convert_fusion
  51.9 2.0 %subtract_convert_fusion = (bf16[16,24,4096]{2,1,0:T(8,128)(2,1)S(1)}, bf16[16,24,4096]{2,1,0:T(8,128)(2,1)S(1)}) fusion(f32[16,4096]{1,0:T(8,128)S(1)} %get-tuple-element.27, f32[24,4096]{1,0:T(8,128)S(1)} %get-tuple-element.25, f32[16,4096]{1,0:T(8,128)S(1)} %get-tuple-element.26, f32[24,4096]{1,0:T(8,128)S(1)} %get-tuple-element.24), kind=kLoop, calls=%fused_computation.5 | loop fusion | flops 12582912 | bytes 7602176 | tf_op jit(solution)/shard_map/convert
  54.0 3.5 %fusion.3 = f32[64,24]{0,1:T(8,128)S(1)} fusion(bf16[4,64,8192,1]{2,1,3,0:T(8,128)(2,1)S(1)} %bitcast.21, bf16[16,24,4096]{2,1,0:T(8,128)(2,1)S(1)} %get-tuple-element.15, bf16[16,24,4096]{2,1,0:T(8,128)(2,1)S(1)} %get-tuple-element.14), kind=kOutput, calls=%fused_computation.7 | convolution fusion | flops 1623292416 | bytes 10491904 | tf_op jit(solution)/shard_map/dot_general | solution.py:174
  57.5 0.7 collective-permute-start
  58.1 0.1 copy.13
  58.2 0.1 reshape.138
  58.3 21.7 %all_to_all.29 = f32[8,1,192]{2,1,0:T(1,128)S(1)} all-to-all(f32[8,1,192]{2,1,0:T(1,128)S(1)} %reshape.138), channel_id=1, replica_groups=mesh['dom'=32,'rot'=8] {'rot'}, dimensions={0} | all-to-all | bytes 12288 | tf_op jit(solution)/shard_map/all_to_all | solution.py:180
  80.0 0.5 broadcast.251
  80.5 0.7 reduce.1
  81.3 0.7 all_to_all.25
  82.0 0.7 copy.18
  (23 shorter events, 0.6 us)
Async XLA Ops:
  4.4 31.6 %copy-start = (bf16[64,8192]{1,0:T(8,128)(2,1)S(1)}, bf16[64,8192]{1,0:T(8,128)(2,1)}, u32[]{:S(2)}) copy-start(bf16[64,8192]{1,0:T(8,128)(2,1)} %get-tuple-element.11) | copy-start | bytes 3145732
  4.4 25.2 %all-to-all-start = ((f32[32,24,320]{2,1,0:T(8,128)}), f32[32,24,320]{2,1,0:T(8,128)S(1)}, u32[]{:S(2)}, u32[]{:S(2)}) async-start(f32[32,24,320]{2,1,0:T(8,128)} %get-tuple-element.9), calls=%async_computation | async-start | bytes 2359296 | tf_op jit(solution)/shard_map/all_to_all | solution.py:133
  30.9 20.5 %all-to-all-start.1 = ((f32[32,24,256]{2,1,0:T(8,128)}), f32[32,24,256]{2,1,0:T(8,128)S(1)}, u32[]{:S(2)}, u32[]{:S(2)}) async-start(f32[32,24,256]{2,1,0:T(8,128)} %broadcast_in_dim.73), calls=%async_computation.1 | async-start | bytes 1572864 | tf_op jit(solution)/shard_map/all_to_all | solution.py:139
  51.8 2.2 %copy-start.1 = (bf16[256,8192]{1,0:T(8,128)(2,1)S(1)}, bf16[256,8192]{1,0:T(8,128)(2,1)}, u32[]{:S(2)}) copy-start(bf16[256,8192]{1,0:T(8,128)(2,1)} %maximum_maximum_fusion) | copy-start | bytes 12582916
  57.5 24.5 %collective-permute-start = (bf16[6,8192]{1,0:T(8,128)(2,1)S(1)}, bf16[6,8192]{1,0:T(8,128)(2,1)S(1)}, u32[]{:S(2)}, u32[]{:S(2)}) collective-permute-start(bf16[6,8192]{1,0:T(8,128)(2,1)S(1)} %constant_dynamic-slice_fusion), channel_id=1, source_target_pairs={{0,0},{8,8},{16,16},{24,24},{32,1},{40,2},{48,3},{56,4},{64,5},{72... | collective-permute-start | bytes 294920 | tf_op jit(solution)/shard_map/ppermute | solution.py:179

commit v20 on v18

--- a/solution.py
+++ b/solution.py
@@ -22,11 +22,8 @@
 
 def split_dot(member, value):
     high = value.astype(jnp.bfloat16)
-    rest = value - high.astype(jnp.float32)
-    mid = rest.astype(jnp.bfloat16)
-    low = (rest - mid.astype(jnp.float32)).astype(jnp.bfloat16)
+    low = (value - high.astype(jnp.float32)).astype(jnp.bfloat16)
     total = jnp.dot(member, high, preferred_element_type=jnp.float32)
-    total = total + jnp.dot(member, mid, preferred_element_type=jnp.float32)
     return total + jnp.dot(member, low, preferred_element_type=jnp.float32)
 
 

time: 81.2 us -> 81 us (level)
  no operation moved by 1% of the time
where the time goes in v20:
time: 81 us; the launch traced here: 80.6 us
  other arithmetic  20.9 us (26%)
  blocking collectives  20.3 us (25%)
  starting transfers between devices  15.2 us (19%)
  waiting for transfers between devices  12.7 us (16%)
  Pallas kernels  3.59 us (4%)
  local copies, waits for them, and re-layouts  3.49 us (4%)
  matrix products  3.46 us (4%)
  between operations  0.94 us (1%)
    all_to_all x1, blocking collectives, local(): best_scores = lax.all_to_all(best, 'rot', 0, 1, tiled=True)  20.3 us
    concatenate x1, other arithmetic, local(): stacked = jnp.concatenate(variants, axis=0)  14.6 us
    all_to_all x1, waiting for transfers between devices, local(): lax.all_to_all(jnp.broadcast_to(plain_chunk[None], (chunks, block, width)...  12.1 us
    all_to_all x1, starting transfers between devices, local(): summed = jnp.sum(lax.all_to_all(payload, 'dom', 0, 0, tiled=True), axis=0)  7.75 us
    all_to_all x1, starting transfers between devices, local(): lax.all_to_all(jnp.broadcast_to(plain_chunk[None], (chunks, block, width)...  6.8 us
    pallas_call x1, Pallas kernels, derotate_and_sum(): pl.pallas_call(prologue_kernel, out_shape=(jax.ShapeDtypeStruct((chunks,...  3.59 us
    dot_general x1, matrix products, local(): lax.dot_general(stacked, turned, (((1,), (1,)), ((), ())), preferred_elem...  3.46 us
    another operation x1, other arithmetic  2.03 us
  transfers between devices with their start and end apart: 3, of which 2 were waited for; matrix products, arithmetic and copies ran while one was open for 24% of the time, Pallas kernels for 0%

profile of v20, /device:TPU:2, one launch (start us, length us, event | category | flops | bytes accessed | tf_op | source)
XLA Modules:
  0.0 80.6 jit_solution(16706383933830169634)
XLA Ops:
  0.6 3.6 %shard_map.86 = (f32[32,24,320]{2,1,0:T(8,128)}, bf16[64,8192]{1,0:T(8,128)(2,1)}) custom-call(bf16[64,8192]{1,0:T(8,128)(2,1)} %x_ref.1, f32[64,128]{1,0:T(8,128)} %constant.129.clone.cos_ref, f32[64,128]{1,0:T(8,128)} %constant.130.clone.sin_ref, s32[64]{0:T(128)} %rot_ref.1, s32[64]{0:T(128)} %group_ref.1, f32[32,64]{1,0:T(8,128)} %table_ref.1, ...), custom_call_target="tpu_custom_call" | custom-call | tf_op jit(solution)/shard_map/pallas_call | solution.py:74
  4.2 7.8 %all-to-all-start = ((f32[32,24,320]{2,1,0:T(8,128)}), f32[32,24,320]{2,1,0:T(8,128)S(1)}, u32[]{:S(2)}, u32[]{:S(2)}) async-start(f32[32,24,320]{2,1,0:T(8,128)} %get-tuple-element.6), calls=%async_computation | async-start | bytes 2359296 | tf_op jit(solution)/shard_map/all_to_all | solution.py:130
  12.2 1.4 %select_select_fusion.1 = (bf16[64,4096]{1,0:T(8,128)(2,1)S(1)}, bf16[64,4096]{1,0:T(8,128)(2,1)S(1)}) fusion(pred[4096]{0:T(1024)(128)(4,1)S(1)} %get-tuple-element.24, pred[4096]{0:T(1024)(128)(4,1)S(1)} %get-tuple-element.25, pred[4096]{0:T(1024)(128)(4,1)S(1)} %broadcast_compare_fusion.8, bf16[64,8192]{1,0:T(8,128)(2,1)} %get-tuple-element.7), kind=kLoop, calls=%fused_computation.12 | loop fusion | flops 2097152 | bytes 2109440 | tf_op jit(solution)/shard_map/jit(_where)/select_n | solution.py:165
  13.7 0.5 select_select_fusion.5
  14.2 14.6 %maximum_maximum_fusion = bf16[256,8192]{1,0:T(8,128)(2,1)} fusion(bf16[64,4096]{1,0:T(8,128)(2,1)S(1)} %get-tuple-element.17, bf16[64,4096]{1,0:T(8,128)(2,1)S(1)} %get-tuple-element.16, bf16[64,4096]{1,0:T(8,128)(2,1)S(1)} %get-tuple-element.18, bf16[64,4096]{1,0:T(8,128)(2,1)S(1)} %get-tuple-element.19, bf16[64,4096]{1,0:T(8,128)(2,1)S(1)} %get-tuple-element.13, ...), kind=kLoop, calls=%fused_computation.6 | loop fusion | flops 29360128 | bytes 8388608 | tf_op jit(solution)/shard_map/concatenate | solution.py:168
  28.8 0.6 all-to-all-done
  29.4 0.1 reduce_sum.18
  29.5 0.1 div.34
  29.6 0.1 div.35
  29.8 0.9 %broadcast_in_dim.73 = f32[32,24,256]{2,1,0:T(8,128)} broadcast(f32[24,256]{1,0:T(8,128)S(1)} %slice_divide_fusion), dimensions={1,2} | broadcast | bytes 811008 | tf_op jit(solution)/shard_map/broadcast_in_dim | solution.py:136
  30.7 6.8 %all-to-all-start.1 = ((f32[32,24,256]{2,1,0:T(8,128)}), f32[32,24,256]{2,1,0:T(8,128)S(1)}, u32[]{:S(2)}, u32[]{:S(2)}) async-start(f32[32,24,256]{2,1,0:T(8,128)} %broadcast_in_dim.73), calls=%async_computation.1 | async-start | bytes 1572864 | tf_op jit(solution)/shard_map/all_to_all | solution.py:135
  37.5 1.0 %fusion.9 = (f32[16,4096]{1,0:T(8,128)S(1)}, f32[16,4096]{1,0:T(8,128)S(1)}) fusion(s32[4096]{0:T(1024)S(1)} %get-tuple-element.32, s32[4096]{0:T(1024)S(1)} %get-tuple-element.33, pred[4096]{0:T(1024)(128)(4,1)S(1)} %fusion.17), kind=kLoop, calls=%fused_computation.24 | loop fusion | flops 983040 | bytes 561152 | tf_op jit(solution)/shard_map/cos | solution.py:104
  38.6 12.1 %all-to-all-done.1 = f32[32,24,256]{2,1,0:T(8,128)S(1)} async-done(((f32[32,24,256]{2,1,0:T(8,128)}), f32[32,24,256]{2,1,0:T(8,128)S(1)}, u32[]{:S(2)}, u32[]{:S(2)}) %all-to-all-start.1) | async-done | bytes 786464 | tf_op jit(solution)/shard_map/all_to_all | solution.py:135
  50.8 0.2 fusion.4
  51.0 0.1 divide_convert_fusion
  51.2 2.0 %subtract_convert_fusion = (bf16[16,24,4096]{2,1,0:T(8,128)(2,1)S(1)}, bf16[16,24,4096]{2,1,0:T(8,128)(2,1)S(1)}) fusion(f32[16,4096]{1,0:T(8,128)S(1)} %get-tuple-element.23, f32[24,4096]{1,0:T(8,128)S(1)} %get-tuple-element.21, f32[16,4096]{1,0:T(8,128)S(1)} %get-tuple-element.22, f32[24,4096]{1,0:T(8,128)S(1)} %get-tuple-element.20), kind=kLoop, calls=%fused_computation.5 | loop fusion | flops 12582912 | bytes 7602176 | tf_op jit(solution)/shard_map/convert
  53.4 3.5 %fusion.3 = f32[64,24]{0,1:T(8,128)S(1)} fusion(bf16[4,64,8192,1]{2,1,3,0:T(8,128)(2,1)S(1)} %bitcast.21, bf16[16,24,4096]{2,1,0:T(8,128)(2,1)S(1)} %get-tuple-element.11, bf16[16,24,4096]{2,1,0:T(8,128)(2,1)S(1)} %get-tuple-element.10), kind=kOutput, calls=%fused_computation.7 | convolution fusion | flops 1623292416 | bytes 10491904 | tf_op jit(solution)/shard_map/dot_general | solution.py:170
  56.8 0.7 collective-permute-start
  57.6 0.1 reshape.138
  57.7 20.3 %all_to_all.29 = f32[8,1,192]{2,1,0:T(1,128)S(1)} all-to-all(f32[8,1,192]{2,1,0:T(1,128)S(1)} %reshape.138), channel_id=1, replica_groups=mesh['dom'=32,'rot'=8] {'rot'}, dimensions={0} | all-to-all | bytes 12288 | tf_op jit(solution)/shard_map/all_to_all | solution.py:176
  78.0 0.5 broadcast.251
  78.5 0.7 reduce.1
  79.2 0.7 all_to_all.25
  79.9 0.7 copy.18
  (23 shorter events, 0.6 us)
Async XLA Ops:
  4.2 9.5 %copy-start = (bf16[64,8192]{1,0:T(8,128)(2,1)S(1)}, bf16[64,8192]{1,0:T(8,128)(2,1)}, u32[]{:S(2)}) copy-start(bf16[64,8192]{1,0:T(8,128)(2,1)} %get-tuple-element.7) | copy-start | bytes 3145732
  4.2 25.2 %all-to-all-start = ((f32[32,24,320]{2,1,0:T(8,128)}), f32[32,24,320]{2,1,0:T(8,128)S(1)}, u32[]{:S(2)}, u32[]{:S(2)}) async-start(f32[32,24,320]{2,1,0:T(8,128)} %get-tuple-element.6), calls=%async_computation | async-start | bytes 2359296 | tf_op jit(solution)/shard_map/all_to_all | solution.py:130
  30.7 20.0 %all-to-all-start.1 = ((f32[32,24,256]{2,1,0:T(8,128)}), f32[32,24,256]{2,1,0:T(8,128)S(1)}, u32[]{:S(2)}, u32[]{:S(2)}) async-start(f32[32,24,256]{2,1,0:T(8,128)} %broadcast_in_dim.73), calls=%async_computation.1 | async-start | bytes 1572864 | tf_op jit(solution)/shard_map/all_to_all | solution.py:135
  51.2 2.2 %copy-start.1 = (bf16[256,8192]{1,0:T(8,128)(2,1)S(1)}, bf16[256,8192]{1,0:T(8,128)(2,1)}, u32[]{:S(2)}) copy-start(bf16[256,8192]{1,0:T(8,128)(2,1)} %maximum_maximum_fusion) | copy-start | bytes 12582916
  56.8 23.1 %collective-permute-start = (bf16[6,8192]{1,0:T(8,128)(2,1)S(1)}, bf16[6,8192]{1,0:T(8,128)(2,1)S(1)}, u32[]{:S(2)}, u32[]{:S(2)}) collective-permute-start(bf16[6,8192]{1,0:T(8,128)(2,1)S(1)} %constant_dynamic-slice_fusion), channel_id=1, source_target_pairs={{0,0},{8,8},{16,16},{24,24},{32,1},{40,2},{48,3},{56,4},{64,5},{72... | collective-permute-start | bytes 294920 | tf_op jit(solution)/shard_map/ppermute | solution.py:175
